TPU v7x, 256 devices: a whole 4x4x8 slice. The times are simulated.
256 devices in a mesh: depth: 8 (over y_hi, x), shots: 32 (over z, y_lo, core).
Axes of the slice: x: 4, y: 4 (y_hi: 2, y_lo: 2; y = y_hi * 2 + y_lo), z: 8, core: 2. Of those that a mesh axis runs over, the one named last changes fastest.
Arguments:
- adj_now: float32 [32, 128, 128, 128], P('shots', 'depth'), may hold values from -6 to 6
- adj_prev: float32 [32, 128, 128, 128], P('shots', 'depth'), may hold values from -6 to 6
- fwd_snap: bfloat16 [32, 4, 128, 128, 128], P('shots', None, 'depth'), may hold values from -6 to 6
- velocity: float32 [128, 128, 128], P('depth', 'shots'), may hold values from 1 to 2
- density: float32 [128, 128, 128], P('depth', 'shots'), may hold values from 1 to 2
- shot_count: int32 [32], P('shots'), may hold values from 1 to 12, 128 in all
- rec_x: int32 [32, 256], P('shots'), may hold values from 0 to 127
- rec_y: int32 [32, 256], P('shots'), may hold values from 0 to 127
- residual: float32 [32, 4, 256], P('shots'), may hold values from -6 to 6
Outputs:
- out_now: float32 [32, 128, 128, 128], P('shots', 'depth')
- out_prev: float32 [32, 128, 128, 128], P('shots', 'depth')
- grad_vel: float32 [128, 128, 128], P('depth', 'shots')
Inputs may be any that keep to these rules, and one draw needn't show every extreme that they name: `shot_count`: the counts sum to 128; the largest is exactly 12.
All inputs are finite; a program needn't handle non-finite values.
Results may differ from a plain program's by a relative error of at most 0.0003.
Values sent between devices are 32-bit elements; how exact they have to be, the bound alone decides.
No kernel may reach another device: no remote copies, remote signals or barrier semaphores. Data moves between devices by JAX's collectives and lax.ppermute only.
A program may use at most 64 MiB of HBM per device.

v0:
```python
import jax
import jax.numpy as jnp
from jax import lax
from jax.sharding import PartitionSpec as P
from jax.experimental import pallas as pl
from jax.experimental.pallas import tpu as pltpu

INTERPRET = False

HALO = 4


def shift_fwd(v, axis, n):
    r = pltpu.roll(v, n - 1, axis)
    idx = lax.broadcasted_iota(jnp.int32, v.shape, axis)
    return jnp.where(idx == n - 1, 0.0, r)


def shift_bwd(v, axis):
    r = pltpu.roll(v, 1, axis)
    idx = lax.broadcasted_iota(jnp.int32, v.shape, axis)
    return jnp.where(idx == 0, 0.0, r)


def stencil_kernel(count_ref, adj_ref, mat_ref, snap_ref, src_ref, now_ref, prev_ref, img_ref,
                   pbuf, qbuf, kz, kxf, kxb, kyf, kyb, kk):
    ext = adj_ref.shape[1]
    nx, ny = adj_ref.shape[2], adj_ref.shape[3]
    steps = snap_ref.shape[0]
    count = count_ref[0]

    def weights(e, carry):
        bc = mat_ref[1, e]
        kz[e] = 0.5 * (bc + mat_ref[1, e + 1])
        kxf[e] = 0.5 * (bc + shift_fwd(bc, 0, nx))
        kxb[e] = 0.5 * (shift_bwd(bc, 0) + bc)
        kyf[e] = 0.5 * (bc + shift_fwd(bc, 1, ny))
        kyb[e] = 0.5 * (shift_bwd(bc, 1) + bc)
        kk[e] = 0.08 * mat_ref[0, e]
        return carry

    lax.fori_loop(0, ext - 1, weights, 0)

    def one_step(step, cur, old, dst, lo, hi):
        moment = steps - 1 - step

        def plane(e, carry):
            pc = cur(e)
            total = kz[e] * (cur(e + 1) - pc) - kz[e - 1] * (pc - cur(e - 1))
            total = total + (kxf[e] * (shift_fwd(pc, 0, nx) - pc) - kxb[e] * (pc - shift_bwd(pc, 0)))
            total = total + (kyf[e] * (shift_fwd(pc, 1, ny) - pc) - kyb[e] * (pc - shift_bwd(pc, 1)))
            weight = jnp.where(e == HALO + 2, 1.0, 0.0)
            new = 2.0 * pc - old(e) + kk[e] * total + 0.08 * src_ref[moment] * weight
            dst(e, new)
            inner = jnp.logical_and(e >= HALO, e < ext - HALO)

            @pl.when(inner)
            def _():
                z = e - HALO
                gained = snap_ref[moment, z].astype(jnp.float32) * new
                if step == 0:
                    img_ref[z] = gained
                elif step == steps - 1:
                    img_ref[z] = count * (img_ref[z] + gained)
                else:
                    img_ref[z] = img_ref[z] + gained

            return carry

        lax.fori_loop(lo, hi, plane, 0)

    def rd(ref, k=None):
        if k is None:
            return lambda e: ref[e]
        return lambda e: ref[k, e]

    def wr(ref):
        def f(e, v):
            ref[e] = v

        return f

    def wr_inner(ref, out):
        def f(e, v):
            ref[e] = v

            @pl.when(jnp.logical_and(e >= HALO, e < ext - HALO))
            def _():
                out[e - HALO] = v

        return f

    def wr_out(out):
        def f(e, v):
            out[e - HALO] = v

        return f

    one_step(0, rd(adj_ref, 0), rd(adj_ref, 1), wr(pbuf), 1, ext - 1)
    one_step(1, rd(pbuf), rd(adj_ref, 0), wr(qbuf), 2, ext - 2)
    one_step(2, rd(qbuf), rd(pbuf), wr_inner(pbuf, prev_ref), 3, ext - 3)
    one_step(3, rd(pbuf), rd(qbuf), wr_out(now_ref), HALO, ext - HALO)


def run_steps(count, adj_ext, mat_ext, snaps, src):
    ext, nx, ny = adj_ext.shape[1:]
    planes = ext - 2 * HALO
    vmem = pltpu.VMEM
    out_shape = [jax.ShapeDtypeStruct((planes, nx, ny), jnp.float32)] * 3
    return pl.pallas_call(
        stencil_kernel,
        out_shape=out_shape,
        in_specs=[pl.BlockSpec(memory_space=pltpu.SMEM)] + [pl.BlockSpec(memory_space=vmem)] * 4,
        out_specs=[pl.BlockSpec(memory_space=vmem)] * 3,
        scratch_shapes=[pltpu.VMEM((ext, nx, ny), jnp.float32)] * 8,
        compiler_params=pltpu.CompilerParams(vmem_limit_bytes=48 * 1024 * 1024),
        interpret=INTERPRET,
    )(count, adj_ext, mat_ext, snaps, src)


def with_halo(shard, sides, width):
    for axis, dim in sides:
        peers, length = (lax.axis_size(axis), shard.shape[dim])
        up = [(i, (i + 1) % peers) for i in range(peers - 1)]
        down = [(j, i) for i, j in up]
        last = lax.slice_in_dim(shard, length - width, length, axis=dim)
        first = lax.slice_in_dim(shard, 0, width, axis=dim)
        before = lax.ppermute(last, axis, up)
        after = lax.ppermute(first, axis, down)
        shard = jnp.concatenate([before, shard, after], axis=dim)
    return shard


def bit_order(peers):
    return list(range(peers.bit_length() - 1))


def gather_rows(shard, axis, dim):
    peers = lax.axis_size(axis)
    me = lax.axis_index(axis)
    pieces = jnp.expand_dims(shard, dim)
    for b in reversed(bit_order(peers)):
        pairs = [(i, i ^ (1 << b)) for i in range(peers)]
        got = lax.ppermute(pieces, axis, pairs)
        mine = (me >> b) & 1
        lo = jnp.where(mine == 0, pieces, got)
        hi = jnp.where(mine == 0, got, pieces)
        both = jnp.stack([lo, hi], axis=dim + 1)
        shape = list(pieces.shape)
        shape[dim] = shape[dim] * 2
        pieces = both.reshape(shape)
    shape = list(shard.shape)
    shape[dim] = shape[dim] * peers
    return pieces.reshape(shape)


def scatter_rows(full, axis, dim):
    peers = lax.axis_size(axis)
    me = lax.axis_index(axis)
    nbits = peers.bit_length() - 1
    rows = full.shape[dim] // peers
    shape = list(full.shape)
    blocks = full.reshape(shape[:dim] + [2] * nbits + [rows] + shape[dim + 1:])
    for b in bit_order(peers):
        where = dim + (nbits - 1 - b)
        mine = (me >> b) & 1
        keep = lax.dynamic_index_in_dim(blocks, mine, axis=where, keepdims=False)
        send = lax.dynamic_index_in_dim(blocks, 1 - mine, axis=where, keepdims=False)
        pairs = [(i, i ^ (1 << b)) for i in range(peers)]
        got = lax.ppermute(send, axis, pairs)
        blocks = keep + got
    return blocks


def source_plane(rows_x, rows_y, amounts, width_x, width_y):
    onehot_x = (rows_x[:, None] == jnp.arange(width_x, dtype=jnp.int32)[None, :]).astype(
        jnp.float32
    )
    onehot_y = (rows_y[:, None] == jnp.arange(width_y, dtype=jnp.int32)[None, :]).astype(
        jnp.float32
    )
    return jnp.dot((onehot_x * amounts[:, None]).T, onehot_y, precision=lax.Precision.HIGHEST)


def body(adj_now, adj_prev, fwd_snap, velocity, density, shot_count, rec_x, rec_y, residual):
    width_x = adj_now.shape[2]
    width_y = adj_now.shape[3]
    steps = fwd_snap.shape[1]
    groups = lax.axis_size("shots")
    adj_ext = with_halo(jnp.stack([adj_now[0], adj_prev[0]]), (("depth", 1),), HALO)
    local = jnp.stack([density * velocity * velocity, 1.0 / density])
    local_ext = with_halo(local, (("depth", 1),), HALO)
    mat_ext = gather_rows(local_ext, "shots", 2)
    holds_source = (lax.axis_index("depth") == 0).astype(jnp.float32)
    src = jnp.stack(
        [source_plane(rec_x[0], rec_y[0], residual[0, t], width_x, width_y) for t in range(steps)]
    ) * holds_source
    count = shot_count.astype(jnp.float32)
    current, older, weighted = run_steps(count, adj_ext, mat_ext, fwd_snap[0], src)
    summed = scatter_rows(weighted, "shots", 1)
    grad_vel = 2.0 * density * velocity * summed / (4.0 * groups)
    return (current[None], older[None], grad_vel)


def solution(mesh):
    in_specs = (
        P("shots", "depth", None, None),
        P("shots", "depth", None, None),
        P("shots", None, "depth", None, None),
        P("depth", "shots", None),
        P("depth", "shots", None),
        P("shots"),
        P("shots", None),
        P("shots", None),
        P("shots", None, None),
    )
    out_specs = (
        P("shots", "depth", None, None),
        P("shots", "depth", None, None),
        P("depth", "shots", None),
    )
    return jax.shard_map(body, mesh=mesh, in_specs=in_specs, out_specs=out_specs, check_vma=False)
```

profile of v0, /device:TPU:6, one launch (start us, length us, event | category | flops | bytes accessed | tf_op | source)
XLA Modules:
  0.0 144.1 jit_solution(633122813292375610)
XLA Ops:
  0.6 0.8 fusion.20
  1.4 5.0 %collective-permute-start.2 = (f32[2,4,4,128]{3,1,2,0:T(4,128)S(1)}, f32[2,4,4,128]{3,1,2,0:T(4,128)S(1)}, u32[]{:S(2)}, u32[]{:S(2)}) collective-permute-start(f32[2,4,4,128]{3,1,2,0:T(4,128)S(1)} %get-tuple-element.26), channel_id=1, source_target_pairs={{0,32},{32,64},{64,96},{96,128},{128,160},{160,192},{192,224},{1,3... | collective-permute-start | bytes 49160 | tf_op jit(solution)/shard_map/ppermute | solution.py:128
  6.5 1.9 %collective-permute-start.3 = (f32[2,4,4,128]{3,1,2,0:T(4,128)S(1)}, f32[2,4,4,128]{3,1,2,0:T(4,128)S(1)}, u32[]{:S(2)}, u32[]{:S(2)}) collective-permute-start(f32[2,4,4,128]{3,1,2,0:T(4,128)S(1)} %get-tuple-element.27), channel_id=1, source_target_pairs={{32,0},{64,32},{96,64},{128,96},{160,128},{192,160},{224,192},{33,... | collective-permute-start | bytes 49160 | tf_op jit(solution)/shard_map/ppermute | solution.py:129
  8.4 0.0 collective-permute-done.2
  8.4 7.3 %collective-permute-done.3 = f32[2,4,4,128]{3,1,2,0:T(4,128)S(1)} collective-permute-done((f32[2,4,4,128]{3,1,2,0:T(4,128)S(1)}, f32[2,4,4,128]{3,1,2,0:T(4,128)S(1)}, u32[]{:S(2)}, u32[]{:S(2)}) %collective-permute-start.3) | collective-permute-done | bytes 16416 | tf_op jit(solution)/shard_map/ppermute | solution.py:129
  15.7 7.3 %collective-permute-start.4 = (f32[2,24,1,4,128]{4,1,3,0,2:T(8,128)S(1)}, f32[2,24,1,4,128]{4,1,3,0,2:T(8,128)S(1)}, u32[]{:S(2)}, u32[]{:S(2)}) collective-permute-start(f32[2,24,1,4,128]{4,1,3,0,2:T(8,128)S(1)} %maximum_bitcast_fusion.1), channel_id=1, source_target_pairs={{0,16},{1,17},{2,18},{3,19},{4,20},{5,21},{6,22},{7,23},{8,24},{9,... | collective-permute-start | bytes 294920 | tf_op jit(solution)/shard_map/ppermute | solution.py:144
  23.0 2.8 %collective-permute-done.4 = f32[2,24,1,4,128]{4,1,3,0,2:T(8,128)S(1)} collective-permute-done((f32[2,24,1,4,128]{4,1,3,0,2:T(8,128)S(1)}, f32[2,24,1,4,128]{4,1,3,0,2:T(8,128)S(1)}, u32[]{:S(2)}, u32[]{:S(2)}) %collective-permute-start.4) | collective-permute-done | bytes 98336 | tf_op jit(solution)/shard_map/ppermute | solution.py:144
  25.8 3.1 %collective-permute-start.5 = (f32[2,24,2,4,128]{4,1,3,2,0:T(8,128)S(1)}, f32[2,24,2,4,128]{4,1,3,2,0:T(8,128)S(1)}, u32[]{:S(2)}, u32[]{:S(2)}) collective-permute-start(f32[2,24,2,4,128]{4,1,3,2,0:T(8,128)S(1)} %maximum_bitcast_fusion), channel_id=1, source_target_pairs={{0,8},{1,9},{2,10},{3,11},{4,12},{5,13},{6,14},{7,15},{8,0},{9,1},... | collective-permute-start | bytes 589832 | tf_op jit(solution)/shard_map/ppermute | solution.py:144
  28.9 7.5 %collective-permute-done.5 = f32[2,24,2,4,128]{4,1,3,2,0:T(8,128)S(1)} collective-permute-done((f32[2,24,2,4,128]{4,1,3,2,0:T(8,128)S(1)}, f32[2,24,2,4,128]{4,1,3,2,0:T(8,128)S(1)}, u32[]{:S(2)}, u32[]{:S(2)}) %collective-permute-start.5) | collective-permute-done | bytes 196640 | tf_op jit(solution)/shard_map/ppermute | solution.py:144
  36.4 0.1 collective-permute-start.6
  36.6 10.7 %collective-permute-done.6 = f32[2,24,4,4,128]{4,1,3,2,0:T(8,128)S(1)} collective-permute-done((f32[2,24,4,4,128]{4,1,3,2,0:T(8,128)S(1)}, f32[2,24,4,4,128]{4,1,3,2,0:T(8,128)S(1)}, u32[]{:S(2)}, u32[]{:S(2)}) %collective-permute-start.6) | collective-permute-done | bytes 393248 | tf_op jit(solution)/shard_map/ppermute | solution.py:144
  47.3 0.1 select_bitcast_fusion.5
  47.3 0.1 pad_maximum_fusion.3
  47.4 0.1 copy.41
  47.5 0.8 collective-permute-start.7
  48.2 17.6 %collective-permute-done.7 = f32[2,24,8,4,128]{4,1,3,2,0:T(8,128)S(1)} collective-permute-done((f32[2,24,8,4,128]{4,1,3,2,0:T(8,128)S(1)}, f32[2,24,8,4,128]{4,1,3,2,0:T(8,128)S(1)}, u32[]{:S(2)}, u32[]{:S(2)}) %collective-permute-start.7) | collective-permute-done | bytes 786464 | tf_op jit(solution)/shard_map/ppermute | solution.py:144
  65.9 0.1 select_bitcast_fusion.3
  66.0 0.1 pad_maximum_fusion.2
  66.1 0.0 copy-start.1
  66.1 0.0 copy-start.2
  66.1 1.3 copy.42
  67.4 0.0 collective-permute-start.8
  67.4 0.2 copy-done.1
  67.7 0.1 constant_dynamic-update-slice_fusion.1
  67.8 0.5 copy-done.2
  68.2 0.1 constant_dynamic-update-slice_fusion
  68.3 1.0 fusion.27
  69.4 2.3 %collective-permute-start = (f32[2,4,128,128]{3,2,1,0:T(8,128)}, f32[2,4,128,128]{3,2,1,0:T(8,128)S(1)}, u32[]{:S(2)}, u32[]{:S(2)}) collective-permute-start(f32[2,4,128,128]{3,2,1,0:T(8,128)} %get-tuple-element.14), channel_id=1, source_target_pairs={{0,32},{32,64},{64,96},{96,128},{128,160},{160,192},{192,224},{1,3... | collective-permute-start | bytes 1572872 | tf_op jit(solution)/shard_map/ppermute | solution.py:128
  71.7 3.5 %collective-permute-start.1 = (f32[2,4,128,128]{3,2,1,0:T(8,128)}, f32[2,4,128,128]{3,2,1,0:T(8,128)S(1)}, u32[]{:S(2)}, u32[]{:S(2)}) collective-permute-start(f32[2,4,128,128]{3,2,1,0:T(8,128)} %get-tuple-element.15), channel_id=1, source_target_pairs={{32,0},{64,32},{96,64},{128,96},{160,128},{192,160},{224,192},{33,... | collective-permute-start | bytes 1572872 | tf_op jit(solution)/shard_map/ppermute | solution.py:129
  75.2 0.0 copy-done.5
  75.2 0.0 copy-done.6
  75.2 0.0 copy-done.7
  75.3 0.4 convolution_bitcast_fusion
  76.3 0.4 convolution_bitcast_fusion.1
  76.7 0.4 convolution_bitcast_fusion.2
  77.1 0.4 convolution_bitcast_fusion.3
  77.6 7.6 %collective-permute-done = f32[2,4,128,128]{3,2,1,0:T(8,128)S(1)} collective-permute-done((f32[2,4,128,128]{3,2,1,0:T(8,128)}, f32[2,4,128,128]{3,2,1,0:T(8,128)S(1)}, u32[]{:S(2)}, u32[]{:S(2)}) %collective-permute-start) | collective-permute-done | bytes 524320 | tf_op jit(solution)/shard_map/ppermute | solution.py:128
  85.2 5.6 %collective-permute-done.1 = f32[2,4,128,128]{3,2,1,0:T(8,128)S(1)} collective-permute-done((f32[2,4,128,128]{3,2,1,0:T(8,128)}, f32[2,4,128,128]{3,2,1,0:T(8,128)S(1)}, u32[]{:S(2)}, u32[]{:S(2)}) %collective-permute-start.1) | collective-permute-done | bytes 524320 | tf_op jit(solution)/shard_map/ppermute | solution.py:129
  90.8 1.8 %pad_maximum_fusion.adj_ref = f32[2,24,128,128]{3,2,1,0:T(8,128)} fusion(f32[2,4,128,128]{3,2,1,0:T(8,128)S(1)} %collective-permute-done.1, f32[2,16,128,128]{3,2,1,0:T(8,128)S(1)} %constant_dynamic-update-slice_fusion, f32[2,4,128,128]{3,2,1,0:T(8,128)S(1)} %collective-permute-done), kind=kLoop, calls=%fused_computation | loop fusion | flops 1572864 | bytes 6291456 | tf_op jit(solution)/shard_map/concatenate | solution.py:130
  92.6 0.0 collective-permute-done.8
  92.6 2.2 %select_bitcast_fusion.1 = (f32[2,24,16,1,4,128]{5,1,4,2,0,3:T(8,128)S(1)}, f32[2,24,16,1,4,128]{5,1,4,2,0,3:T(8,128)S(1)}) fusion(f32[2,24,16,4,128]{4,1,3,2,0:T(8,128)} %bitcast.16, f32[2,24,16,4,128]{4,1,3,2,0:T(8,128)} %collective-permute-done.8, pred[]{:T(512)S(6)} %eq.28), kind=kLoop, calls=%fused_computation.4 | loop fusion | flops 786432 | bytes 6291457 | tf_op jit(solution)/shard_map/stack | solution.py:148
  94.8 0.2 pad_maximum_fusion.1
  95.0 0.0 copy-start
  95.0 2.5 %copy.43 = f32[2,24,16,2,4,128]{5,4,3,2,1,0:T(4,128)} copy(f32[2,24,16,2,4,128]{5,1,4,2,0,3:T(8,128)S(1)} %pad_maximum_fusion.1) | data formatting | bytes 6291456 | tf_op jit(solution)/shard_map/stack | solution.py:148
  97.5 0.0 copy-done
  97.5 15.5 %shard_map.112 = (f32[16,128,128]{2,1,0:T(8,128)}, f32[16,128,128]{2,1,0:T(8,128)}, f32[16,128,128]{2,1,0:T(8,128)S(1)}) custom-call(f32[1]{0:T(128)S(6)} %convert_element_type.4.count_ref, f32[2,24,128,128]{3,2,1,0:T(8,128)} %pad_maximum_fusion.adj_ref, f32[2,24,128,128]{3,2,1,0:T(8,128)} %bitcast.89, bf16[4,16,128,128]{3,2,1,0:T(8,128)(2,1)S(1)} %bitcast.87, ...), custom_call_target="tpu_custom_call" | custom-call | tf_op jit(solution)/shard_map/pallas_call | solution.py:110
  113.0 0.2 constant_dynamic-slice_fusion.1
  113.2 0.3 copy.56
  113.5 0.0 copy-start.3
  113.5 0.0 copy-start.4
  113.6 0.1 collective-permute-start.9
  113.7 1.9 %collective-permute-done.9 = f32[16,2,2,2,2,4,128]{6,0,5,4,3,2,1:T(8,128)S(1)} collective-permute-done((f32[16,2,2,2,2,4,128]{6,0,5,4,3,2,1:T(8,128)S(1)}, f32[16,2,2,2,2,4,128]{6,0,5,4,3,2,1:T(8,128)S(1)}, u32[]{:S(2)}, u32[]{:S(2)}) %collective-permute-start.9) | collective-permute-done | bytes 524320 | tf_op jit(solution)/shard_map/ppermute | solution.py:170
  115.6 0.3 bitcast_add_fusion
  115.9 0.8 collective-permute-start.10
  116.7 7.7 %collective-permute-done.10 = f32[16,2,2,2,4,128]{5,0,4,3,2,1:T(8,128)S(1)} collective-permute-done((f32[16,2,2,2,4,128]{5,0,4,3,2,1:T(8,128)S(1)}, f32[16,2,2,2,4,128]{5,0,4,3,2,1:T(8,128)S(1)}, u32[]{:S(2)}, u32[]{:S(2)}) %collective-permute-start.10) | collective-permute-done | bytes 262176 | tf_op jit(solution)/shard_map/ppermute | solution.py:170
  124.4 0.7 collective-permute-start.11
  125.1 4.4 %collective-permute-done.11 = f32[16,2,2,4,128]{4,0,3,2,1:T(8,128)S(1)} collective-permute-done((f32[16,2,2,4,128]{4,0,3,2,1:T(8,128)S(1)}, f32[16,2,2,4,128]{4,0,3,2,1:T(8,128)S(1)}, u32[]{:S(2)}, u32[]{:S(2)}) %collective-permute-start.11) | collective-permute-done | bytes 131104 | tf_op jit(solution)/shard_map/ppermute | solution.py:170
  129.5 0.1 collective-permute-start.12
  129.6 5.9 %collective-permute-done.12 = f32[16,2,4,128]{3,0,2,1:T(8,128)S(1)} collective-permute-done((f32[16,2,4,128]{3,0,2,1:T(8,128)S(1)}, f32[16,2,4,128]{3,0,2,1:T(8,128)S(1)}, u32[]{:S(2)}, u32[]{:S(2)}) %collective-permute-start.12) | collective-permute-done | bytes 65568 | tf_op jit(solution)/shard_map/ppermute | solution.py:170
  135.5 3.9 %collective-permute-start.13 = (f32[16,4,128]{2,0,1:T(8,128)S(1)}, f32[16,4,128]{2,0,1:T(8,128)S(1)}, u32[]{:S(2)}, u32[]{:S(2)}) collective-permute-start(f32[16,4,128]{2,0,1:T(8,128)S(1)} %dynamic-slice_bitcast_fusion.3), channel_id=1, source_target_pairs={{0,16},{1,17},{2,18},{3,19},{4,20},{5,21},{6,22},{7,23},{8,24},{9,... | collective-permute-start | bytes 98312 | tf_op jit(solution)/shard_map/ppermute | solution.py:170
  139.4 4.0 %collective-permute-done.13 = f32[16,4,128]{2,0,1:T(8,128)S(1)} collective-permute-done((f32[16,4,128]{2,0,1:T(8,128)S(1)}, f32[16,4,128]{2,0,1:T(8,128)S(1)}, u32[]{:S(2)}, u32[]{:S(2)}) %collective-permute-start.13) | collective-permute-done | bytes 32800 | tf_op jit(solution)/shard_map/ppermute | solution.py:170
  143.4 0.0 copy-done.3
  143.4 0.0 copy-done.4
  143.4 0.6 copy.48
  (19 shorter events, 0.3 us)
Async XLA Ops:
  1.4 7.0 %collective-permute-start.2 = (f32[2,4,4,128]{3,1,2,0:T(4,128)S(1)}, f32[2,4,4,128]{3,1,2,0:T(4,128)S(1)}, u32[]{:S(2)}, u32[]{:S(2)}) collective-permute-start(f32[2,4,4,128]{3,1,2,0:T(4,128)S(1)} %get-tuple-element.26), channel_id=1, source_target_pairs={{0,32},{32,64},{64,96},{96,128},{128,160},{160,192},{192,224},{1,3... | collective-permute-start | bytes 49160 | tf_op jit(solution)/shard_map/ppermute | solution.py:128
  6.5 9.2 %collective-permute-start.3 = (f32[2,4,4,128]{3,1,2,0:T(4,128)S(1)}, f32[2,4,4,128]{3,1,2,0:T(4,128)S(1)}, u32[]{:S(2)}, u32[]{:S(2)}) collective-permute-start(f32[2,4,4,128]{3,1,2,0:T(4,128)S(1)} %get-tuple-element.27), channel_id=1, source_target_pairs={{32,0},{64,32},{96,64},{128,96},{160,128},{192,160},{224,192},{33,... | collective-permute-start | bytes 49160 | tf_op jit(solution)/shard_map/ppermute | solution.py:129
  15.7 10.0 %collective-permute-start.4 = (f32[2,24,1,4,128]{4,1,3,0,2:T(8,128)S(1)}, f32[2,24,1,4,128]{4,1,3,0,2:T(8,128)S(1)}, u32[]{:S(2)}, u32[]{:S(2)}) collective-permute-start(f32[2,24,1,4,128]{4,1,3,0,2:T(8,128)S(1)} %maximum_bitcast_fusion.1), channel_id=1, source_target_pairs={{0,16},{1,17},{2,18},{3,19},{4,20},{5,21},{6,22},{7,23},{8,24},{9,... | collective-permute-start | bytes 294920 | tf_op jit(solution)/shard_map/ppermute | solution.py:144
  25.8 10.5 %collective-permute-start.5 = (f32[2,24,2,4,128]{4,1,3,2,0:T(8,128)S(1)}, f32[2,24,2,4,128]{4,1,3,2,0:T(8,128)S(1)}, u32[]{:S(2)}, u32[]{:S(2)}) collective-permute-start(f32[2,24,2,4,128]{4,1,3,2,0:T(8,128)S(1)} %maximum_bitcast_fusion), channel_id=1, source_target_pairs={{0,8},{1,9},{2,10},{3,11},{4,12},{5,13},{6,14},{7,15},{8,0},{9,1},... | collective-permute-start | bytes 589832 | tf_op jit(solution)/shard_map/ppermute | solution.py:144
  36.4 10.8 %collective-permute-start.6 = (f32[2,24,4,4,128]{4,1,3,2,0:T(8,128)S(1)}, f32[2,24,4,4,128]{4,1,3,2,0:T(8,128)S(1)}, u32[]{:S(2)}, u32[]{:S(2)}) collective-permute-start(f32[2,24,4,4,128]{4,1,3,2,0:T(8,128)S(1)} %bitcast.92), channel_id=1, source_target_pairs={{0,4},{1,5},{2,6},{3,7},{4,0},{5,1},{6,2},{7,3},{8,12},{9,13},{10,... | collective-permute-start | bytes 1179656 | tf_op jit(solution)/shard_map/ppermute | solution.py:144
  47.5 18.4 %collective-permute-start.7 = (f32[2,24,8,4,128]{4,1,3,2,0:T(8,128)S(1)}, f32[2,24,8,4,128]{4,1,3,2,0:T(8,128)S(1)}, u32[]{:S(2)}, u32[]{:S(2)}) collective-permute-start(f32[2,24,8,4,128]{4,1,3,2,0:T(8,128)S(1)} %bitcast.90), channel_id=1, source_target_pairs={{0,2},{1,3},{2,0},{3,1},{4,6},{5,7},{6,4},{7,5},{8,10},{9,11},{10,... | collective-permute-start | bytes 2359304 | tf_op jit(solution)/shard_map/ppermute | solution.py:144
  66.1 1.6 %copy-start.1 = (f32[1,16,128,128]{3,2,1,0:T(8,128)S(1)}, f32[1,16,128,128]{3,2,1,0:T(8,128)}, u32[]{:S(2)}) copy-start(f32[1,16,128,128]{3,2,1,0:T(8,128)} %param.9) | copy-start | bytes 3145732
  66.1 2.1 %copy-start.2 = (f32[1,16,128,128]{3,2,1,0:T(8,128)S(1)}, f32[1,16,128,128]{3,2,1,0:T(8,128)}, u32[]{:S(2)}) copy-start(f32[1,16,128,128]{3,2,1,0:T(8,128)} %param.10) | copy-start | bytes 3145732
  67.4 25.2 %collective-permute-start.8 = (f32[2,24,16,4,128]{4,1,3,2,0:T(8,128)}, f32[2,24,16,4,128]{4,1,3,2,0:T(8,128)}, u32[]{:S(2)}, u32[]{:S(2)}) collective-permute-start(f32[2,24,16,4,128]{4,1,3,2,0:T(8,128)} %bitcast.16), channel_id=1, source_target_pairs={{0,1},{1,0},{2,3},{3,2},{4,5},{5,4},{6,7},{7,6},{8,9},{9,8},{10,11... | collective-permute-start | bytes 4718600 | tf_op jit(solution)/shard_map/ppermute | solution.py:144
  68.2 7.0 %copy-start.5 = (f32[1,4,256]{2,1,0:T(4,128)S(1)}, f32[1,4,256]{2,1,0:T(4,128)}, u32[]{:S(2)}) copy-start(f32[1,4,256]{2,1,0:T(4,128)} %param.17) | copy-start | bytes 12292
  68.2 7.0 %copy-start.6 = (s32[1,256]{1,0:T(1,128)S(1)}, s32[1,256]{1,0:T(1,128)}, u32[]{:S(2)}) copy-start(s32[1,256]{1,0:T(1,128)} %param.16) | copy-start | bytes 3076
  68.2 7.0 %copy-start.7 = (s32[1,256]{1,0:T(1,128)S(1)}, s32[1,256]{1,0:T(1,128)}, u32[]{:S(2)}) copy-start(s32[1,256]{1,0:T(1,128)} %param.15) | copy-start | bytes 3076
  69.4 15.8 %collective-permute-start = (f32[2,4,128,128]{3,2,1,0:T(8,128)}, f32[2,4,128,128]{3,2,1,0:T(8,128)S(1)}, u32[]{:S(2)}, u32[]{:S(2)}) collective-permute-start(f32[2,4,128,128]{3,2,1,0:T(8,128)} %get-tuple-element.14), channel_id=1, source_target_pairs={{0,32},{32,64},{64,96},{96,128},{128,160},{160,192},{192,224},{1,3... | collective-permute-start | bytes 1572872 | tf_op jit(solution)/shard_map/ppermute | solution.py:128
  71.7 19.1 %collective-permute-start.1 = (f32[2,4,128,128]{3,2,1,0:T(8,128)}, f32[2,4,128,128]{3,2,1,0:T(8,128)S(1)}, u32[]{:S(2)}, u32[]{:S(2)}) collective-permute-start(f32[2,4,128,128]{3,2,1,0:T(8,128)} %get-tuple-element.15), channel_id=1, source_target_pairs={{32,0},{64,32},{96,64},{128,96},{160,128},{192,160},{224,192},{33,... | collective-permute-start | bytes 1572872 | tf_op jit(solution)/shard_map/ppermute | solution.py:129
  95.0 2.5 %copy-start = (bf16[1,4,16,128,128]{4,3,2,1,0:T(8,128)(2,1)S(1)}, bf16[1,4,16,128,128]{4,3,2,1,0:T(8,128)(2,1)}, u32[]{:S(2)}) copy-start(bf16[1,4,16,128,128]{4,3,2,1,0:T(8,128)(2,1)} %param.11) | copy-start | bytes 6291460
  113.5 29.9 %copy-start.3 = (f32[16,4,128]{2,1,0:T(4,128)S(1)}, f32[16,4,128]{2,1,0:T(4,128)}, u32[]{:S(2)}) copy-start(f32[16,4,128]{2,1,0:T(4,128)} %param.12) | copy-start | bytes 98308
  113.5 29.9 %copy-start.4 = (f32[16,4,128]{2,1,0:T(4,128)S(1)}, f32[16,4,128]{2,1,0:T(4,128)}, u32[]{:S(2)}) copy-start(f32[16,4,128]{2,1,0:T(4,128)} %param.13) | copy-start | bytes 98308
  113.6 2.0 %collective-permute-start.9 = (f32[16,2,2,2,2,4,128]{6,0,5,4,3,2,1:T(8,128)S(1)}, f32[16,2,2,2,2,4,128]{6,0,5,4,3,2,1:T(8,128)S(1)}, u32[]{:S(2)}, u32[]{:S(2)}) collective-permute-start(f32[16,2,2,2,2,4,128]{6,0,5,4,3,2,1:T(8,128)S(1)} %bitcast.94), channel_id=1, source_target_pairs={{0,1},{1,0},{2,3},{3,2},{4,5},{5,4},{6,7},{7,6},{8,9},{9,8},{10,11... | collective-permute-start | bytes 1572872 | tf_op jit(solution)/shard_map/ppermute | solution.py:170
  115.9 8.4 %collective-permute-start.10 = (f32[16,2,2,2,4,128]{5,0,4,3,2,1:T(8,128)S(1)}, f32[16,2,2,2,4,128]{5,0,4,3,2,1:T(8,128)S(1)}, u32[]{:S(2)}, u32[]{:S(2)}) collective-permute-start(f32[16,2,2,2,4,128]{5,0,4,3,2,1:T(8,128)S(1)} %dynamic-slice_bitcast_fusion), channel_id=1, source_target_pairs={{0,2},{1,3},{2,0},{3,1},{4,6},{5,7},{6,4},{7,5},{8,10},{9,11},{10,... | collective-permute-start | bytes 786440 | tf_op jit(solution)/shard_map/ppermute | solution.py:170
  124.4 5.1 %collective-permute-start.11 = (f32[16,2,2,4,128]{4,0,3,2,1:T(8,128)S(1)}, f32[16,2,2,4,128]{4,0,3,2,1:T(8,128)S(1)}, u32[]{:S(2)}, u32[]{:S(2)}) collective-permute-start(f32[16,2,2,4,128]{4,0,3,2,1:T(8,128)S(1)} %dynamic-slice_bitcast_fusion.1), channel_id=1, source_target_pairs={{0,4},{1,5},{2,6},{3,7},{4,0},{5,1},{6,2},{7,3},{8,12},{9,13},{10,... | collective-permute-start | bytes 393224 | tf_op jit(solution)/shard_map/ppermute | solution.py:170
  129.5 6.0 %collective-permute-start.12 = (f32[16,2,4,128]{3,0,2,1:T(8,128)S(1)}, f32[16,2,4,128]{3,0,2,1:T(8,128)S(1)}, u32[]{:S(2)}, u32[]{:S(2)}) collective-permute-start(f32[16,2,4,128]{3,0,2,1:T(8,128)S(1)} %dynamic-slice_bitcast_fusion.2), channel_id=1, source_target_pairs={{0,8},{1,9},{2,10},{3,11},{4,12},{5,13},{6,14},{7,15},{8,0},{9,1},... | collective-permute-start | bytes 196616 | tf_op jit(solution)/shard_map/ppermute | solution.py:170
  135.5 7.9 %collective-permute-start.13 = (f32[16,4,128]{2,0,1:T(8,128)S(1)}, f32[16,4,128]{2,0,1:T(8,128)S(1)}, u32[]{:S(2)}, u32[]{:S(2)}) collective-permute-start(f32[16,4,128]{2,0,1:T(8,128)S(1)} %dynamic-slice_bitcast_fusion.3), channel_id=1, source_target_pairs={{0,16},{1,17},{2,18},{3,19},{4,20},{5,21},{6,22},{7,23},{8,24},{9,... | collective-permute-start | bytes 98312 | tf_op jit(solution)/shard_map/ppermute | solution.py:170
where the time goes:
time: 144 us
  waiting for transfers between devices  82.9 us (58%)
  starting transfers between devices  29.5 us (20%)
  Pallas kernels  15.5 us (11%)
  local copies, waits for them, and re-layouts  7.04 us (5%)
  other arithmetic  5.87 us (4%)
  between operations  1.65 us (1%)
  matrix products  1.61 us (1%)
    ppermute x5, waiting for transfers between devices, gather_rows(): got = lax.ppermute(pieces, axis, pairs)  38.6 us
    ppermute x5, waiting for transfers between devices, scatter_rows(): got = lax.ppermute(send, axis, pairs)  23.8 us
    pallas_call x1, Pallas kernels, run_steps(): pl.pallas_call(stencil_kernel, out_shape=out_shape, in_specs=[pl.BlockSpe...  15.5 us
    ppermute x2, waiting for transfers between devices, with_halo(): after = lax.ppermute(first, axis, down)  12.9 us
    ppermute x5, starting transfers between devices, gather_rows(): got = lax.ppermute(pieces, axis, pairs)  11.2 us
    ppermute x2, waiting for transfers between devices, with_halo(): before = lax.ppermute(last, axis, up)  7.58 us
    ppermute x2, starting transfers between devices, with_halo(): before = lax.ppermute(last, axis, up)  7.3 us
    ppermute x5, starting transfers between devices, scatter_rows(): got = lax.ppermute(send, axis, pairs)  5.55 us
  transfers between devices with their start and end apart: 14, of which 12 were waited for; matrix products, arithmetic and copies ran while one was open for 3% of the time, Pallas kernels for 0%

commit v1 on v0

--- a/solution.py
+++ b/solution.py
@@ -131,15 +131,20 @@
     return shard
 
 
-def bit_order(peers):
-    return list(range(peers.bit_length() - 1))
-
-
-def gather_rows(shard, axis, dim):
+def gather_rows(shard, axis, dim, direct):
     peers = lax.axis_size(axis)
     me = lax.axis_index(axis)
-    pieces = jnp.expand_dims(shard, dim)
-    for b in reversed(bit_order(peers)):
+    nbits = peers.bit_length() - 1
+    low = nbits - direct
+    span, stride = 1 << direct, 1 << low
+    top = me >> low
+    got = [shard]
+    for k in range(1, span):
+        pairs = [(i, (((i >> low) + k) % span) * stride + (i % stride)) for i in range(peers)]
+        got.append(lax.ppermute(shard, axis, pairs))
+    ahead = jnp.stack([got[0]] + got[1:][::-1], axis=dim)
+    pieces = jnp.roll(ahead, top, axis=dim)
+    for b in reversed(range(low)):
         pairs = [(i, i ^ (1 << b)) for i in range(peers)]
         got = lax.ppermute(pieces, axis, pairs)
         mine = (me >> b) & 1
@@ -154,22 +159,30 @@
     return pieces.reshape(shape)
 
 
-def scatter_rows(full, axis, dim):
+def scatter_rows(full, axis, dim, direct):
     peers = lax.axis_size(axis)
     me = lax.axis_index(axis)
     nbits = peers.bit_length() - 1
+    low = nbits - direct
+    span, stride = 1 << direct, 1 << low
+    top = me >> low
     rows = full.shape[dim] // peers
     shape = list(full.shape)
-    blocks = full.reshape(shape[:dim] + [2] * nbits + [rows] + shape[dim + 1:])
-    for b in bit_order(peers):
-        where = dim + (nbits - 1 - b)
+    blocks = full.reshape(shape[:dim] + [span] + [2] * low + [rows] + shape[dim + 1:])
+    for b in range(low):
+        where = dim + 1 + (low - 1 - b)
         mine = (me >> b) & 1
         keep = lax.dynamic_index_in_dim(blocks, mine, axis=where, keepdims=False)
         send = lax.dynamic_index_in_dim(blocks, 1 - mine, axis=where, keepdims=False)
         pairs = [(i, i ^ (1 << b)) for i in range(peers)]
         got = lax.ppermute(send, axis, pairs)
         blocks = keep + got
-    return blocks
+    total = lax.dynamic_index_in_dim(blocks, top, axis=dim, keepdims=False)
+    for k in range(1, span):
+        pairs = [(i, (((i >> low) + k) % span) * stride + (i % stride)) for i in range(peers)]
+        send = lax.dynamic_index_in_dim(blocks, (top + k) % span, axis=dim, keepdims=False)
+        total = total + lax.ppermute(send, axis, pairs)
+    return total
 
 
 def source_plane(rows_x, rows_y, amounts, width_x, width_y):
@@ -189,15 +202,15 @@
     groups = lax.axis_size("shots")
     adj_ext = with_halo(jnp.stack([adj_now[0], adj_prev[0]]), (("depth", 1),), HALO)
     local = jnp.stack([density * velocity * velocity, 1.0 / density])
-    local_ext = with_halo(local, (("depth", 1),), HALO)
-    mat_ext = gather_rows(local_ext, "shots", 2)
+    packed = gather_rows(local, "shots", 2, 3)
+    mat_ext = with_halo(packed, (("depth", 1),), HALO)
     holds_source = (lax.axis_index("depth") == 0).astype(jnp.float32)
     src = jnp.stack(
         [source_plane(rec_x[0], rec_y[0], residual[0, t], width_x, width_y) for t in range(steps)]
     ) * holds_source
     count = shot_count.astype(jnp.float32)
     current, older, weighted = run_steps(count, adj_ext, mat_ext, fwd_snap[0], src)
-    summed = scatter_rows(weighted, "shots", 1)
+    summed = scatter_rows(weighted, "shots", 1, 3)
     grad_vel = 2.0 * density * velocity * summed / (4.0 * groups)
     return (current[None], older[None], grad_vel)
 

time: 144 us -> 125 us (0.87)
  waiting for transfers between devices: 82.9 us -> 42.1 us
  starting transfers between devices: 29.5 us -> 51.7 us
  local copies, waits for them, and re-layouts: 7.04 us -> 3.49 us
  other arithmetic: 5.87 us -> 8.52 us
    ppermute x0 -> x14, starting transfers between devices: none -> 32.5 us  [the longest x7 17.4 us: gather_rows(): got.append(lax.ppermute(shard, axis, pairs))]
    ppermute x5 -> x2, waiting for transfers between devices: 38.6 us -> 11.1 us  [gather_rows(): got = lax.ppermute(pieces, axis, pairs)]
    ppermute x5 -> x2, waiting for transfers between devices: 23.8 us -> 9.55 us  [scatter_rows(): got = lax.ppermute(send, axis, pairs)]
    ppermute x5 -> x2, starting transfers between devices: 11.2 us -> 1.76 us  [gather_rows(): got = lax.ppermute(pieces, axis, pairs)]
    ppermute x0 -> x14, waiting for transfers between devices: none -> 9.26 us  [the longest x7 7.28 us: gather_rows(): got.append(lax.ppermute(shard, axis, pairs))]
    ppermute x2, waiting for transfers between devices: 7.58 us -> 1.81 us  [with_halo(): before = lax.ppermute(last, axis, up)]
    ppermute x2, starting transfers between devices: 7.3 us -> 12.5 us  [with_halo(): before = lax.ppermute(last, axis, up)]
    ppermute x5 -> x2, starting transfers between devices: 5.55 us -> 1.04 us  [scatter_rows(): got = lax.ppermute(send, axis, pairs)]
  transfers between devices with their start and end apart: 14 -> 22, of which waited for: 12 -> 12; matrix products, arithmetic and copies ran while one was open for 3% -> 7% of each run, Pallas kernels for 0% -> 0%
where the time goes in v1:
time: 125 us
  starting transfers between devices  51.7 us (41%)
  waiting for transfers between devices  42.1 us (34%)
  Pallas kernels  15.5 us (12%)
  other arithmetic  8.52 us (7%)
  local copies, waits for them, and re-layouts  3.49 us (3%)
  between operations  1.7 us (1%)
  matrix products  1.61 us (1%)
    ppermute x7, starting transfers between devices, gather_rows(): got.append(lax.ppermute(shard, axis, pairs))  17.4 us
    pallas_call x1, Pallas kernels, run_steps(): pl.pallas_call(stencil_kernel, out_shape=out_shape, in_specs=[pl.BlockSpe...  15.5 us
    ppermute x7, starting transfers between devices, scatter_rows(): total = total + lax.ppermute(send, axis, pairs)  15.1 us
    ppermute x2, starting transfers between devices, with_halo(): before = lax.ppermute(last, axis, up)  12.5 us
    ppermute x2, waiting for transfers between devices, gather_rows(): got = lax.ppermute(pieces, axis, pairs)  11.1 us
    ppermute x2, waiting for transfers between devices, with_halo(): after = lax.ppermute(first, axis, down)  10.4 us
    ppermute x2, waiting for transfers between devices, scatter_rows(): got = lax.ppermute(send, axis, pairs)  9.55 us
    ppermute x7, waiting for transfers between devices, gather_rows(): got.append(lax.ppermute(shard, axis, pairs))  7.28 us
  transfers between devices with their start and end apart: 22, of which 12 were waited for; matrix products, arithmetic and copies ran while one was open for 7% of the time, Pallas kernels for 0%

profile of v1, /device:TPU:6, one launch (start us, length us, event | category | flops | bytes accessed | tf_op | source)
XLA Modules:
  0.0 124.6 jit_solution(1952092548224811911)
XLA Ops:
  0.6 0.8 fusion.20
  1.4 5.9 %collective-permute-start.2 = (f32[2,16,4,128]{3,1,2,0:T(8,128)S(1)}, f32[2,16,4,128]{3,1,2,0:T(8,128)S(1)}, u32[]{:S(2)}, u32[]{:S(2)}) collective-permute-start(f32[2,16,4,128]{3,1,2,0:T(8,128)S(1)} %pad_maximum_fusion.4), channel_id=1, source_target_pairs={{0,28},{1,29},{2,30},{3,31},{4,0},{5,1},{6,2},{7,3},{8,4},{9,5},{1... | collective-permute-start | bytes 196616 | tf_op jit(solution)/shard_map/ppermute | solution.py:144
  7.4 1.5 %collective-permute-start.3 = (f32[2,16,4,128]{3,1,2,0:T(8,128)S(1)}, f32[2,16,4,128]{3,1,2,0:T(8,128)S(1)}, u32[]{:S(2)}, u32[]{:S(2)}) collective-permute-start(f32[2,16,4,128]{3,1,2,0:T(8,128)S(1)} %pad_maximum_fusion.4), channel_id=1, source_target_pairs={{0,24},{1,25},{2,26},{3,27},{4,28},{5,29},{6,30},{7,31},{8,0},{9,1... | collective-permute-start | bytes 196616 | tf_op jit(solution)/shard_map/ppermute | solution.py:144
  8.8 0.4 collective-permute-start.4
  9.3 5.0 %collective-permute-start.5 = (f32[2,16,4,128]{3,1,2,0:T(8,128)S(1)}, f32[2,16,4,128]{3,1,2,0:T(8,128)S(1)}, u32[]{:S(2)}, u32[]{:S(2)}) collective-permute-start(f32[2,16,4,128]{3,1,2,0:T(8,128)S(1)} %pad_maximum_fusion.4), channel_id=1, source_target_pairs={{0,16},{1,17},{2,18},{3,19},{4,20},{5,21},{6,22},{7,23},{8,24},{9,... | collective-permute-start | bytes 196616 | tf_op jit(solution)/shard_map/ppermute | solution.py:144
  14.3 0.0 collective-permute-start.6
  14.3 0.0 collective-permute-done.2
  14.3 2.5 %collective-permute-start.7 = (f32[2,16,4,128]{3,1,2,0:T(8,128)S(1)}, f32[2,16,4,128]{3,1,2,0:T(8,128)S(1)}, u32[]{:S(2)}, u32[]{:S(2)}) collective-permute-start(f32[2,16,4,128]{3,1,2,0:T(8,128)S(1)} %pad_maximum_fusion.4), channel_id=1, source_target_pairs={{0,8},{1,9},{2,10},{3,11},{4,12},{5,13},{6,14},{7,15},{8,16},{9,17... | collective-permute-start | bytes 196616 | tf_op jit(solution)/shard_map/ppermute | solution.py:144
  16.9 0.0 collective-permute-done.3
  16.9 2.0 %collective-permute-start.8 = (f32[2,16,4,128]{3,1,2,0:T(8,128)S(1)}, f32[2,16,4,128]{3,1,2,0:T(8,128)S(1)}, u32[]{:S(2)}, u32[]{:S(2)}) collective-permute-start(f32[2,16,4,128]{3,1,2,0:T(8,128)S(1)} %pad_maximum_fusion.4), channel_id=1, source_target_pairs={{0,4},{1,5},{2,6},{3,7},{4,8},{5,9},{6,10},{7,11},{8,12},{9,13},{1... | collective-permute-start | bytes 196616 | tf_op jit(solution)/shard_map/ppermute | solution.py:144
  18.9 0.1 collective-permute-done.4
  19.0 0.0 collective-permute-done.5
  19.0 5.1 %collective-permute-done.6 = f32[2,16,4,128]{3,1,2,0:T(8,128)S(1)} collective-permute-done((f32[2,16,4,128]{3,1,2,0:T(8,128)S(1)}, f32[2,16,4,128]{3,1,2,0:T(8,128)S(1)}, u32[]{:S(2)}, u32[]{:S(2)}) %collective-permute-start.6) | collective-permute-done | bytes 65568 | tf_op jit(solution)/shard_map/ppermute | solution.py:144
  24.2 2.0 %collective-permute-done.7 = f32[2,16,4,128]{3,1,2,0:T(8,128)S(1)} collective-permute-done((f32[2,16,4,128]{3,1,2,0:T(8,128)S(1)}, f32[2,16,4,128]{3,1,2,0:T(8,128)S(1)}, u32[]{:S(2)}, u32[]{:S(2)}) %collective-permute-start.7) | collective-permute-done | bytes 65568 | tf_op jit(solution)/shard_map/ppermute | solution.py:144
  26.4 1.7 %collective-permute-start.9 = (f32[2,16,8,4,128]{4,1,3,2,0:T(8,128)S(1)}, f32[2,16,8,4,128]{4,1,3,2,0:T(8,128)S(1)}, u32[]{:S(2)}, u32[]{:S(2)}) collective-permute-start(f32[2,16,8,4,128]{4,1,3,2,0:T(8,128)S(1)} %constant_dynamic-slice_fusion.2), channel_id=1, source_target_pairs={{0,2},{1,3},{2,0},{3,1},{4,6},{5,7},{6,4},{7,5},{8,10},{9,11},{10,... | collective-permute-start | bytes 1572872 | tf_op jit(solution)/shard_map/ppermute | solution.py:149
  28.1 11.1 %collective-permute-done.9 = f32[2,16,8,4,128]{4,1,3,2,0:T(8,128)S(1)} collective-permute-done((f32[2,16,8,4,128]{4,1,3,2,0:T(8,128)S(1)}, f32[2,16,8,4,128]{4,1,3,2,0:T(8,128)S(1)}, u32[]{:S(2)}, u32[]{:S(2)}) %collective-permute-start.9) | collective-permute-done | bytes 524320 | tf_op jit(solution)/shard_map/ppermute | solution.py:149
  39.1 0.1 select_bitcast_fusion.3
  39.2 0.0 copy-start.2
  39.3 0.1 pad_maximum_fusion.3
  39.3 0.1 collective-permute-start.10
  39.5 0.1 constant_dynamic-update-slice_fusion.1
  39.5 0.9 copy-done.2
  40.5 0.1 constant_dynamic-update-slice_fusion
  40.6 1.0 fusion.34
  41.6 5.0 %collective-permute-start = (f32[2,4,128,128]{3,2,1,0:T(8,128)}, f32[2,4,128,128]{3,2,1,0:T(8,128)}, u32[]{:S(2)}, u32[]{:S(2)}) collective-permute-start(f32[2,4,128,128]{3,2,1,0:T(8,128)} %get-tuple-element.13), channel_id=1, source_target_pairs={{0,32},{32,64},{64,96},{96,128},{128,160},{160,192},{192,224},{1,3... | collective-permute-start | bytes 1572872 | tf_op jit(solution)/shard_map/ppermute | solution.py:128
  46.6 1.9 %collective-permute-start.1 = (f32[2,4,128,128]{3,2,1,0:T(8,128)}, f32[2,4,128,128]{3,2,1,0:T(8,128)}, u32[]{:S(2)}, u32[]{:S(2)}) collective-permute-start(f32[2,4,128,128]{3,2,1,0:T(8,128)} %get-tuple-element.14), channel_id=1, source_target_pairs={{32,0},{64,32},{96,64},{128,96},{160,128},{192,160},{224,192},{33,... | collective-permute-start | bytes 1572872 | tf_op jit(solution)/shard_map/ppermute | solution.py:129
  49.3 0.4 convolution_bitcast_fusion
  49.7 0.4 convolution_bitcast_fusion.1
  50.1 0.0 collective-permute-done.10
  50.1 1.4 %select_bitcast_fusion.1 = (f32[2,16,16,1,4,128]{5,1,4,2,0,3:T(8,128)S(1)}, f32[2,16,16,1,4,128]{5,1,4,2,0,3:T(8,128)S(1)}) fusion(f32[2,16,16,4,128]{4,1,3,2,0:T(8,128)S(1)} %bitcast.126, f32[2,16,16,4,128]{4,1,3,2,0:T(8,128)} %collective-permute-done.10, pred[]{:T(512)S(6)} %eq.32), kind=kLoop, calls=%fused_computation.9 | loop fusion | flops 524288 | bytes 4194305 | tf_op jit(solution)/shard_map/stack | solution.py:153
  51.5 0.1 pad_maximum_fusion.2
  51.6 0.8 copy.34
  52.5 0.1 fusion.33
  52.6 7.5 %collective-permute-start.11 = (f32[2,4,128,128]{3,2,1,0:T(8,128)S(1)}, f32[2,4,128,128]{3,2,1,0:T(8,128)S(1)}, u32[]{:S(2)}, u32[]{:S(2)}) collective-permute-start(f32[2,4,128,128]{3,2,1,0:T(8,128)S(1)} %get-tuple-element.9), channel_id=1, source_target_pairs={{0,32},{32,64},{64,96},{96,128},{128,160},{160,192},{192,224},{1,3... | collective-permute-start | bytes 1572872 | tf_op jit(solution)/shard_map/ppermute | solution.py:128
  60.1 1.9 %collective-permute-start.12 = (f32[2,4,128,128]{3,2,1,0:T(8,128)S(1)}, f32[2,4,128,128]{3,2,1,0:T(8,128)S(1)}, u32[]{:S(2)}, u32[]{:S(2)}) collective-permute-start(f32[2,4,128,128]{3,2,1,0:T(8,128)S(1)} %get-tuple-element.10), channel_id=1, source_target_pairs={{32,0},{64,32},{96,64},{128,96},{160,128},{192,160},{224,192},{33,... | collective-permute-start | bytes 1572872 | tf_op jit(solution)/shard_map/ppermute | solution.py:129
  62.0 0.4 convolution_bitcast_fusion.2
  62.4 0.4 convolution_bitcast_fusion.3
  62.9 2.7 %collective-permute-done.1 = f32[2,4,128,128]{3,2,1,0:T(8,128)} collective-permute-done((f32[2,4,128,128]{3,2,1,0:T(8,128)}, f32[2,4,128,128]{3,2,1,0:T(8,128)}, u32[]{:S(2)}, u32[]{:S(2)}) %collective-permute-start.1) | collective-permute-done | bytes 524320 | tf_op jit(solution)/shard_map/ppermute | solution.py:129
  65.6 3.1 %pad_maximum_fusion.adj_ref = f32[2,24,128,128]{3,2,1,0:T(8,128)} fusion(f32[2,4,128,128]{3,2,1,0:T(8,128)} %collective-permute-done.1, f32[2,16,128,128]{3,2,1,0:T(8,128)S(1)} %constant_dynamic-update-slice_fusion, f32[2,4,128,128]{3,2,1,0:T(8,128)} %collective-permute-done), kind=kLoop, calls=%fused_computation | loop fusion | flops 1572864 | bytes 6291456 | tf_op jit(solution)/shard_map/concatenate | solution.py:130
  68.6 1.8 %collective-permute-done.11 = f32[2,4,128,128]{3,2,1,0:T(8,128)S(1)} collective-permute-done((f32[2,4,128,128]{3,2,1,0:T(8,128)S(1)}, f32[2,4,128,128]{3,2,1,0:T(8,128)S(1)}, u32[]{:S(2)}, u32[]{:S(2)}) %collective-permute-start.11) | collective-permute-done | bytes 524320 | tf_op jit(solution)/shard_map/ppermute | solution.py:128
  70.4 7.7 %collective-permute-done.12 = f32[2,4,128,128]{3,2,1,0:T(8,128)S(1)} collective-permute-done((f32[2,4,128,128]{3,2,1,0:T(8,128)S(1)}, f32[2,4,128,128]{3,2,1,0:T(8,128)S(1)}, u32[]{:S(2)}, u32[]{:S(2)}) %collective-permute-start.12) | collective-permute-done | bytes 524320 | tf_op jit(solution)/shard_map/ppermute | solution.py:129
  78.2 2.0 %pad_maximum_fusion.1.mat_ref = f32[2,24,128,128]{3,2,1,0:T(8,128)} fusion(f32[2,4,128,128]{3,2,1,0:T(8,128)S(1)} %collective-permute-done.12, f32[2,16,128,128]{3,2,1,0:T(8,128)S(1)} %bitcast.124, f32[2,4,128,128]{3,2,1,0:T(8,128)S(1)} %collective-permute-done.11), kind=kLoop, calls=%fused_computation.1 | loop fusion | flops 1572864 | bytes 6291456 | tf_op jit(solution)/shard_map/concatenate | solution.py:130
  80.2 15.5 %shard_map.112 = (f32[16,128,128]{2,1,0:T(8,128)}, f32[16,128,128]{2,1,0:T(8,128)}, f32[16,128,128]{2,1,0:T(8,128)S(1)}) custom-call(f32[1]{0:T(128)S(6)} %convert_element_type.4.count_ref, f32[2,24,128,128]{3,2,1,0:T(8,128)} %pad_maximum_fusion.adj_ref, f32[2,24,128,128]{3,2,1,0:T(8,128)} %pad_maximum_fusion.1.mat_ref, ...), custom_call_target="tpu_custom_call" | custom-call | tf_op jit(solution)/shard_map/pallas_call | solution.py:110
  95.7 0.1 dynamic-slice_bitcast_fusion
  95.8 0.1 collective-permute-start.13
  95.9 0.0 copy-start.3
  95.9 0.0 copy-start.4
  95.9 1.9 %collective-permute-done.13 = f32[16,8,2,4,128]{4,3,2,1,0:T(4,128)S(1)} collective-permute-done((f32[16,8,2,4,128]{4,3,2,1,0:T(4,128)S(1)}, f32[16,8,2,4,128]{4,3,2,1,0:T(4,128)S(1)}, u32[]{:S(2)}, u32[]{:S(2)}) %collective-permute-start.13) | collective-permute-done | bytes 524320 | tf_op jit(solution)/shard_map/ppermute | solution.py:178
  97.8 0.1 bitcast_add_fusion
  97.9 0.1 constant_dynamic-slice_fusion.1
  98.1 0.9 collective-permute-start.14
  99.1 7.7 %collective-permute-done.14 = f32[16,8,4,128]{3,2,0,1:T(4,128)S(1)} collective-permute-done((f32[16,8,4,128]{3,2,0,1:T(4,128)S(1)}, f32[16,8,4,128]{3,2,0,1:T(4,128)S(1)}, u32[]{:S(2)}, u32[]{:S(2)}) %collective-permute-start.14) | collective-permute-done | bytes 262176 | tf_op jit(solution)/shard_map/ppermute | solution.py:178
  106.7 0.1 bitcast_add_fusion.1
  106.8 1.4 %collective-permute-start.15 = (f32[16,4,128]{2,1,0:T(4,128)S(1)}, f32[16,4,128]{2,1,0:T(4,128)S(1)}, u32[]{:S(2)}, u32[]{:S(2)}) collective-permute-start(f32[16,4,128]{2,1,0:T(4,128)S(1)} %get-tuple-element.19), channel_id=1, source_target_pairs={{0,4},{1,5},{2,6},{3,7},{4,8},{5,9},{6,10},{7,11},{8,12},{9,13},{1... | collective-permute-start | bytes 98312 | tf_op jit(solution)/shard_map/ppermute | solution.py:184
  108.2 1.8 %collective-permute-start.16 = (f32[16,4,128]{2,1,0:T(4,128)S(1)}, f32[16,4,128]{2,1,0:T(4,128)S(1)}, u32[]{:S(2)}, u32[]{:S(2)}) collective-permute-start(f32[16,4,128]{2,1,0:T(4,128)S(1)} %get-tuple-element.25), channel_id=1, source_target_pairs={{0,8},{1,9},{2,10},{3,11},{4,12},{5,13},{6,14},{7,15},{8,16},{9,17... | collective-permute-start | bytes 98312 | tf_op jit(solution)/shard_map/ppermute | solution.py:184
  110.0 1.3 %collective-permute-start.17 = (f32[16,4,128]{2,1,0:T(4,128)S(1)}, f32[16,4,128]{2,1,0:T(4,128)S(1)}, u32[]{:S(2)}, u32[]{:S(2)}) collective-permute-start(f32[16,4,128]{2,1,0:T(4,128)S(1)} %get-tuple-element.24), channel_id=1, source_target_pairs={{0,12},{1,13},{2,14},{3,15},{4,16},{5,17},{6,18},{7,19},{8,20},{9,... | collective-permute-start | bytes 98312 | tf_op jit(solution)/shard_map/ppermute | solution.py:184
  111.3 5.1 %collective-permute-start.18 = (f32[16,4,128]{2,1,0:T(4,128)S(1)}, f32[16,4,128]{2,1,0:T(4,128)S(1)}, u32[]{:S(2)}, u32[]{:S(2)}) collective-permute-start(f32[16,4,128]{2,1,0:T(4,128)S(1)} %get-tuple-element.23), channel_id=1, source_target_pairs={{0,16},{1,17},{2,18},{3,19},{4,20},{5,21},{6,22},{7,23},{8,24},{9,... | collective-permute-start | bytes 98312 | tf_op jit(solution)/shard_map/ppermute | solution.py:184
  116.4 1.6 %collective-permute-start.19 = (f32[16,4,128]{2,1,0:T(4,128)S(1)}, f32[16,4,128]{2,1,0:T(4,128)S(1)}, u32[]{:S(2)}, u32[]{:S(2)}) collective-permute-start(f32[16,4,128]{2,1,0:T(4,128)S(1)} %get-tuple-element.22), channel_id=1, source_target_pairs={{0,20},{1,21},{2,22},{3,23},{4,24},{5,25},{6,26},{7,27},{8,28},{9,... | collective-permute-start | bytes 98312 | tf_op jit(solution)/shard_map/ppermute | solution.py:184
  118.0 2.0 %collective-permute-start.20 = (f32[16,4,128]{2,1,0:T(4,128)S(1)}, f32[16,4,128]{2,1,0:T(4,128)S(1)}, u32[]{:S(2)}, u32[]{:S(2)}) collective-permute-start(f32[16,4,128]{2,1,0:T(4,128)S(1)} %get-tuple-element.21), channel_id=1, source_target_pairs={{0,24},{1,25},{2,26},{3,27},{4,28},{5,29},{6,30},{7,31},{8,0},{9,1... | collective-permute-start | bytes 98312 | tf_op jit(solution)/shard_map/ppermute | solution.py:184
  120.0 1.9 %collective-permute-start.21 = (f32[16,4,128]{2,1,0:T(4,128)S(1)}, f32[16,4,128]{2,1,0:T(4,128)S(1)}, u32[]{:S(2)}, u32[]{:S(2)}) collective-permute-start(f32[16,4,128]{2,1,0:T(4,128)S(1)} %get-tuple-element.20), channel_id=1, source_target_pairs={{0,28},{1,29},{2,30},{3,31},{4,0},{5,1},{6,2},{7,3},{8,4},{9,5},{1... | collective-permute-start | bytes 98312 | tf_op jit(solution)/shard_map/ppermute | solution.py:184
  122.0 0.4 collective-permute-done.19
  122.4 0.6 collective-permute-done.20
  123.0 1.0 collective-permute-done.21
  124.0 0.7 fusion.28
  (40 shorter events, 0.3 us)
Async XLA Ops:
  1.4 12.9 %collective-permute-start.2 = (f32[2,16,4,128]{3,1,2,0:T(8,128)S(1)}, f32[2,16,4,128]{3,1,2,0:T(8,128)S(1)}, u32[]{:S(2)}, u32[]{:S(2)}) collective-permute-start(f32[2,16,4,128]{3,1,2,0:T(8,128)S(1)} %pad_maximum_fusion.4), channel_id=1, source_target_pairs={{0,28},{1,29},{2,30},{3,31},{4,0},{5,1},{6,2},{7,3},{8,4},{9,5},{1... | collective-permute-start | bytes 196616 | tf_op jit(solution)/shard_map/ppermute | solution.py:144
  7.4 9.5 %collective-permute-start.3 = (f32[2,16,4,128]{3,1,2,0:T(8,128)S(1)}, f32[2,16,4,128]{3,1,2,0:T(8,128)S(1)}, u32[]{:S(2)}, u32[]{:S(2)}) collective-permute-start(f32[2,16,4,128]{3,1,2,0:T(8,128)S(1)} %pad_maximum_fusion.4), channel_id=1, source_target_pairs={{0,24},{1,25},{2,26},{3,27},{4,28},{5,29},{6,30},{7,31},{8,0},{9,1... | collective-permute-start | bytes 196616 | tf_op jit(solution)/shard_map/ppermute | solution.py:144
  8.8 10.2 %collective-permute-start.4 = (f32[2,16,4,128]{3,1,2,0:T(8,128)S(1)}, f32[2,16,4,128]{3,1,2,0:T(8,128)S(1)}, u32[]{:S(2)}, u32[]{:S(2)}) collective-permute-start(f32[2,16,4,128]{3,1,2,0:T(8,128)S(1)} %pad_maximum_fusion.4), channel_id=1, source_target_pairs={{0,20},{1,21},{2,22},{3,23},{4,24},{5,25},{6,26},{7,27},{8,28},{9,... | collective-permute-start | bytes 196616 | tf_op jit(solution)/shard_map/ppermute | solution.py:144
  9.3 9.8 %collective-permute-start.5 = (f32[2,16,4,128]{3,1,2,0:T(8,128)S(1)}, f32[2,16,4,128]{3,1,2,0:T(8,128)S(1)}, u32[]{:S(2)}, u32[]{:S(2)}) collective-permute-start(f32[2,16,4,128]{3,1,2,0:T(8,128)S(1)} %pad_maximum_fusion.4), channel_id=1, source_target_pairs={{0,16},{1,17},{2,18},{3,19},{4,20},{5,21},{6,22},{7,23},{8,24},{9,... | collective-permute-start | bytes 196616 | tf_op jit(solution)/shard_map/ppermute | solution.py:144
  14.3 9.9 %collective-permute-start.6 = (f32[2,16,4,128]{3,1,2,0:T(8,128)S(1)}, f32[2,16,4,128]{3,1,2,0:T(8,128)S(1)}, u32[]{:S(2)}, u32[]{:S(2)}) collective-permute-start(f32[2,16,4,128]{3,1,2,0:T(8,128)S(1)} %pad_maximum_fusion.4), channel_id=1, source_target_pairs={{0,12},{1,13},{2,14},{3,15},{4,16},{5,17},{6,18},{7,19},{8,20},{9,... | collective-permute-start | bytes 196616 | tf_op jit(solution)/shard_map/ppermute | solution.py:144
  14.3 11.8 %collective-permute-start.7 = (f32[2,16,4,128]{3,1,2,0:T(8,128)S(1)}, f32[2,16,4,128]{3,1,2,0:T(8,128)S(1)}, u32[]{:S(2)}, u32[]{:S(2)}) collective-permute-start(f32[2,16,4,128]{3,1,2,0:T(8,128)S(1)} %pad_maximum_fusion.4), channel_id=1, source_target_pairs={{0,8},{1,9},{2,10},{3,11},{4,12},{5,13},{6,14},{7,15},{8,16},{9,17... | collective-permute-start | bytes 196616 | tf_op jit(solution)/shard_map/ppermute | solution.py:144
  16.9 9.3 %collective-permute-start.8 = (f32[2,16,4,128]{3,1,2,0:T(8,128)S(1)}, f32[2,16,4,128]{3,1,2,0:T(8,128)S(1)}, u32[]{:S(2)}, u32[]{:S(2)}) collective-permute-start(f32[2,16,4,128]{3,1,2,0:T(8,128)S(1)} %pad_maximum_fusion.4), channel_id=1, source_target_pairs={{0,4},{1,5},{2,6},{3,7},{4,8},{5,9},{6,10},{7,11},{8,12},{9,13},{1... | collective-permute-start | bytes 196616 | tf_op jit(solution)/shard_map/ppermute | solution.py:144
  26.4 12.7 %collective-permute-start.9 = (f32[2,16,8,4,128]{4,1,3,2,0:T(8,128)S(1)}, f32[2,16,8,4,128]{4,1,3,2,0:T(8,128)S(1)}, u32[]{:S(2)}, u32[]{:S(2)}) collective-permute-start(f32[2,16,8,4,128]{4,1,3,2,0:T(8,128)S(1)} %constant_dynamic-slice_fusion.2), channel_id=1, source_target_pairs={{0,2},{1,3},{2,0},{3,1},{4,6},{5,7},{6,4},{7,5},{8,10},{9,11},{10,... | collective-permute-start | bytes 1572872 | tf_op jit(solution)/shard_map/ppermute | solution.py:149
  28.0 11.4 %copy-start.1 = (f32[1,16,128,128]{3,2,1,0:T(8,128)S(1)}, f32[1,16,128,128]{3,2,1,0:T(8,128)}, u32[]{:S(2)}) copy-start(f32[1,16,128,128]{3,2,1,0:T(8,128)} %param.9) | copy-start | bytes 3145732
  39.2 1.2 copy-start.2
  39.3 10.7 %collective-permute-start.10 = (f32[2,16,16,4,128]{4,1,3,2,0:T(8,128)S(1)}, f32[2,16,16,4,128]{4,1,3,2,0:T(8,128)}, u32[]{:S(2)}, u32[]{:S(2)}) collective-permute-start(f32[2,16,16,4,128]{4,1,3,2,0:T(8,128)S(1)} %bitcast.125), channel_id=1, source_target_pairs={{0,1},{1,0},{2,3},{3,2},{4,5},{5,4},{6,7},{7,6},{8,9},{9,8},{10,11... | collective-permute-start | bytes 3145736 | tf_op jit(solution)/shard_map/ppermute | solution.py:149
  40.5 8.7 %copy-start.5 = (f32[1,4,256]{2,1,0:T(4,128)S(1)}, f32[1,4,256]{2,1,0:T(4,128)}, u32[]{:S(2)}) copy-start(f32[1,4,256]{2,1,0:T(4,128)} %param.17) | copy-start | bytes 12292
  40.5 8.8 %copy-start.6 = (s32[1,256]{1,0:T(1,128)S(1)}, s32[1,256]{1,0:T(1,128)}, u32[]{:S(2)}) copy-start(s32[1,256]{1,0:T(1,128)} %param.16) | copy-start | bytes 3076
  40.5 8.8 %copy-start.7 = (s32[1,256]{1,0:T(1,128)S(1)}, s32[1,256]{1,0:T(1,128)}, u32[]{:S(2)}) copy-start(s32[1,256]{1,0:T(1,128)} %param.15) | copy-start | bytes 3076
  41.6 21.3 %collective-permute-start = (f32[2,4,128,128]{3,2,1,0:T(8,128)}, f32[2,4,128,128]{3,2,1,0:T(8,128)}, u32[]{:S(2)}, u32[]{:S(2)}) collective-permute-start(f32[2,4,128,128]{3,2,1,0:T(8,128)} %get-tuple-element.13), channel_id=1, source_target_pairs={{0,32},{32,64},{64,96},{96,128},{128,160},{160,192},{192,224},{1,3... | collective-permute-start | bytes 1572872 | tf_op jit(solution)/shard_map/ppermute | solution.py:128
  46.6 19.0 %collective-permute-start.1 = (f32[2,4,128,128]{3,2,1,0:T(8,128)}, f32[2,4,128,128]{3,2,1,0:T(8,128)}, u32[]{:S(2)}, u32[]{:S(2)}) collective-permute-start(f32[2,4,128,128]{3,2,1,0:T(8,128)} %get-tuple-element.14), channel_id=1, source_target_pairs={{32,0},{64,32},{96,64},{128,96},{160,128},{192,160},{224,192},{33,... | collective-permute-start | bytes 1572872 | tf_op jit(solution)/shard_map/ppermute | solution.py:129
  52.6 17.9 %collective-permute-start.11 = (f32[2,4,128,128]{3,2,1,0:T(8,128)S(1)}, f32[2,4,128,128]{3,2,1,0:T(8,128)S(1)}, u32[]{:S(2)}, u32[]{:S(2)}) collective-permute-start(f32[2,4,128,128]{3,2,1,0:T(8,128)S(1)} %get-tuple-element.9), channel_id=1, source_target_pairs={{0,32},{32,64},{64,96},{96,128},{128,160},{160,192},{192,224},{1,3... | collective-permute-start | bytes 1572872 | tf_op jit(solution)/shard_map/ppermute | solution.py:128
  60.1 18.1 %collective-permute-start.12 = (f32[2,4,128,128]{3,2,1,0:T(8,128)S(1)}, f32[2,4,128,128]{3,2,1,0:T(8,128)S(1)}, u32[]{:S(2)}, u32[]{:S(2)}) collective-permute-start(f32[2,4,128,128]{3,2,1,0:T(8,128)S(1)} %get-tuple-element.10), channel_id=1, source_target_pairs={{32,0},{64,32},{96,64},{128,96},{160,128},{192,160},{224,192},{33,... | collective-permute-start | bytes 1572872 | tf_op jit(solution)/shard_map/ppermute | solution.py:129
  68.6 11.6 %copy-start = (bf16[1,4,16,128,128]{4,3,2,1,0:T(8,128)(2,1)S(1)}, bf16[1,4,16,128,128]{4,3,2,1,0:T(8,128)(2,1)}, u32[]{:S(2)}) copy-start(bf16[1,4,16,128,128]{4,3,2,1,0:T(8,128)(2,1)} %param.11) | copy-start | bytes 6291460
  95.8 2.0 %collective-permute-start.13 = (f32[16,8,2,4,128]{4,3,2,1,0:T(4,128)S(1)}, f32[16,8,2,4,128]{4,3,2,1,0:T(4,128)S(1)}, u32[]{:S(2)}, u32[]{:S(2)}) collective-permute-start(f32[16,8,2,4,128]{4,3,2,1,0:T(4,128)S(1)} %dynamic-slice_bitcast_fusion), channel_id=1, source_target_pairs={{0,1},{1,0},{2,3},{3,2},{4,5},{5,4},{6,7},{7,6},{8,9},{9,8},{10,11... | collective-permute-start | bytes 1572872 | tf_op jit(solution)/shard_map/ppermute | solution.py:178
  95.9 28.1 %copy-start.3 = (f32[16,4,128]{2,1,0:T(4,128)S(1)}, f32[16,4,128]{2,1,0:T(4,128)}, u32[]{:S(2)}) copy-start(f32[16,4,128]{2,1,0:T(4,128)} %param.12) | copy-start | bytes 98308
  95.9 28.0 %copy-start.4 = (f32[16,4,128]{2,1,0:T(4,128)S(1)}, f32[16,4,128]{2,1,0:T(4,128)}, u32[]{:S(2)}) copy-start(f32[16,4,128]{2,1,0:T(4,128)} %param.13) | copy-start | bytes 98308
  98.1 8.6 %collective-permute-start.14 = (f32[16,8,4,128]{3,2,0,1:T(4,128)S(1)}, f32[16,8,4,128]{3,2,0,1:T(4,128)S(1)}, u32[]{:S(2)}, u32[]{:S(2)}) collective-permute-start(f32[16,8,4,128]{3,2,0,1:T(4,128)S(1)} %bitcast.127), channel_id=1, source_target_pairs={{0,2},{1,3},{2,0},{3,1},{4,6},{5,7},{6,4},{7,5},{8,10},{9,11},{10,... | collective-permute-start | bytes 786440 | tf_op jit(solution)/shard_map/ppermute | solution.py:178
  106.8 11.1 %collective-permute-start.15 = (f32[16,4,128]{2,1,0:T(4,128)S(1)}, f32[16,4,128]{2,1,0:T(4,128)S(1)}, u32[]{:S(2)}, u32[]{:S(2)}) collective-permute-start(f32[16,4,128]{2,1,0:T(4,128)S(1)} %get-tuple-element.19), channel_id=1, source_target_pairs={{0,4},{1,5},{2,6},{3,7},{4,8},{5,9},{6,10},{7,11},{8,12},{9,13},{1... | collective-permute-start | bytes 98312 | tf_op jit(solution)/shard_map/ppermute | solution.py:184
  108.2 11.8 %collective-permute-start.16 = (f32[16,4,128]{2,1,0:T(4,128)S(1)}, f32[16,4,128]{2,1,0:T(4,128)S(1)}, u32[]{:S(2)}, u32[]{:S(2)}) collective-permute-start(f32[16,4,128]{2,1,0:T(4,128)S(1)} %get-tuple-element.25), channel_id=1, source_target_pairs={{0,8},{1,9},{2,10},{3,11},{4,12},{5,13},{6,14},{7,15},{8,16},{9,17... | collective-permute-start | bytes 98312 | tf_op jit(solution)/shard_map/ppermute | solution.py:184
  110.0 12.0 %collective-permute-start.17 = (f32[16,4,128]{2,1,0:T(4,128)S(1)}, f32[16,4,128]{2,1,0:T(4,128)S(1)}, u32[]{:S(2)}, u32[]{:S(2)}) collective-permute-start(f32[16,4,128]{2,1,0:T(4,128)S(1)} %get-tuple-element.24), channel_id=1, source_target_pairs={{0,12},{1,13},{2,14},{3,15},{4,16},{5,17},{6,18},{7,19},{8,20},{9,... | collective-permute-start | bytes 98312 | tf_op jit(solution)/shard_map/ppermute | solution.py:184
  111.3 10.6 %collective-permute-start.18 = (f32[16,4,128]{2,1,0:T(4,128)S(1)}, f32[16,4,128]{2,1,0:T(4,128)S(1)}, u32[]{:S(2)}, u32[]{:S(2)}) collective-permute-start(f32[16,4,128]{2,1,0:T(4,128)S(1)} %get-tuple-element.23), channel_id=1, source_target_pairs={{0,16},{1,17},{2,18},{3,19},{4,20},{5,21},{6,22},{7,23},{8,24},{9,... | collective-permute-start | bytes 98312 | tf_op jit(solution)/shard_map/ppermute | solution.py:184
  116.4 6.0 %collective-permute-start.19 = (f32[16,4,128]{2,1,0:T(4,128)S(1)}, f32[16,4,128]{2,1,0:T(4,128)S(1)}, u32[]{:S(2)}, u32[]{:S(2)}) collective-permute-start(f32[16,4,128]{2,1,0:T(4,128)S(1)} %get-tuple-element.22), channel_id=1, source_target_pairs={{0,20},{1,21},{2,22},{3,23},{4,24},{5,25},{6,26},{7,27},{8,28},{9,... | collective-permute-start | bytes 98312 | tf_op jit(solution)/shard_map/ppermute | solution.py:184
  118.0 5.0 %collective-permute-start.20 = (f32[16,4,128]{2,1,0:T(4,128)S(1)}, f32[16,4,128]{2,1,0:T(4,128)S(1)}, u32[]{:S(2)}, u32[]{:S(2)}) collective-permute-start(f32[16,4,128]{2,1,0:T(4,128)S(1)} %get-tuple-element.21), channel_id=1, source_target_pairs={{0,24},{1,25},{2,26},{3,27},{4,28},{5,29},{6,30},{7,31},{8,0},{9,1... | collective-permute-start | bytes 98312 | tf_op jit(solution)/shard_map/ppermute | solution.py:184
  120.0 3.9 %collective-permute-start.21 = (f32[16,4,128]{2,1,0:T(4,128)S(1)}, f32[16,4,128]{2,1,0:T(4,128)S(1)}, u32[]{:S(2)}, u32[]{:S(2)}) collective-permute-start(f32[16,4,128]{2,1,0:T(4,128)S(1)} %get-tuple-element.20), channel_id=1, source_target_pairs={{0,28},{1,29},{2,30},{3,31},{4,0},{5,1},{6,2},{7,3},{8,4},{9,5},{1... | collective-permute-start | bytes 98312 | tf_op jit(solution)/shard_map/ppermute | solution.py:184

commit v2 on v0

--- a/solution.py
+++ b/solution.py
@@ -22,27 +22,51 @@
     return jnp.where(idx == 0, 0.0, r)
 
 
-def stencil_kernel(count_ref, adj_ref, mat_ref, snap_ref, src_ref, now_ref, prev_ref, img_ref,
-                   pbuf, qbuf, kz, kxf, kxb, kyf, kyb, kk):
-    ext = adj_ref.shape[1]
-    nx, ny = adj_ref.shape[2], adj_ref.shape[3]
-    steps = snap_ref.shape[0]
+def stencil_kernel(count_ref, now_hbm, prev_hbm, adj_lo, adj_hi, mat_hbm, mat_lo, mat_hi, snap_hbm,
+                   src_hbm, now_ref, prev_ref, img_ref, curb, oldb, matb, snapb, srcb, pbuf, qbuf,
+                   kz, kxf, kxb, kyf, kyb, kk, sems):
+    ext = curb.shape[0]
+    nx, ny = curb.shape[1], curb.shape[2]
+    planes = ext - 2 * HALO
+    steps = snapb.shape[0]
     count = count_ref[0]
+    copies = []
+
+    def fetch(src, dst):
+        c = pltpu.make_async_copy(src, dst, sems.at[len(copies)])
+        c.start()
+        copies.append(c)
+        return c
+
+    inner_at, lo_at, hi_at = pl.ds(HALO, planes), pl.ds(0, HALO), pl.ds(HALO + planes, HALO)
+    need_mat = [fetch(mat_hbm, matb.at[:, inner_at]), fetch(mat_lo, matb.at[:, lo_at]),
+                fetch(mat_hi, matb.at[:, hi_at])]
+    need_adj = [fetch(now_hbm, curb.at[inner_at]), fetch(adj_lo.at[0], curb.at[lo_at]),
+                fetch(adj_hi.at[0], curb.at[hi_at]), fetch(prev_hbm, oldb.at[inner_at]),
+                fetch(adj_lo.at[1], oldb.at[lo_at]), fetch(adj_hi.at[1], oldb.at[hi_at]),
+                fetch(src_hbm, srcb)]
+    need_snap = [fetch(snap_hbm.at[steps - 1 - step], snapb.at[steps - 1 - step])
+                 for step in range(steps)]
+    for c in need_mat:
+        c.wait()
 
     def weights(e, carry):
-        bc = mat_ref[1, e]
-        kz[e] = 0.5 * (bc + mat_ref[1, e + 1])
+        bc = matb[1, e]
+        kz[e] = 0.5 * (bc + matb[1, e + 1])
         kxf[e] = 0.5 * (bc + shift_fwd(bc, 0, nx))
         kxb[e] = 0.5 * (shift_bwd(bc, 0) + bc)
         kyf[e] = 0.5 * (bc + shift_fwd(bc, 1, ny))
         kyb[e] = 0.5 * (shift_bwd(bc, 1) + bc)
-        kk[e] = 0.08 * mat_ref[0, e]
+        kk[e] = 0.08 * matb[0, e]
         return carry
 
     lax.fori_loop(0, ext - 1, weights, 0)
+    for c in need_adj:
+        c.wait()
 
     def one_step(step, cur, old, dst, lo, hi):
         moment = steps - 1 - step
+        need_snap[step].wait()
 
         def plane(e, carry):
             pc = cur(e)
@@ -50,14 +74,14 @@
             total = total + (kxf[e] * (shift_fwd(pc, 0, nx) - pc) - kxb[e] * (pc - shift_bwd(pc, 0)))
             total = total + (kyf[e] * (shift_fwd(pc, 1, ny) - pc) - kyb[e] * (pc - shift_bwd(pc, 1)))
             weight = jnp.where(e == HALO + 2, 1.0, 0.0)
-            new = 2.0 * pc - old(e) + kk[e] * total + 0.08 * src_ref[moment] * weight
+            new = 2.0 * pc - old(e) + kk[e] * total + 0.08 * srcb[moment] * weight
             dst(e, new)
             inner = jnp.logical_and(e >= HALO, e < ext - HALO)
 
             @pl.when(inner)
             def _():
                 z = e - HALO
-                gained = snap_ref[moment, z].astype(jnp.float32) * new
+                gained = snapb[moment, z].astype(jnp.float32) * new
                 if step == 0:
                     img_ref[z] = gained
                 elif step == steps - 1:
@@ -69,10 +93,8 @@
 
         lax.fori_loop(lo, hi, plane, 0)
 
-    def rd(ref, k=None):
-        if k is None:
-            return lambda e: ref[e]
-        return lambda e: ref[k, e]
+    def rd(ref):
+        return lambda e: ref[e]
 
     def wr(ref):
         def f(e, v):
@@ -96,39 +118,39 @@
 
         return f
 
-    one_step(0, rd(adj_ref, 0), rd(adj_ref, 1), wr(pbuf), 1, ext - 1)
-    one_step(1, rd(pbuf), rd(adj_ref, 0), wr(qbuf), 2, ext - 2)
+    one_step(0, rd(curb), rd(oldb), wr(pbuf), 1, ext - 1)
+    one_step(1, rd(pbuf), rd(curb), wr(qbuf), 2, ext - 2)
     one_step(2, rd(qbuf), rd(pbuf), wr_inner(pbuf, prev_ref), 3, ext - 3)
     one_step(3, rd(pbuf), rd(qbuf), wr_out(now_ref), HALO, ext - HALO)
 
 
-def run_steps(count, adj_ext, mat_ext, snaps, src):
-    ext, nx, ny = adj_ext.shape[1:]
-    planes = ext - 2 * HALO
+def run_steps(count, adj_now, adj_prev, adj_lo, adj_hi, mat, mat_lo, mat_hi, snaps, src):
+    planes, nx, ny = adj_now.shape
+    ext = planes + 2 * HALO
+    steps = snaps.shape[0]
     vmem = pltpu.VMEM
     out_shape = [jax.ShapeDtypeStruct((planes, nx, ny), jnp.float32)] * 3
+    field = pltpu.VMEM((ext, nx, ny), jnp.float32)
     return pl.pallas_call(
         stencil_kernel,
         out_shape=out_shape,
-        in_specs=[pl.BlockSpec(memory_space=pltpu.SMEM)] + [pl.BlockSpec(memory_space=vmem)] * 4,
+        in_specs=[pl.BlockSpec(memory_space=pltpu.SMEM)] + [pl.BlockSpec(memory_space=pl.ANY)] * 9,
         out_specs=[pl.BlockSpec(memory_space=vmem)] * 3,
-        scratch_shapes=[pltpu.VMEM((ext, nx, ny), jnp.float32)] * 8,
-        compiler_params=pltpu.CompilerParams(vmem_limit_bytes=48 * 1024 * 1024),
+        scratch_shapes=[field, field, pltpu.VMEM((2, ext, nx, ny), jnp.float32),
+                        pltpu.VMEM(snaps.shape, snaps.dtype), pltpu.VMEM(src.shape, jnp.float32)]
+        + [field] * 8 + [pltpu.SemaphoreType.DMA((10 + steps,))],
+        compiler_params=pltpu.CompilerParams(vmem_limit_bytes=56 * 1024 * 1024),
         interpret=INTERPRET,
-    )(count, adj_ext, mat_ext, snaps, src)
-
-
-def with_halo(shard, sides, width):
-    for axis, dim in sides:
-        peers, length = (lax.axis_size(axis), shard.shape[dim])
-        up = [(i, (i + 1) % peers) for i in range(peers - 1)]
-        down = [(j, i) for i, j in up]
-        last = lax.slice_in_dim(shard, length - width, length, axis=dim)
-        first = lax.slice_in_dim(shard, 0, width, axis=dim)
-        before = lax.ppermute(last, axis, up)
-        after = lax.ppermute(first, axis, down)
-        shard = jnp.concatenate([before, shard, after], axis=dim)
-    return shard
+    )(count, adj_now, adj_prev, adj_lo, adj_hi, mat, mat_lo, mat_hi, snaps, src)
+
+
+def halo_of(shard, axis, dim, width):
+    peers, length = (lax.axis_size(axis), shard.shape[dim])
+    up = [(i, (i + 1) % peers) for i in range(peers - 1)]
+    down = [(j, i) for i, j in up]
+    last = lax.slice_in_dim(shard, length - width, length, axis=dim)
+    first = lax.slice_in_dim(shard, 0, width, axis=dim)
+    return lax.ppermute(last, axis, up), lax.ppermute(first, axis, down)
 
 
 def bit_order(peers):
@@ -187,16 +209,18 @@
     width_y = adj_now.shape[3]
     steps = fwd_snap.shape[1]
     groups = lax.axis_size("shots")
-    adj_ext = with_halo(jnp.stack([adj_now[0], adj_prev[0]]), (("depth", 1),), HALO)
+    adj_lo, adj_hi = halo_of(jnp.stack([adj_now[0], adj_prev[0]]), "depth", 1, HALO)
     local = jnp.stack([density * velocity * velocity, 1.0 / density])
-    local_ext = with_halo(local, (("depth", 1),), HALO)
-    mat_ext = gather_rows(local_ext, "shots", 2)
+    packed = gather_rows(local, "shots", 2)
+    mat_lo, mat_hi = halo_of(packed, "depth", 1, HALO)
     holds_source = (lax.axis_index("depth") == 0).astype(jnp.float32)
     src = jnp.stack(
         [source_plane(rec_x[0], rec_y[0], residual[0, t], width_x, width_y) for t in range(steps)]
     ) * holds_source
     count = shot_count.astype(jnp.float32)
-    current, older, weighted = run_steps(count, adj_ext, mat_ext, fwd_snap[0], src)
+    current, older, weighted = run_steps(
+        count, adj_now[0], adj_prev[0], adj_lo, adj_hi, packed, mat_lo, mat_hi, fwd_snap[0], src
+    )
     summed = scatter_rows(weighted, "shots", 1)
     grad_vel = 2.0 * density * velocity * summed / (4.0 * groups)
     return (current[None], older[None], grad_vel)

time: 144 us -> 125 us (0.87)
  waiting for transfers between devices: 82.9 us -> 63.3 us
  starting transfers between devices: 29.5 us -> 34 us
  other arithmetic: 5.87 us -> 2.55 us
    ppermute x5, waiting for transfers between devices: 38.6 us -> 26 us  [gather_rows(): got = lax.ppermute(pieces, axis, pairs)]
    ppermute x4, waiting for transfers between devices: 20.5 us -> 13.3 us  [halo_of(): return (lax.ppermute(last, axis, up), lax.ppermute(first, axis, down))]
    ppermute x4, starting transfers between devices: 12.8 us -> 16.4 us  [halo_of(): return (lax.ppermute(last, axis, up), lax.ppermute(first, axis, down))]
    another operation x3, local copies, waits for them, and re-layouts: 3.86 us -> 0.95 us  [gather_rows(): both = jnp.stack([lo, hi], axis=dim + 1)]
    another operation x9, other arithmetic: 2.8 us -> 0.62 us  [gather_rows(): both = jnp.stack([lo, hi], axis=dim + 1)]
    concatenate x1 -> x0, other arithmetic: 1.84 us -> none  [with_halo(): shard = jnp.concatenate([before, shard, after], axis=dim)]
  transfers between devices with their start and end apart: 14 -> 14, of which waited for: 12 -> 12; matrix products, arithmetic and copies ran while one was open for 3% -> 5% of each run, Pallas kernels for 0% -> 0%
where the time goes in v2:
time: 125 us
  waiting for transfers between devices  63.3 us (51%)
  starting transfers between devices  34 us (27%)
  Pallas kernels  14.9 us (12%)
  local copies, waits for them, and re-layouts  6.8 us (5%)
  other arithmetic  2.55 us (2%)
  between operations  1.69 us (1%)
  matrix products  1.61 us (1%)
    ppermute x5, waiting for transfers between devices, gather_rows(): got = lax.ppermute(pieces, axis, pairs)  26 us
    ppermute x5, waiting for transfers between devices, scatter_rows(): got = lax.ppermute(send, axis, pairs)  24.1 us
    ppermute x4, starting transfers between devices, halo_of(): return (lax.ppermute(last, axis, up), lax.ppermute(first, axis, down))  16.4 us
    pallas_call x1, Pallas kernels, run_steps(): pl.pallas_call(stencil_kernel, out_shape=out_shape, in_specs=[pl.BlockSpe...  14.9 us
    ppermute x4, waiting for transfers between devices, halo_of(): return (lax.ppermute(last, axis, up), lax.ppermute(first, axis, down))  13.3 us
    ppermute x5, starting transfers between devices, gather_rows(): got = lax.ppermute(pieces, axis, pairs)  12.1 us
    ppermute x5, starting transfers between devices, scatter_rows(): got = lax.ppermute(send, axis, pairs)  5.53 us
  transfers between devices with their start and end apart: 14, of which 12 were waited for; matrix products, arithmetic and copies ran while one was open for 5% of the time, Pallas kernels for 0%

profile of v2, /device:TPU:6, one launch (start us, length us, event | category | flops | bytes accessed | tf_op | source)
XLA Modules:
  0.0 124.8 jit_solution(6652747207094556961)
XLA Ops:
  0.6 0.8 fusion.20
  1.4 7.3 %collective-permute-start.2 = (f32[2,16,1,4,128]{4,1,3,0,2:T(8,128)S(1)}, f32[2,16,1,4,128]{4,1,3,0,2:T(8,128)S(1)}, u32[]{:S(2)}, u32[]{:S(2)}) collective-permute-start(f32[2,16,1,4,128]{4,1,3,0,2:T(8,128)S(1)} %maximum_bitcast_fusion.1), channel_id=1, source_target_pairs={{0,16},{1,17},{2,18},{3,19},{4,20},{5,21},{6,22},{7,23},{8,24},{9,... | collective-permute-start | bytes 196616 | tf_op jit(solution)/shard_map/ppermute | solution.py:166
  8.7 2.4 %collective-permute-done.2 = f32[2,16,1,4,128]{4,1,3,0,2:T(8,128)S(1)} collective-permute-done((f32[2,16,1,4,128]{4,1,3,0,2:T(8,128)S(1)}, f32[2,16,1,4,128]{4,1,3,0,2:T(8,128)S(1)}, u32[]{:S(2)}, u32[]{:S(2)}) %collective-permute-start.2) | collective-permute-done | bytes 65568 | tf_op jit(solution)/shard_map/ppermute | solution.py:166
  11.2 3.0 %collective-permute-start.3 = (f32[2,16,2,4,128]{4,1,3,2,0:T(8,128)S(1)}, f32[2,16,2,4,128]{4,1,3,2,0:T(8,128)S(1)}, u32[]{:S(2)}, u32[]{:S(2)}) collective-permute-start(f32[2,16,2,4,128]{4,1,3,2,0:T(8,128)S(1)} %maximum_bitcast_fusion), channel_id=1, source_target_pairs={{0,8},{1,9},{2,10},{3,11},{4,12},{5,13},{6,14},{7,15},{8,0},{9,1},... | collective-permute-start | bytes 393224 | tf_op jit(solution)/shard_map/ppermute | solution.py:166
  14.2 5.1 %collective-permute-done.3 = f32[2,16,2,4,128]{4,1,3,2,0:T(8,128)S(1)} collective-permute-done((f32[2,16,2,4,128]{4,1,3,2,0:T(8,128)S(1)}, f32[2,16,2,4,128]{4,1,3,2,0:T(8,128)S(1)}, u32[]{:S(2)}, u32[]{:S(2)}) %collective-permute-start.3) | collective-permute-done | bytes 131104 | tf_op jit(solution)/shard_map/ppermute | solution.py:166
  19.3 0.1 collective-permute-start.4
  19.4 7.6 %collective-permute-done.4 = f32[2,16,4,4,128]{4,1,3,2,0:T(8,128)S(1)} collective-permute-done((f32[2,16,4,4,128]{4,1,3,2,0:T(8,128)S(1)}, f32[2,16,4,4,128]{4,1,3,2,0:T(8,128)S(1)}, u32[]{:S(2)}, u32[]{:S(2)}) %collective-permute-start.4) | collective-permute-done | bytes 262176 | tf_op jit(solution)/shard_map/ppermute | solution.py:166
  27.2 1.7 %collective-permute-start.5 = (f32[2,16,8,4,128]{4,1,3,2,0:T(8,128)S(1)}, f32[2,16,8,4,128]{4,1,3,2,0:T(8,128)S(1)}, u32[]{:S(2)}, u32[]{:S(2)}) collective-permute-start(f32[2,16,8,4,128]{4,1,3,2,0:T(8,128)S(1)} %bitcast.96), channel_id=1, source_target_pairs={{0,2},{1,3},{2,0},{3,1},{4,6},{5,7},{6,4},{7,5},{8,10},{9,11},{10,... | collective-permute-start | bytes 1572872 | tf_op jit(solution)/shard_map/ppermute | solution.py:166
  28.8 10.8 %collective-permute-done.5 = f32[2,16,8,4,128]{4,1,3,2,0:T(8,128)S(1)} collective-permute-done((f32[2,16,8,4,128]{4,1,3,2,0:T(8,128)S(1)}, f32[2,16,8,4,128]{4,1,3,2,0:T(8,128)S(1)}, u32[]{:S(2)}, u32[]{:S(2)}) %collective-permute-start.5) | collective-permute-done | bytes 524320 | tf_op jit(solution)/shard_map/ppermute | solution.py:166
  39.6 0.1 select_bitcast_fusion.3
  39.8 0.0 copy-start.1
  39.8 0.1 pad_maximum_fusion.1
  39.9 0.0 copy-start.2
  39.9 0.1 copy.42
  40.0 0.1 collective-permute-start.6
  40.1 0.9 copy-done.1
  41.0 0.1 constant_dynamic-update-slice_fusion.1
  41.1 0.3 copy-done.2
  41.3 0.1 constant_dynamic-update-slice_fusion
  41.4 1.1 fusion.28
  42.5 5.0 %collective-permute-start = (f32[2,4,128,128]{3,2,1,0:T(8,128)}, f32[2,4,128,128]{3,2,1,0:T(8,128)S(1)}, u32[]{:S(2)}, u32[]{:S(2)}) collective-permute-start(f32[2,4,128,128]{3,2,1,0:T(8,128)} %get-tuple-element.17), channel_id=1, source_target_pairs={{0,32},{32,64},{64,96},{96,128},{128,160},{160,192},{192,224},{1,3... | collective-permute-start | bytes 1572872 | tf_op jit(solution)/shard_map/ppermute | solution.py:153
  47.5 1.9 %collective-permute-start.1 = (f32[2,4,128,128]{3,2,1,0:T(8,128)}, f32[2,4,128,128]{3,2,1,0:T(8,128)S(1)}, u32[]{:S(2)}, u32[]{:S(2)}) collective-permute-start(f32[2,4,128,128]{3,2,1,0:T(8,128)} %get-tuple-element.16), channel_id=1, source_target_pairs={{32,0},{64,32},{96,64},{128,96},{160,128},{192,160},{224,192},{33,... | collective-permute-start | bytes 1572872 | tf_op jit(solution)/shard_map/ppermute | solution.py:153
  49.4 0.0 copy-done.7
  49.5 0.0 collective-permute-done.6
  49.5 0.2 select_bitcast_fusion.1
  49.6 0.1 pad_maximum_fusion
  49.8 0.8 copy.43
  50.6 0.0 copy-start
  50.6 0.0 copy-start.8
  50.6 0.0 copy-start.9
  50.6 1.0 fusion.27
  51.7 7.5 %collective-permute-start.7 = (f32[2,4,128,128]{3,2,1,0:T(8,128)}, f32[2,4,128,128]{3,2,1,0:T(8,128)}, u32[]{:S(2)}, u32[]{:S(2)}) collective-permute-start(f32[2,4,128,128]{3,2,1,0:T(8,128)} %get-tuple-element.13), channel_id=1, source_target_pairs={{0,32},{32,64},{64,96},{96,128},{128,160},{160,192},{192,224},{1,3... | collective-permute-start | bytes 1572872 | tf_op jit(solution)/shard_map/ppermute | solution.py:153
  59.2 1.9 %collective-permute-start.8 = (f32[2,4,128,128]{3,2,1,0:T(8,128)}, f32[2,4,128,128]{3,2,1,0:T(8,128)}, u32[]{:S(2)}, u32[]{:S(2)}) collective-permute-start(f32[2,4,128,128]{3,2,1,0:T(8,128)} %get-tuple-element.12), channel_id=1, source_target_pairs={{32,0},{64,32},{96,64},{128,96},{160,128},{192,160},{224,192},{33,... | collective-permute-start | bytes 1572872 | tf_op jit(solution)/shard_map/ppermute | solution.py:153
  61.2 0.0 copy-done.8
  61.2 0.0 copy-done.9
  61.2 0.4 convolution_bitcast_fusion
  62.2 0.4 convolution_bitcast_fusion.1
  62.6 0.4 convolution_bitcast_fusion.2
  63.1 0.4 convolution_bitcast_fusion.3
  63.5 0.7 maximum_multiply_fusion.src_hbm
  64.2 0.0 collective-permute-done.adj_lo
  64.2 2.0 %collective-permute-done.1.adj_hi = f32[2,4,128,128]{3,2,1,0:T(8,128)S(1)} collective-permute-done((f32[2,4,128,128]{3,2,1,0:T(8,128)}, f32[2,4,128,128]{3,2,1,0:T(8,128)S(1)}, u32[]{:S(2)}, u32[]{:S(2)}) %collective-permute-start.1) | collective-permute-done | bytes 524320 | tf_op jit(solution)/shard_map/ppermute | solution.py:153
  66.2 3.5 %collective-permute-done.7.mat_lo = f32[2,4,128,128]{3,2,1,0:T(8,128)} collective-permute-done((f32[2,4,128,128]{3,2,1,0:T(8,128)}, f32[2,4,128,128]{3,2,1,0:T(8,128)}, u32[]{:S(2)}, u32[]{:S(2)}) %collective-permute-start.7) | collective-permute-done | bytes 524320 | tf_op jit(solution)/shard_map/ppermute | solution.py:153
  69.7 7.7 %collective-permute-done.8.mat_hi = f32[2,4,128,128]{3,2,1,0:T(8,128)} collective-permute-done((f32[2,4,128,128]{3,2,1,0:T(8,128)}, f32[2,4,128,128]{3,2,1,0:T(8,128)}, u32[]{:S(2)}, u32[]{:S(2)}) %collective-permute-start.8) | collective-permute-done | bytes 524320 | tf_op jit(solution)/shard_map/ppermute | solution.py:153
  77.5 0.0 copy-done
  77.5 0.0 copy-done.3
  77.5 14.9 %shard_map.112 = (f32[16,128,128]{2,1,0:T(8,128)}, f32[16,128,128]{2,1,0:T(8,128)}, f32[16,128,128]{2,1,0:T(8,128)}) custom-call(f32[1]{0:T(128)S(6)} %convert_element_type.4.count_ref, f32[16,128,128]{2,1,0:T(8,128)} %bitcast.91, f32[16,128,128]{2,1,0:T(8,128)} %bitcast.92, f32[2,4,128,128]{3,2,1,0:T(8,128)} %copy-done.3, f32[2,4,128,128]{3,2,1,0:T(8,128)} %copy-done.4, ...), custom_call_target="tpu_custom_call" | custom-call | tf_op jit(solution)/shard_map/pallas_call | solution.py:134
  92.3 1.4 %constant_dynamic-slice_fusion.1 = (f32[16,2,2,2,2,1,4,128]{7,6,5,4,3,2,1,0:T(4,128)S(1)}, f32[16,2,2,2,2,1,4,128]{7,6,5,4,3,2,1,0:T(4,128)S(1)}) fusion(f32[16,2,2,2,2,2,4,128]{7,6,5,4,3,2,1,0:T(4,128)} %bitcast.98, s32[]{:T(128)S(6)} %select_n.110, s32[]{:T(128)S(6)} %select_n.111), kind=kLoop, calls=%fused_computation.61 | loop fusion | bytes 2097160 | tf_op jit(solution)/shard_map/jit(dynamic_index_in_dim)/dynamic_slice | solution.py:189
  93.7 0.3 copy.56
  94.0 0.0 copy-start.5
  94.0 0.0 copy-start.6
  94.0 0.1 collective-permute-start.9
  94.2 1.9 %collective-permute-done.9 = f32[16,2,2,2,2,4,128]{6,0,5,4,3,2,1:T(8,128)S(1)} collective-permute-done((f32[16,2,2,2,2,4,128]{6,0,5,4,3,2,1:T(8,128)S(1)}, f32[16,2,2,2,2,4,128]{6,0,5,4,3,2,1:T(8,128)S(1)}, u32[]{:S(2)}, u32[]{:S(2)}) %collective-permute-start.9) | collective-permute-done | bytes 524320 | tf_op jit(solution)/shard_map/ppermute | solution.py:192
  96.0 0.3 bitcast_add_fusion
  96.4 0.8 collective-permute-start.10
  97.2 7.7 %collective-permute-done.10 = f32[16,2,2,2,4,128]{5,0,4,3,2,1:T(8,128)S(1)} collective-permute-done((f32[16,2,2,2,4,128]{5,0,4,3,2,1:T(8,128)S(1)}, f32[16,2,2,2,4,128]{5,0,4,3,2,1:T(8,128)S(1)}, u32[]{:S(2)}, u32[]{:S(2)}) %collective-permute-start.10) | collective-permute-done | bytes 262176 | tf_op jit(solution)/shard_map/ppermute | solution.py:192
  104.9 0.7 collective-permute-start.11
  105.6 4.4 %collective-permute-done.11 = f32[16,2,2,4,128]{4,0,3,2,1:T(8,128)S(1)} collective-permute-done((f32[16,2,2,4,128]{4,0,3,2,1:T(8,128)S(1)}, f32[16,2,2,4,128]{4,0,3,2,1:T(8,128)S(1)}, u32[]{:S(2)}, u32[]{:S(2)}) %collective-permute-start.11) | collective-permute-done | bytes 131104 | tf_op jit(solution)/shard_map/ppermute | solution.py:192
  110.0 0.1 collective-permute-start.12
  110.1 5.9 %collective-permute-done.12 = f32[16,2,4,128]{3,0,2,1:T(8,128)S(1)} collective-permute-done((f32[16,2,4,128]{3,0,2,1:T(8,128)S(1)}, f32[16,2,4,128]{3,0,2,1:T(8,128)S(1)}, u32[]{:S(2)}, u32[]{:S(2)}) %collective-permute-start.12) | collective-permute-done | bytes 65568 | tf_op jit(solution)/shard_map/ppermute | solution.py:192
  116.0 3.9 %collective-permute-start.13 = (f32[16,4,128]{2,0,1:T(8,128)S(1)}, f32[16,4,128]{2,0,1:T(8,128)S(1)}, u32[]{:S(2)}, u32[]{:S(2)}) collective-permute-start(f32[16,4,128]{2,0,1:T(8,128)S(1)} %dynamic-slice_bitcast_fusion.3), channel_id=1, source_target_pairs={{0,16},{1,17},{2,18},{3,19},{4,20},{5,21},{6,22},{7,23},{8,24},{9,... | collective-permute-start | bytes 98312 | tf_op jit(solution)/shard_map/ppermute | solution.py:192
  119.9 4.3 %collective-permute-done.13 = f32[16,4,128]{2,0,1:T(8,128)S(1)} collective-permute-done((f32[16,4,128]{2,0,1:T(8,128)S(1)}, f32[16,4,128]{2,0,1:T(8,128)S(1)}, u32[]{:S(2)}, u32[]{:S(2)}) %collective-permute-start.13) | collective-permute-done | bytes 32800 | tf_op jit(solution)/shard_map/ppermute | solution.py:192
  124.2 0.0 copy-done.6
  124.2 0.6 copy.48
  (22 shorter events, 0.3 us)
Async XLA Ops:
  1.4 9.7 %collective-permute-start.2 = (f32[2,16,1,4,128]{4,1,3,0,2:T(8,128)S(1)}, f32[2,16,1,4,128]{4,1,3,0,2:T(8,128)S(1)}, u32[]{:S(2)}, u32[]{:S(2)}) collective-permute-start(f32[2,16,1,4,128]{4,1,3,0,2:T(8,128)S(1)} %maximum_bitcast_fusion.1), channel_id=1, source_target_pairs={{0,16},{1,17},{2,18},{3,19},{4,20},{5,21},{6,22},{7,23},{8,24},{9,... | collective-permute-start | bytes 196616 | tf_op jit(solution)/shard_map/ppermute | solution.py:166
  11.2 8.1 %collective-permute-start.3 = (f32[2,16,2,4,128]{4,1,3,2,0:T(8,128)S(1)}, f32[2,16,2,4,128]{4,1,3,2,0:T(8,128)S(1)}, u32[]{:S(2)}, u32[]{:S(2)}) collective-permute-start(f32[2,16,2,4,128]{4,1,3,2,0:T(8,128)S(1)} %maximum_bitcast_fusion), channel_id=1, source_target_pairs={{0,8},{1,9},{2,10},{3,11},{4,12},{5,13},{6,14},{7,15},{8,0},{9,1},... | collective-permute-start | bytes 393224 | tf_op jit(solution)/shard_map/ppermute | solution.py:166
  19.3 7.7 %collective-permute-start.4 = (f32[2,16,4,4,128]{4,1,3,2,0:T(8,128)S(1)}, f32[2,16,4,4,128]{4,1,3,2,0:T(8,128)S(1)}, u32[]{:S(2)}, u32[]{:S(2)}) collective-permute-start(f32[2,16,4,4,128]{4,1,3,2,0:T(8,128)S(1)} %bitcast.99), channel_id=1, source_target_pairs={{0,4},{1,5},{2,6},{3,7},{4,0},{5,1},{6,2},{7,3},{8,12},{9,13},{10,... | collective-permute-start | bytes 786440 | tf_op jit(solution)/shard_map/ppermute | solution.py:166
  27.2 12.5 %collective-permute-start.5 = (f32[2,16,8,4,128]{4,1,3,2,0:T(8,128)S(1)}, f32[2,16,8,4,128]{4,1,3,2,0:T(8,128)S(1)}, u32[]{:S(2)}, u32[]{:S(2)}) collective-permute-start(f32[2,16,8,4,128]{4,1,3,2,0:T(8,128)S(1)} %bitcast.96), channel_id=1, source_target_pairs={{0,2},{1,3},{2,0},{3,1},{4,6},{5,7},{6,4},{7,5},{8,10},{9,11},{10,... | collective-permute-start | bytes 1572872 | tf_op jit(solution)/shard_map/ppermute | solution.py:166
  39.8 1.2 copy-start.1
  39.9 1.5 %copy-start.2 = (f32[1,16,128,128]{3,2,1,0:T(8,128)S(1)}, f32[1,16,128,128]{3,2,1,0:T(8,128)}, u32[]{:S(2)}) copy-start(f32[1,16,128,128]{3,2,1,0:T(8,128)} %param.10) | copy-start | bytes 3145732
  40.0 9.5 %collective-permute-start.6 = (f32[2,16,16,4,128]{4,1,3,2,0:T(8,128)S(1)}, f32[2,16,16,4,128]{4,1,3,2,0:T(8,128)S(1)}, u32[]{:S(2)}, u32[]{:S(2)}) collective-permute-start(f32[2,16,16,4,128]{4,1,3,2,0:T(8,128)S(1)} %bitcast.93), channel_id=1, source_target_pairs={{0,1},{1,0},{2,3},{3,2},{4,5},{5,4},{6,7},{7,6},{8,9},{9,8},{10,11... | collective-permute-start | bytes 3145736 | tf_op jit(solution)/shard_map/ppermute | solution.py:166
  41.3 8.1 %copy-start.7 = (f32[1,4,256]{2,1,0:T(4,128)S(1)}, f32[1,4,256]{2,1,0:T(4,128)}, u32[]{:S(2)}) copy-start(f32[1,4,256]{2,1,0:T(4,128)} %param.17) | copy-start | bytes 12292
  42.5 21.7 %collective-permute-start = (f32[2,4,128,128]{3,2,1,0:T(8,128)}, f32[2,4,128,128]{3,2,1,0:T(8,128)S(1)}, u32[]{:S(2)}, u32[]{:S(2)}) collective-permute-start(f32[2,4,128,128]{3,2,1,0:T(8,128)} %get-tuple-element.17), channel_id=1, source_target_pairs={{0,32},{32,64},{64,96},{96,128},{128,160},{160,192},{192,224},{1,3... | collective-permute-start | bytes 1572872 | tf_op jit(solution)/shard_map/ppermute | solution.py:153
  47.5 18.7 %collective-permute-start.1 = (f32[2,4,128,128]{3,2,1,0:T(8,128)}, f32[2,4,128,128]{3,2,1,0:T(8,128)S(1)}, u32[]{:S(2)}, u32[]{:S(2)}) collective-permute-start(f32[2,4,128,128]{3,2,1,0:T(8,128)} %get-tuple-element.16), channel_id=1, source_target_pairs={{32,0},{64,32},{96,64},{128,96},{160,128},{192,160},{224,192},{33,... | collective-permute-start | bytes 1572872 | tf_op jit(solution)/shard_map/ppermute | solution.py:153
  50.6 26.9 %copy-start = (f32[2,16,16,2,4,128]{5,4,3,2,1,0:T(4,128)}, f32[2,16,16,2,4,128]{5,4,3,2,1,0:T(4,128)S(1)}, u32[]{:S(2)}) copy-start(f32[2,16,16,2,4,128]{5,4,3,2,1,0:T(4,128)S(1)} %copy.43) | copy-start | bytes 6291460
  50.6 10.5 %copy-start.8 = (s32[1,256]{1,0:T(1,128)S(1)}, s32[1,256]{1,0:T(1,128)}, u32[]{:S(2)}) copy-start(s32[1,256]{1,0:T(1,128)} %param.16) | copy-start | bytes 3076
  50.6 10.5 %copy-start.9 = (s32[1,256]{1,0:T(1,128)S(1)}, s32[1,256]{1,0:T(1,128)}, u32[]{:S(2)}) copy-start(s32[1,256]{1,0:T(1,128)} %param.15) | copy-start | bytes 3076
  51.7 18.0 %collective-permute-start.7 = (f32[2,4,128,128]{3,2,1,0:T(8,128)}, f32[2,4,128,128]{3,2,1,0:T(8,128)}, u32[]{:S(2)}, u32[]{:S(2)}) collective-permute-start(f32[2,4,128,128]{3,2,1,0:T(8,128)} %get-tuple-element.13), channel_id=1, source_target_pairs={{0,32},{32,64},{64,96},{96,128},{128,160},{160,192},{192,224},{1,3... | collective-permute-start | bytes 1572872 | tf_op jit(solution)/shard_map/ppermute | solution.py:153
  59.2 18.2 %collective-permute-start.8 = (f32[2,4,128,128]{3,2,1,0:T(8,128)}, f32[2,4,128,128]{3,2,1,0:T(8,128)}, u32[]{:S(2)}, u32[]{:S(2)}) collective-permute-start(f32[2,4,128,128]{3,2,1,0:T(8,128)} %get-tuple-element.12), channel_id=1, source_target_pairs={{32,0},{64,32},{96,64},{128,96},{160,128},{192,160},{224,192},{33,... | collective-permute-start | bytes 1572872 | tf_op jit(solution)/shard_map/ppermute | solution.py:153
  64.2 13.3 %copy-start.3 = (f32[2,4,128,128]{3,2,1,0:T(8,128)}, f32[2,4,128,128]{3,2,1,0:T(8,128)S(1)}, u32[]{:S(2)}) copy-start(f32[2,4,128,128]{3,2,1,0:T(8,128)S(1)} %collective-permute-done.adj_lo) | copy-start | bytes 1572868
  66.2 11.3 %copy-start.4 = (f32[2,4,128,128]{3,2,1,0:T(8,128)}, f32[2,4,128,128]{3,2,1,0:T(8,128)S(1)}, u32[]{:S(2)}) copy-start(f32[2,4,128,128]{3,2,1,0:T(8,128)S(1)} %collective-permute-done.1.adj_hi) | copy-start | bytes 1572868
  94.0 30.2 %copy-start.5 = (f32[16,4,128]{2,1,0:T(4,128)S(1)}, f32[16,4,128]{2,1,0:T(4,128)}, u32[]{:S(2)}) copy-start(f32[16,4,128]{2,1,0:T(4,128)} %param.12) | copy-start | bytes 98308
  94.0 30.2 %copy-start.6 = (f32[16,4,128]{2,1,0:T(4,128)S(1)}, f32[16,4,128]{2,1,0:T(4,128)}, u32[]{:S(2)}) copy-start(f32[16,4,128]{2,1,0:T(4,128)} %param.13) | copy-start | bytes 98308
  94.0 2.0 %collective-permute-start.9 = (f32[16,2,2,2,2,4,128]{6,0,5,4,3,2,1:T(8,128)S(1)}, f32[16,2,2,2,2,4,128]{6,0,5,4,3,2,1:T(8,128)S(1)}, u32[]{:S(2)}, u32[]{:S(2)}) collective-permute-start(f32[16,2,2,2,2,4,128]{6,0,5,4,3,2,1:T(8,128)S(1)} %bitcast.101), channel_id=1, source_target_pairs={{0,1},{1,0},{2,3},{3,2},{4,5},{5,4},{6,7},{7,6},{8,9},{9,8},{10,11... | collective-permute-start | bytes 1572872 | tf_op jit(solution)/shard_map/ppermute | solution.py:192
  96.4 8.4 %collective-permute-start.10 = (f32[16,2,2,2,4,128]{5,0,4,3,2,1:T(8,128)S(1)}, f32[16,2,2,2,4,128]{5,0,4,3,2,1:T(8,128)S(1)}, u32[]{:S(2)}, u32[]{:S(2)}) collective-permute-start(f32[16,2,2,2,4,128]{5,0,4,3,2,1:T(8,128)S(1)} %dynamic-slice_bitcast_fusion), channel_id=1, source_target_pairs={{0,2},{1,3},{2,0},{3,1},{4,6},{5,7},{6,4},{7,5},{8,10},{9,11},{10,... | collective-permute-start | bytes 786440 | tf_op jit(solution)/shard_map/ppermute | solution.py:192
  104.9 5.1 %collective-permute-start.11 = (f32[16,2,2,4,128]{4,0,3,2,1:T(8,128)S(1)}, f32[16,2,2,4,128]{4,0,3,2,1:T(8,128)S(1)}, u32[]{:S(2)}, u32[]{:S(2)}) collective-permute-start(f32[16,2,2,4,128]{4,0,3,2,1:T(8,128)S(1)} %dynamic-slice_bitcast_fusion.1), channel_id=1, source_target_pairs={{0,4},{1,5},{2,6},{3,7},{4,0},{5,1},{6,2},{7,3},{8,12},{9,13},{10,... | collective-permute-start | bytes 393224 | tf_op jit(solution)/shard_map/ppermute | solution.py:192
  110.0 6.0 %collective-permute-start.12 = (f32[16,2,4,128]{3,0,2,1:T(8,128)S(1)}, f32[16,2,4,128]{3,0,2,1:T(8,128)S(1)}, u32[]{:S(2)}, u32[]{:S(2)}) collective-permute-start(f32[16,2,4,128]{3,0,2,1:T(8,128)S(1)} %dynamic-slice_bitcast_fusion.2), channel_id=1, source_target_pairs={{0,8},{1,9},{2,10},{3,11},{4,12},{5,13},{6,14},{7,15},{8,0},{9,1},... | collective-permute-start | bytes 196616 | tf_op jit(solution)/shard_map/ppermute | solution.py:192
  116.0 8.2 %collective-permute-start.13 = (f32[16,4,128]{2,0,1:T(8,128)S(1)}, f32[16,4,128]{2,0,1:T(8,128)S(1)}, u32[]{:S(2)}, u32[]{:S(2)}) collective-permute-start(f32[16,4,128]{2,0,1:T(8,128)S(1)} %dynamic-slice_bitcast_fusion.3), channel_id=1, source_target_pairs={{0,16},{1,17},{2,18},{3,19},{4,20},{5,21},{6,22},{7,23},{8,24},{9,... | collective-permute-start | bytes 98312 | tf_op jit(solution)/shard_map/ppermute | solution.py:192

commit v3 on v2

--- a/solution.py
+++ b/solution.py
@@ -24,7 +24,7 @@
 
 def stencil_kernel(count_ref, now_hbm, prev_hbm, adj_lo, adj_hi, mat_hbm, mat_lo, mat_hi, snap_hbm,
                    src_hbm, now_ref, prev_ref, img_ref, curb, oldb, matb, snapb, srcb, pbuf, qbuf,
-                   kz, kxf, kxb, kyf, kyb, kk, sems):
+                   wc, wzf, wzb, wxf, wxb, wyf, wyb, sems):
     ext = curb.shape[0]
     nx, ny = curb.shape[1], curb.shape[2]
     planes = ext - 2 * HALO
@@ -52,12 +52,22 @@
 
     def weights(e, carry):
         bc = matb[1, e]
-        kz[e] = 0.5 * (bc + matb[1, e + 1])
-        kxf[e] = 0.5 * (bc + shift_fwd(bc, 0, nx))
-        kxb[e] = 0.5 * (shift_bwd(bc, 0) + bc)
-        kyf[e] = 0.5 * (bc + shift_fwd(bc, 1, ny))
-        kyb[e] = 0.5 * (shift_bwd(bc, 1) + bc)
-        kk[e] = 0.08 * matb[0, e]
+        kap = 0.08 * matb[0, e]
+        zf = 0.5 * (bc + matb[1, e + 1])
+        zb = 0.5 * (matb[1, jnp.maximum(e - 1, 0)] + bc)
+        xf = 0.5 * (bc + shift_fwd(bc, 0, nx))
+        xb = 0.5 * (shift_bwd(bc, 0) + bc)
+        yf = 0.5 * (bc + shift_fwd(bc, 1, ny))
+        yb = 0.5 * (shift_bwd(bc, 1) + bc)
+        xi = lax.broadcasted_iota(jnp.int32, bc.shape, 0)
+        yi = lax.broadcasted_iota(jnp.int32, bc.shape, 1)
+        wc[e] = 2.0 - kap * (((zf + zb) + (xf + xb)) + (yf + yb))
+        wzf[e] = kap * zf
+        wzb[e] = kap * zb
+        wxf[e] = jnp.where(xi == nx - 1, 0.0, kap * xf)
+        wxb[e] = jnp.where(xi == 0, 0.0, kap * xb)
+        wyf[e] = jnp.where(yi == ny - 1, 0.0, kap * yf)
+        wyb[e] = jnp.where(yi == 0, 0.0, kap * yb)
         return carry
 
     lax.fori_loop(0, ext - 1, weights, 0)
@@ -68,13 +78,17 @@
         moment = steps - 1 - step
         need_snap[step].wait()
 
-        def plane(e, carry):
+        def plane(e, with_source):
             pc = cur(e)
-            total = kz[e] * (cur(e + 1) - pc) - kz[e - 1] * (pc - cur(e - 1))
-            total = total + (kxf[e] * (shift_fwd(pc, 0, nx) - pc) - kxb[e] * (pc - shift_bwd(pc, 0)))
-            total = total + (kyf[e] * (shift_fwd(pc, 1, ny) - pc) - kyb[e] * (pc - shift_bwd(pc, 1)))
-            weight = jnp.where(e == HALO + 2, 1.0, 0.0)
-            new = 2.0 * pc - old(e) + kk[e] * total + 0.08 * srcb[moment] * weight
+            new = wc[e] * pc + wzf[e] * cur(e + 1)
+            new = new + wzb[e] * cur(e - 1)
+            new = new + wxf[e] * pltpu.roll(pc, nx - 1, 0)
+            new = new + wxb[e] * pltpu.roll(pc, 1, 0)
+            new = new + wyf[e] * pltpu.roll(pc, ny - 1, 1)
+            new = new + wyb[e] * pltpu.roll(pc, 1, 1)
+            new = new - old(e)
+            if with_source:
+                new = new + 0.08 * srcb[moment]
             dst(e, new)
             inner = jnp.logical_and(e >= HALO, e < ext - HALO)
 
@@ -89,9 +103,14 @@
                 else:
                     img_ref[z] = img_ref[z] + gained
 
+        def plain(e, carry):
+            plane(e, False)
             return carry
 
-        lax.fori_loop(lo, hi, plane, 0)
+        at_source = HALO + 2
+        lax.fori_loop(lo, at_source, plain, 0)
+        plane(at_source, True)
+        lax.fori_loop(at_source + 1, hi, plain, 0)
 
     def rd(ref):
         return lambda e: ref[e]
@@ -138,7 +157,7 @@
         out_specs=[pl.BlockSpec(memory_space=vmem)] * 3,
         scratch_shapes=[field, field, pltpu.VMEM((2, ext, nx, ny), jnp.float32),
                         pltpu.VMEM(snaps.shape, snaps.dtype), pltpu.VMEM(src.shape, jnp.float32)]
-        + [field] * 8 + [pltpu.SemaphoreType.DMA((10 + steps,))],
+        + [field] * 9 + [pltpu.SemaphoreType.DMA((10 + steps,))],
         compiler_params=pltpu.CompilerParams(vmem_limit_bytes=56 * 1024 * 1024),
         interpret=INTERPRET,
     )(count, adj_now, adj_prev, adj_lo, adj_hi, mat, mat_lo, mat_hi, snaps, src)

time: 125 us -> 125 us (level)
  no operation moved by 1% of the time
where the time goes in v3:
time: 125 us
  waiting for transfers between devices  63.3 us (51%)
  starting transfers between devices  34 us (27%)
  Pallas kernels  14.6 us (12%)
  local copies, waits for them, and re-layouts  6.8 us (5%)
  other arithmetic  2.55 us (2%)
  between operations  1.69 us (1%)
  matrix products  1.61 us (1%)
    ppermute x5, waiting for transfers between devices, gather_rows(): got = lax.ppermute(pieces, axis, pairs)  26 us
    ppermute x5, waiting for transfers between devices, scatter_rows(): got = lax.ppermute(send, axis, pairs)  24.1 us
    ppermute x4, starting transfers between devices, halo_of(): return (lax.ppermute(last, axis, up), lax.ppermute(first, axis, down))  16.4 us
    pallas_call x1, Pallas kernels, run_steps(): pl.pallas_call(stencil_kernel, out_shape=out_shape, in_specs=[pl.BlockSpe...  14.6 us
    ppermute x4, waiting for transfers between devices, halo_of(): return (lax.ppermute(last, axis, up), lax.ppermute(first, axis, down))  13.3 us
    ppermute x5, starting transfers between devices, gather_rows(): got = lax.ppermute(pieces, axis, pairs)  12.1 us
    ppermute x5, starting transfers between devices, scatter_rows(): got = lax.ppermute(send, axis, pairs)  5.53 us
  transfers between devices with their start and end apart: 14, of which 12 were waited for; matrix products, arithmetic and copies ran while one was open for 5% of the time, Pallas kernels for 0%

profile of v3, /device:TPU:6, one launch (start us, length us, event | category | flops | bytes accessed | tf_op | source)
XLA Modules:
  0.0 124.6 jit_solution(16009906829306394098)
XLA Ops:
  0.6 0.8 fusion.20
  1.4 7.3 %collective-permute-start.2 = (f32[2,16,1,4,128]{4,1,3,0,2:T(8,128)S(1)}, f32[2,16,1,4,128]{4,1,3,0,2:T(8,128)S(1)}, u32[]{:S(2)}, u32[]{:S(2)}) collective-permute-start(f32[2,16,1,4,128]{4,1,3,0,2:T(8,128)S(1)} %maximum_bitcast_fusion.1), channel_id=1, source_target_pairs={{0,16},{1,17},{2,18},{3,19},{4,20},{5,21},{6,22},{7,23},{8,24},{9,... | collective-permute-start | bytes 196616 | tf_op jit(solution)/shard_map/ppermute | solution.py:185
  8.7 2.4 %collective-permute-done.2 = f32[2,16,1,4,128]{4,1,3,0,2:T(8,128)S(1)} collective-permute-done((f32[2,16,1,4,128]{4,1,3,0,2:T(8,128)S(1)}, f32[2,16,1,4,128]{4,1,3,0,2:T(8,128)S(1)}, u32[]{:S(2)}, u32[]{:S(2)}) %collective-permute-start.2) | collective-permute-done | bytes 65568 | tf_op jit(solution)/shard_map/ppermute | solution.py:185
  11.2 3.0 %collective-permute-start.3 = (f32[2,16,2,4,128]{4,1,3,2,0:T(8,128)S(1)}, f32[2,16,2,4,128]{4,1,3,2,0:T(8,128)S(1)}, u32[]{:S(2)}, u32[]{:S(2)}) collective-permute-start(f32[2,16,2,4,128]{4,1,3,2,0:T(8,128)S(1)} %maximum_bitcast_fusion), channel_id=1, source_target_pairs={{0,8},{1,9},{2,10},{3,11},{4,12},{5,13},{6,14},{7,15},{8,0},{9,1},... | collective-permute-start | bytes 393224 | tf_op jit(solution)/shard_map/ppermute | solution.py:185
  14.2 5.1 %collective-permute-done.3 = f32[2,16,2,4,128]{4,1,3,2,0:T(8,128)S(1)} collective-permute-done((f32[2,16,2,4,128]{4,1,3,2,0:T(8,128)S(1)}, f32[2,16,2,4,128]{4,1,3,2,0:T(8,128)S(1)}, u32[]{:S(2)}, u32[]{:S(2)}) %collective-permute-start.3) | collective-permute-done | bytes 131104 | tf_op jit(solution)/shard_map/ppermute | solution.py:185
  19.3 0.1 collective-permute-start.4
  19.4 7.6 %collective-permute-done.4 = f32[2,16,4,4,128]{4,1,3,2,0:T(8,128)S(1)} collective-permute-done((f32[2,16,4,4,128]{4,1,3,2,0:T(8,128)S(1)}, f32[2,16,4,4,128]{4,1,3,2,0:T(8,128)S(1)}, u32[]{:S(2)}, u32[]{:S(2)}) %collective-permute-start.4) | collective-permute-done | bytes 262176 | tf_op jit(solution)/shard_map/ppermute | solution.py:185
  27.2 1.7 %collective-permute-start.5 = (f32[2,16,8,4,128]{4,1,3,2,0:T(8,128)S(1)}, f32[2,16,8,4,128]{4,1,3,2,0:T(8,128)S(1)}, u32[]{:S(2)}, u32[]{:S(2)}) collective-permute-start(f32[2,16,8,4,128]{4,1,3,2,0:T(8,128)S(1)} %bitcast.96), channel_id=1, source_target_pairs={{0,2},{1,3},{2,0},{3,1},{4,6},{5,7},{6,4},{7,5},{8,10},{9,11},{10,... | collective-permute-start | bytes 1572872 | tf_op jit(solution)/shard_map/ppermute | solution.py:185
  28.8 10.8 %collective-permute-done.5 = f32[2,16,8,4,128]{4,1,3,2,0:T(8,128)S(1)} collective-permute-done((f32[2,16,8,4,128]{4,1,3,2,0:T(8,128)S(1)}, f32[2,16,8,4,128]{4,1,3,2,0:T(8,128)S(1)}, u32[]{:S(2)}, u32[]{:S(2)}) %collective-permute-start.5) | collective-permute-done | bytes 524320 | tf_op jit(solution)/shard_map/ppermute | solution.py:185
  39.6 0.1 select_bitcast_fusion.3
  39.8 0.0 copy-start.1
  39.8 0.1 pad_maximum_fusion.1
  39.9 0.0 copy-start.2
  39.9 0.1 copy.42
  40.0 0.1 collective-permute-start.6
  40.1 0.9 copy-done.1
  41.0 0.1 constant_dynamic-update-slice_fusion.1
  41.1 0.3 copy-done.2
  41.3 0.1 constant_dynamic-update-slice_fusion
  41.4 1.1 fusion.28
  42.5 5.0 %collective-permute-start = (f32[2,4,128,128]{3,2,1,0:T(8,128)}, f32[2,4,128,128]{3,2,1,0:T(8,128)S(1)}, u32[]{:S(2)}, u32[]{:S(2)}) collective-permute-start(f32[2,4,128,128]{3,2,1,0:T(8,128)} %get-tuple-element.17), channel_id=1, source_target_pairs={{0,32},{32,64},{64,96},{96,128},{128,160},{160,192},{192,224},{1,3... | collective-permute-start | bytes 1572872 | tf_op jit(solution)/shard_map/ppermute | solution.py:172
  47.5 1.9 %collective-permute-start.1 = (f32[2,4,128,128]{3,2,1,0:T(8,128)}, f32[2,4,128,128]{3,2,1,0:T(8,128)S(1)}, u32[]{:S(2)}, u32[]{:S(2)}) collective-permute-start(f32[2,4,128,128]{3,2,1,0:T(8,128)} %get-tuple-element.16), channel_id=1, source_target_pairs={{32,0},{64,32},{96,64},{128,96},{160,128},{192,160},{224,192},{33,... | collective-permute-start | bytes 1572872 | tf_op jit(solution)/shard_map/ppermute | solution.py:172
  49.4 0.0 copy-done.7
  49.5 0.0 collective-permute-done.6
  49.5 0.2 select_bitcast_fusion.1
  49.6 0.1 pad_maximum_fusion
  49.8 0.8 copy.43
  50.6 0.0 copy-start
  50.6 0.0 copy-start.8
  50.6 0.0 copy-start.9
  50.6 1.0 fusion.27
  51.7 7.5 %collective-permute-start.7 = (f32[2,4,128,128]{3,2,1,0:T(8,128)}, f32[2,4,128,128]{3,2,1,0:T(8,128)}, u32[]{:S(2)}, u32[]{:S(2)}) collective-permute-start(f32[2,4,128,128]{3,2,1,0:T(8,128)} %get-tuple-element.13), channel_id=1, source_target_pairs={{0,32},{32,64},{64,96},{96,128},{128,160},{160,192},{192,224},{1,3... | collective-permute-start | bytes 1572872 | tf_op jit(solution)/shard_map/ppermute | solution.py:172
  59.2 1.9 %collective-permute-start.8 = (f32[2,4,128,128]{3,2,1,0:T(8,128)}, f32[2,4,128,128]{3,2,1,0:T(8,128)}, u32[]{:S(2)}, u32[]{:S(2)}) collective-permute-start(f32[2,4,128,128]{3,2,1,0:T(8,128)} %get-tuple-element.12), channel_id=1, source_target_pairs={{32,0},{64,32},{96,64},{128,96},{160,128},{192,160},{224,192},{33,... | collective-permute-start | bytes 1572872 | tf_op jit(solution)/shard_map/ppermute | solution.py:172
  61.2 0.0 copy-done.8
  61.2 0.0 copy-done.9
  61.2 0.4 convolution_bitcast_fusion
  62.2 0.4 convolution_bitcast_fusion.1
  62.6 0.4 convolution_bitcast_fusion.2
  63.1 0.4 convolution_bitcast_fusion.3
  63.5 0.7 maximum_multiply_fusion.src_hbm
  64.2 0.0 collective-permute-done.adj_lo
  64.2 2.0 %collective-permute-done.1.adj_hi = f32[2,4,128,128]{3,2,1,0:T(8,128)S(1)} collective-permute-done((f32[2,4,128,128]{3,2,1,0:T(8,128)}, f32[2,4,128,128]{3,2,1,0:T(8,128)S(1)}, u32[]{:S(2)}, u32[]{:S(2)}) %collective-permute-start.1) | collective-permute-done | bytes 524320 | tf_op jit(solution)/shard_map/ppermute | solution.py:172
  66.2 3.5 %collective-permute-done.7.mat_lo = f32[2,4,128,128]{3,2,1,0:T(8,128)} collective-permute-done((f32[2,4,128,128]{3,2,1,0:T(8,128)}, f32[2,4,128,128]{3,2,1,0:T(8,128)}, u32[]{:S(2)}, u32[]{:S(2)}) %collective-permute-start.7) | collective-permute-done | bytes 524320 | tf_op jit(solution)/shard_map/ppermute | solution.py:172
  69.7 7.7 %collective-permute-done.8.mat_hi = f32[2,4,128,128]{3,2,1,0:T(8,128)} collective-permute-done((f32[2,4,128,128]{3,2,1,0:T(8,128)}, f32[2,4,128,128]{3,2,1,0:T(8,128)}, u32[]{:S(2)}, u32[]{:S(2)}) %collective-permute-start.8) | collective-permute-done | bytes 524320 | tf_op jit(solution)/shard_map/ppermute | solution.py:172
  77.5 0.0 copy-done
  77.5 0.0 copy-done.3
  77.5 14.6 %shard_map.112 = (f32[16,128,128]{2,1,0:T(8,128)}, f32[16,128,128]{2,1,0:T(8,128)}, f32[16,128,128]{2,1,0:T(8,128)}) custom-call(f32[1]{0:T(128)S(6)} %convert_element_type.4.count_ref, f32[16,128,128]{2,1,0:T(8,128)} %bitcast.91, f32[16,128,128]{2,1,0:T(8,128)} %bitcast.92, f32[2,4,128,128]{3,2,1,0:T(8,128)} %copy-done.3, f32[2,4,128,128]{3,2,1,0:T(8,128)} %copy-done.4, ...), custom_call_target="tpu_custom_call" | custom-call | tf_op jit(solution)/shard_map/pallas_call | solution.py:153
  92.1 1.4 %constant_dynamic-slice_fusion.1 = (f32[16,2,2,2,2,1,4,128]{7,6,5,4,3,2,1,0:T(4,128)S(1)}, f32[16,2,2,2,2,1,4,128]{7,6,5,4,3,2,1,0:T(4,128)S(1)}) fusion(f32[16,2,2,2,2,2,4,128]{7,6,5,4,3,2,1,0:T(4,128)} %bitcast.98, s32[]{:T(128)S(6)} %select_n.110, s32[]{:T(128)S(6)} %select_n.111), kind=kLoop, calls=%fused_computation.61 | loop fusion | bytes 2097160 | tf_op jit(solution)/shard_map/jit(dynamic_index_in_dim)/dynamic_slice | solution.py:208
  93.5 0.3 copy.56
  93.8 0.0 copy-start.5
  93.8 0.0 copy-start.6
  93.8 0.1 collective-permute-start.9
  93.9 1.9 %collective-permute-done.9 = f32[16,2,2,2,2,4,128]{6,0,5,4,3,2,1:T(8,128)S(1)} collective-permute-done((f32[16,2,2,2,2,4,128]{6,0,5,4,3,2,1:T(8,128)S(1)}, f32[16,2,2,2,2,4,128]{6,0,5,4,3,2,1:T(8,128)S(1)}, u32[]{:S(2)}, u32[]{:S(2)}) %collective-permute-start.9) | collective-permute-done | bytes 524320 | tf_op jit(solution)/shard_map/ppermute | solution.py:211
  95.8 0.3 bitcast_add_fusion
  96.1 0.8 collective-permute-start.10
  96.9 7.7 %collective-permute-done.10 = f32[16,2,2,2,4,128]{5,0,4,3,2,1:T(8,128)S(1)} collective-permute-done((f32[16,2,2,2,4,128]{5,0,4,3,2,1:T(8,128)S(1)}, f32[16,2,2,2,4,128]{5,0,4,3,2,1:T(8,128)S(1)}, u32[]{:S(2)}, u32[]{:S(2)}) %collective-permute-start.10) | collective-permute-done | bytes 262176 | tf_op jit(solution)/shard_map/ppermute | solution.py:211
  104.6 0.7 collective-permute-start.11
  105.3 4.4 %collective-permute-done.11 = f32[16,2,2,4,128]{4,0,3,2,1:T(8,128)S(1)} collective-permute-done((f32[16,2,2,4,128]{4,0,3,2,1:T(8,128)S(1)}, f32[16,2,2,4,128]{4,0,3,2,1:T(8,128)S(1)}, u32[]{:S(2)}, u32[]{:S(2)}) %collective-permute-start.11) | collective-permute-done | bytes 131104 | tf_op jit(solution)/shard_map/ppermute | solution.py:211
  109.7 0.1 collective-permute-start.12
  109.8 5.9 %collective-permute-done.12 = f32[16,2,4,128]{3,0,2,1:T(8,128)S(1)} collective-permute-done((f32[16,2,4,128]{3,0,2,1:T(8,128)S(1)}, f32[16,2,4,128]{3,0,2,1:T(8,128)S(1)}, u32[]{:S(2)}, u32[]{:S(2)}) %collective-permute-start.12) | collective-permute-done | bytes 65568 | tf_op jit(solution)/shard_map/ppermute | solution.py:211
  115.7 3.9 %collective-permute-start.13 = (f32[16,4,128]{2,0,1:T(8,128)S(1)}, f32[16,4,128]{2,0,1:T(8,128)S(1)}, u32[]{:S(2)}, u32[]{:S(2)}) collective-permute-start(f32[16,4,128]{2,0,1:T(8,128)S(1)} %dynamic-slice_bitcast_fusion.3), channel_id=1, source_target_pairs={{0,16},{1,17},{2,18},{3,19},{4,20},{5,21},{6,22},{7,23},{8,24},{9,... | collective-permute-start | bytes 98312 | tf_op jit(solution)/shard_map/ppermute | solution.py:211
  119.7 4.3 %collective-permute-done.13 = f32[16,4,128]{2,0,1:T(8,128)S(1)} collective-permute-done((f32[16,4,128]{2,0,1:T(8,128)S(1)}, f32[16,4,128]{2,0,1:T(8,128)S(1)}, u32[]{:S(2)}, u32[]{:S(2)}) %collective-permute-start.13) | collective-permute-done | bytes 32800 | tf_op jit(solution)/shard_map/ppermute | solution.py:211
  123.9 0.0 copy-done.6
  124.0 0.6 copy.48
  (22 shorter events, 0.3 us)
Async XLA Ops:
  1.4 9.7 %collective-permute-start.2 = (f32[2,16,1,4,128]{4,1,3,0,2:T(8,128)S(1)}, f32[2,16,1,4,128]{4,1,3,0,2:T(8,128)S(1)}, u32[]{:S(2)}, u32[]{:S(2)}) collective-permute-start(f32[2,16,1,4,128]{4,1,3,0,2:T(8,128)S(1)} %maximum_bitcast_fusion.1), channel_id=1, source_target_pairs={{0,16},{1,17},{2,18},{3,19},{4,20},{5,21},{6,22},{7,23},{8,24},{9,... | collective-permute-start | bytes 196616 | tf_op jit(solution)/shard_map/ppermute | solution.py:185
  11.2 8.1 %collective-permute-start.3 = (f32[2,16,2,4,128]{4,1,3,2,0:T(8,128)S(1)}, f32[2,16,2,4,128]{4,1,3,2,0:T(8,128)S(1)}, u32[]{:S(2)}, u32[]{:S(2)}) collective-permute-start(f32[2,16,2,4,128]{4,1,3,2,0:T(8,128)S(1)} %maximum_bitcast_fusion), channel_id=1, source_target_pairs={{0,8},{1,9},{2,10},{3,11},{4,12},{5,13},{6,14},{7,15},{8,0},{9,1},... | collective-permute-start | bytes 393224 | tf_op jit(solution)/shard_map/ppermute | solution.py:185
  19.3 7.7 %collective-permute-start.4 = (f32[2,16,4,4,128]{4,1,3,2,0:T(8,128)S(1)}, f32[2,16,4,4,128]{4,1,3,2,0:T(8,128)S(1)}, u32[]{:S(2)}, u32[]{:S(2)}) collective-permute-start(f32[2,16,4,4,128]{4,1,3,2,0:T(8,128)S(1)} %bitcast.99), channel_id=1, source_target_pairs={{0,4},{1,5},{2,6},{3,7},{4,0},{5,1},{6,2},{7,3},{8,12},{9,13},{10,... | collective-permute-start | bytes 786440 | tf_op jit(solution)/shard_map/ppermute | solution.py:185
  27.2 12.5 %collective-permute-start.5 = (f32[2,16,8,4,128]{4,1,3,2,0:T(8,128)S(1)}, f32[2,16,8,4,128]{4,1,3,2,0:T(8,128)S(1)}, u32[]{:S(2)}, u32[]{:S(2)}) collective-permute-start(f32[2,16,8,4,128]{4,1,3,2,0:T(8,128)S(1)} %bitcast.96), channel_id=1, source_target_pairs={{0,2},{1,3},{2,0},{3,1},{4,6},{5,7},{6,4},{7,5},{8,10},{9,11},{10,... | collective-permute-start | bytes 1572872 | tf_op jit(solution)/shard_map/ppermute | solution.py:185
  39.8 1.2 copy-start.1
  39.9 1.5 %copy-start.2 = (f32[1,16,128,128]{3,2,1,0:T(8,128)S(1)}, f32[1,16,128,128]{3,2,1,0:T(8,128)}, u32[]{:S(2)}) copy-start(f32[1,16,128,128]{3,2,1,0:T(8,128)} %param.10) | copy-start | bytes 3145732
  40.0 9.5 %collective-permute-start.6 = (f32[2,16,16,4,128]{4,1,3,2,0:T(8,128)S(1)}, f32[2,16,16,4,128]{4,1,3,2,0:T(8,128)S(1)}, u32[]{:S(2)}, u32[]{:S(2)}) collective-permute-start(f32[2,16,16,4,128]{4,1,3,2,0:T(8,128)S(1)} %bitcast.93), channel_id=1, source_target_pairs={{0,1},{1,0},{2,3},{3,2},{4,5},{5,4},{6,7},{7,6},{8,9},{9,8},{10,11... | collective-permute-start | bytes 3145736 | tf_op jit(solution)/shard_map/ppermute | solution.py:185
  41.3 8.1 %copy-start.7 = (f32[1,4,256]{2,1,0:T(4,128)S(1)}, f32[1,4,256]{2,1,0:T(4,128)}, u32[]{:S(2)}) copy-start(f32[1,4,256]{2,1,0:T(4,128)} %param.17) | copy-start | bytes 12292
  42.5 21.7 %collective-permute-start = (f32[2,4,128,128]{3,2,1,0:T(8,128)}, f32[2,4,128,128]{3,2,1,0:T(8,128)S(1)}, u32[]{:S(2)}, u32[]{:S(2)}) collective-permute-start(f32[2,4,128,128]{3,2,1,0:T(8,128)} %get-tuple-element.17), channel_id=1, source_target_pairs={{0,32},{32,64},{64,96},{96,128},{128,160},{160,192},{192,224},{1,3... | collective-permute-start | bytes 1572872 | tf_op jit(solution)/shard_map/ppermute | solution.py:172
  47.5 18.7 %collective-permute-start.1 = (f32[2,4,128,128]{3,2,1,0:T(8,128)}, f32[2,4,128,128]{3,2,1,0:T(8,128)S(1)}, u32[]{:S(2)}, u32[]{:S(2)}) collective-permute-start(f32[2,4,128,128]{3,2,1,0:T(8,128)} %get-tuple-element.16), channel_id=1, source_target_pairs={{32,0},{64,32},{96,64},{128,96},{160,128},{192,160},{224,192},{33,... | collective-permute-start | bytes 1572872 | tf_op jit(solution)/shard_map/ppermute | solution.py:172
  50.6 26.9 %copy-start = (f32[2,16,16,2,4,128]{5,4,3,2,1,0:T(4,128)}, f32[2,16,16,2,4,128]{5,4,3,2,1,0:T(4,128)S(1)}, u32[]{:S(2)}) copy-start(f32[2,16,16,2,4,128]{5,4,3,2,1,0:T(4,128)S(1)} %copy.43) | copy-start | bytes 6291460
  50.6 10.5 %copy-start.8 = (s32[1,256]{1,0:T(1,128)S(1)}, s32[1,256]{1,0:T(1,128)}, u32[]{:S(2)}) copy-start(s32[1,256]{1,0:T(1,128)} %param.16) | copy-start | bytes 3076
  50.6 10.5 %copy-start.9 = (s32[1,256]{1,0:T(1,128)S(1)}, s32[1,256]{1,0:T(1,128)}, u32[]{:S(2)}) copy-start(s32[1,256]{1,0:T(1,128)} %param.15) | copy-start | bytes 3076
  51.7 18.0 %collective-permute-start.7 = (f32[2,4,128,128]{3,2,1,0:T(8,128)}, f32[2,4,128,128]{3,2,1,0:T(8,128)}, u32[]{:S(2)}, u32[]{:S(2)}) collective-permute-start(f32[2,4,128,128]{3,2,1,0:T(8,128)} %get-tuple-element.13), channel_id=1, source_target_pairs={{0,32},{32,64},{64,96},{96,128},{128,160},{160,192},{192,224},{1,3... | collective-permute-start | bytes 1572872 | tf_op jit(solution)/shard_map/ppermute | solution.py:172
  59.2 18.2 %collective-permute-start.8 = (f32[2,4,128,128]{3,2,1,0:T(8,128)}, f32[2,4,128,128]{3,2,1,0:T(8,128)}, u32[]{:S(2)}, u32[]{:S(2)}) collective-permute-start(f32[2,4,128,128]{3,2,1,0:T(8,128)} %get-tuple-element.12), channel_id=1, source_target_pairs={{32,0},{64,32},{96,64},{128,96},{160,128},{192,160},{224,192},{33,... | collective-permute-start | bytes 1572872 | tf_op jit(solution)/shard_map/ppermute | solution.py:172
  64.2 13.3 %copy-start.3 = (f32[2,4,128,128]{3,2,1,0:T(8,128)}, f32[2,4,128,128]{3,2,1,0:T(8,128)S(1)}, u32[]{:S(2)}) copy-start(f32[2,4,128,128]{3,2,1,0:T(8,128)S(1)} %collective-permute-done.adj_lo) | copy-start | bytes 1572868
  66.2 11.3 %copy-start.4 = (f32[2,4,128,128]{3,2,1,0:T(8,128)}, f32[2,4,128,128]{3,2,1,0:T(8,128)S(1)}, u32[]{:S(2)}) copy-start(f32[2,4,128,128]{3,2,1,0:T(8,128)S(1)} %collective-permute-done.1.adj_hi) | copy-start | bytes 1572868
  93.8 30.2 %copy-start.5 = (f32[16,4,128]{2,1,0:T(4,128)S(1)}, f32[16,4,128]{2,1,0:T(4,128)}, u32[]{:S(2)}) copy-start(f32[16,4,128]{2,1,0:T(4,128)} %param.12) | copy-start | bytes 98308
  93.8 30.2 %copy-start.6 = (f32[16,4,128]{2,1,0:T(4,128)S(1)}, f32[16,4,128]{2,1,0:T(4,128)}, u32[]{:S(2)}) copy-start(f32[16,4,128]{2,1,0:T(4,128)} %param.13) | copy-start | bytes 98308
  93.8 2.0 %collective-permute-start.9 = (f32[16,2,2,2,2,4,128]{6,0,5,4,3,2,1:T(8,128)S(1)}, f32[16,2,2,2,2,4,128]{6,0,5,4,3,2,1:T(8,128)S(1)}, u32[]{:S(2)}, u32[]{:S(2)}) collective-permute-start(f32[16,2,2,2,2,4,128]{6,0,5,4,3,2,1:T(8,128)S(1)} %bitcast.101), channel_id=1, source_target_pairs={{0,1},{1,0},{2,3},{3,2},{4,5},{5,4},{6,7},{7,6},{8,9},{9,8},{10,11... | collective-permute-start | bytes 1572872 | tf_op jit(solution)/shard_map/ppermute | solution.py:211
  96.1 8.4 %collective-permute-start.10 = (f32[16,2,2,2,4,128]{5,0,4,3,2,1:T(8,128)S(1)}, f32[16,2,2,2,4,128]{5,0,4,3,2,1:T(8,128)S(1)}, u32[]{:S(2)}, u32[]{:S(2)}) collective-permute-start(f32[16,2,2,2,4,128]{5,0,4,3,2,1:T(8,128)S(1)} %dynamic-slice_bitcast_fusion), channel_id=1, source_target_pairs={{0,2},{1,3},{2,0},{3,1},{4,6},{5,7},{6,4},{7,5},{8,10},{9,11},{10,... | collective-permute-start | bytes 786440 | tf_op jit(solution)/shard_map/ppermute | solution.py:211
  104.6 5.1 %collective-permute-start.11 = (f32[16,2,2,4,128]{4,0,3,2,1:T(8,128)S(1)}, f32[16,2,2,4,128]{4,0,3,2,1:T(8,128)S(1)}, u32[]{:S(2)}, u32[]{:S(2)}) collective-permute-start(f32[16,2,2,4,128]{4,0,3,2,1:T(8,128)S(1)} %dynamic-slice_bitcast_fusion.1), channel_id=1, source_target_pairs={{0,4},{1,5},{2,6},{3,7},{4,0},{5,1},{6,2},{7,3},{8,12},{9,13},{10,... | collective-permute-start | bytes 393224 | tf_op jit(solution)/shard_map/ppermute | solution.py:211
  109.7 6.0 %collective-permute-start.12 = (f32[16,2,4,128]{3,0,2,1:T(8,128)S(1)}, f32[16,2,4,128]{3,0,2,1:T(8,128)S(1)}, u32[]{:S(2)}, u32[]{:S(2)}) collective-permute-start(f32[16,2,4,128]{3,0,2,1:T(8,128)S(1)} %dynamic-slice_bitcast_fusion.2), channel_id=1, source_target_pairs={{0,8},{1,9},{2,10},{3,11},{4,12},{5,13},{6,14},{7,15},{8,0},{9,1},... | collective-permute-start | bytes 196616 | tf_op jit(solution)/shard_map/ppermute | solution.py:211
  115.7 8.2 %collective-permute-start.13 = (f32[16,4,128]{2,0,1:T(8,128)S(1)}, f32[16,4,128]{2,0,1:T(8,128)S(1)}, u32[]{:S(2)}, u32[]{:S(2)}) collective-permute-start(f32[16,4,128]{2,0,1:T(8,128)S(1)} %dynamic-slice_bitcast_fusion.3), channel_id=1, source_target_pairs={{0,16},{1,17},{2,18},{3,19},{4,20},{5,21},{6,22},{7,23},{8,24},{9,... | collective-permute-start | bytes 98312 | tf_op jit(solution)/shard_map/ppermute | solution.py:211

commit v4 on v2

--- a/solution.py
+++ b/solution.py
@@ -10,21 +10,9 @@
 HALO = 4
 
 
-def shift_fwd(v, axis, n):
-    r = pltpu.roll(v, n - 1, axis)
-    idx = lax.broadcasted_iota(jnp.int32, v.shape, axis)
-    return jnp.where(idx == n - 1, 0.0, r)
-
-
-def shift_bwd(v, axis):
-    r = pltpu.roll(v, 1, axis)
-    idx = lax.broadcasted_iota(jnp.int32, v.shape, axis)
-    return jnp.where(idx == 0, 0.0, r)
-
-
 def stencil_kernel(count_ref, now_hbm, prev_hbm, adj_lo, adj_hi, mat_hbm, mat_lo, mat_hi, snap_hbm,
                    src_hbm, now_ref, prev_ref, img_ref, curb, oldb, matb, snapb, srcb, pbuf, qbuf,
-                   kz, kxf, kxb, kyf, kyb, kk, sems):
+                   wc, wzf, wzb, wxf, wxb, wyf, wyb, sems):
     ext = curb.shape[0]
     nx, ny = curb.shape[1], curb.shape[2]
     planes = ext - 2 * HALO
@@ -50,14 +38,38 @@
     for c in need_mat:
         c.wait()
 
+    rows = 8
+    chunks = nx // rows
+    sub = lax.broadcasted_iota(jnp.int32, (rows, ny), 0)
+    lane = lax.broadcasted_iota(jnp.int32, (rows, ny), 1)
+
+    def around(get, c):
+        mid = get(pl.ds(c * rows, rows))
+        up = get(pl.ds(max(c - 1, 0) * rows, rows))
+        down = get(pl.ds(min(c + 1, chunks - 1) * rows, rows))
+        ahead = jnp.where(sub == rows - 1, pltpu.roll(down, rows - 1, 0), pltpu.roll(mid, rows - 1, 0))
+        behind = jnp.where(sub == 0, pltpu.roll(up, 1, 0), pltpu.roll(mid, 1, 0))
+        return mid, ahead, behind
+
     def weights(e, carry):
-        bc = matb[1, e]
-        kz[e] = 0.5 * (bc + matb[1, e + 1])
-        kxf[e] = 0.5 * (bc + shift_fwd(bc, 0, nx))
-        kxb[e] = 0.5 * (shift_bwd(bc, 0) + bc)
-        kyf[e] = 0.5 * (bc + shift_fwd(bc, 1, ny))
-        kyb[e] = 0.5 * (shift_bwd(bc, 1) + bc)
-        kk[e] = 0.08 * matb[0, e]
+        for c in range(chunks):
+            r = pl.ds(c * rows, rows)
+            bc, bxa, bxb = around(lambda q: matb[1, e, q], c)
+            xi = sub + c * rows
+            kap = 0.08 * matb[0, e, r]
+            zf = 0.5 * (bc + matb[1, e + 1, r])
+            zb = 0.5 * (matb[1, jnp.maximum(e - 1, 0), r] + bc)
+            xf = 0.5 * (bc + jnp.where(xi == nx - 1, 0.0, bxa))
+            xb = 0.5 * (jnp.where(xi == 0, 0.0, bxb) + bc)
+            yf = 0.5 * (bc + jnp.where(lane == ny - 1, 0.0, pltpu.roll(bc, ny - 1, 1)))
+            yb = 0.5 * (jnp.where(lane == 0, 0.0, pltpu.roll(bc, 1, 1)) + bc)
+            wc[e, r] = 2.0 - kap * (((zf + zb) + (xf + xb)) + (yf + yb))
+            wzf[e, r] = kap * zf
+            wzb[e, r] = kap * zb
+            wxf[e, r] = jnp.where(xi == nx - 1, 0.0, kap * xf)
+            wxb[e, r] = jnp.where(xi == 0, 0.0, kap * xb)
+            wyf[e, r] = jnp.where(lane == ny - 1, 0.0, kap * yf)
+            wyb[e, r] = jnp.where(lane == 0, 0.0, kap * yb)
         return carry
 
     lax.fori_loop(0, ext - 1, weights, 0)
@@ -68,53 +80,64 @@
         moment = steps - 1 - step
         need_snap[step].wait()
 
-        def plane(e, carry):
-            pc = cur(e)
-            total = kz[e] * (cur(e + 1) - pc) - kz[e - 1] * (pc - cur(e - 1))
-            total = total + (kxf[e] * (shift_fwd(pc, 0, nx) - pc) - kxb[e] * (pc - shift_bwd(pc, 0)))
-            total = total + (kyf[e] * (shift_fwd(pc, 1, ny) - pc) - kyb[e] * (pc - shift_bwd(pc, 1)))
-            weight = jnp.where(e == HALO + 2, 1.0, 0.0)
-            new = 2.0 * pc - old(e) + kk[e] * total + 0.08 * srcb[moment] * weight
-            dst(e, new)
+        def plane(e, with_source):
             inner = jnp.logical_and(e >= HALO, e < ext - HALO)
-
-            @pl.when(inner)
-            def _():
-                z = e - HALO
-                gained = snapb[moment, z].astype(jnp.float32) * new
-                if step == 0:
-                    img_ref[z] = gained
-                elif step == steps - 1:
-                    img_ref[z] = count * (img_ref[z] + gained)
-                else:
-                    img_ref[z] = img_ref[z] + gained
-
+            for c in range(chunks):
+                r = pl.ds(c * rows, rows)
+                pc, pxa, pxb = around(lambda q: cur(e, q), c)
+                new = wc[e, r] * pc + wzf[e, r] * cur(e + 1, r)
+                new = new + wzb[e, r] * cur(e - 1, r)
+                new = new + wxf[e, r] * pxa
+                new = new + wxb[e, r] * pxb
+                new = new + wyf[e, r] * pltpu.roll(pc, ny - 1, 1)
+                new = new + wyb[e, r] * pltpu.roll(pc, 1, 1)
+                new = new - old(e, r)
+                if with_source:
+                    new = new + 0.08 * srcb[moment, r]
+                dst(e, r, new)
+
+                @pl.when(inner)
+                def _():
+                    z = e - HALO
+                    gained = snapb[moment, z, r].astype(jnp.float32) * new
+                    if step == 0:
+                        img_ref[z, r] = gained
+                    elif step == steps - 1:
+                        img_ref[z, r] = count * (img_ref[z, r] + gained)
+                    else:
+                        img_ref[z, r] = img_ref[z, r] + gained
+
+        def plain(e, carry):
+            plane(e, False)
             return carry
 
-        lax.fori_loop(lo, hi, plane, 0)
+        at_source = HALO + 2
+        lax.fori_loop(lo, at_source, plain, 0)
+        plane(at_source, True)
+        lax.fori_loop(at_source + 1, hi, plain, 0)
 
     def rd(ref):
-        return lambda e: ref[e]
+        return lambda e, r: ref[e, r]
 
     def wr(ref):
-        def f(e, v):
-            ref[e] = v
+        def f(e, r, v):
+            ref[e, r] = v
 
         return f
 
     def wr_inner(ref, out):
-        def f(e, v):
-            ref[e] = v
+        def f(e, r, v):
+            ref[e, r] = v
 
             @pl.when(jnp.logical_and(e >= HALO, e < ext - HALO))
             def _():
-                out[e - HALO] = v
+                out[e - HALO, r] = v
 
         return f
 
     def wr_out(out):
-        def f(e, v):
-            out[e - HALO] = v
+        def f(e, r, v):
+            out[e - HALO, r] = v
 
         return f
 
@@ -138,7 +161,7 @@
         out_specs=[pl.BlockSpec(memory_space=vmem)] * 3,
         scratch_shapes=[field, field, pltpu.VMEM((2, ext, nx, ny), jnp.float32),
                         pltpu.VMEM(snaps.shape, snaps.dtype), pltpu.VMEM(src.shape, jnp.float32)]
-        + [field] * 8 + [pltpu.SemaphoreType.DMA((10 + steps,))],
+        + [field] * 9 + [pltpu.SemaphoreType.DMA((10 + steps,))],
         compiler_params=pltpu.CompilerParams(vmem_limit_bytes=56 * 1024 * 1024),
         interpret=INTERPRET,
     )(count, adj_now, adj_prev, adj_lo, adj_hi, mat, mat_lo, mat_hi, snaps, src)

time: 125 us -> 204 us (1.63)
  the two profiles are of different devices: /device:TPU:6 before, /device:TPU:24 now
where the time goes in v4:
time: 204 us; the launch traced here: 200 us
  Pallas kernels  93.5 us (46%)
  waiting for transfers between devices  58 us (28%)
  starting transfers between devices  35.8 us (18%)
  local copies, waits for them, and re-layouts  6.8 us (3%)
  other arithmetic  2.55 us (1%)
    pallas_call x1, Pallas kernels, run_steps(): pl.pallas_call(stencil_kernel, out_shape=out_shape, in_specs=[pl.BlockSpe...  93.5 us
    ppermute x5, waiting for transfers between devices, gather_rows(): got = lax.ppermute(pieces, axis, pairs)  26.8 us
    ppermute x5, waiting for transfers between devices, scatter_rows(): got = lax.ppermute(send, axis, pairs)  24 us
    ppermute x4, starting transfers between devices, halo_of(): return (lax.ppermute(last, axis, up), lax.ppermute(first, axis, down))  18.9 us
    ppermute x5, starting transfers between devices, gather_rows(): got = lax.ppermute(pieces, axis, pairs)  11.3 us
    ppermute x4, waiting for transfers between devices, halo_of(): return (lax.ppermute(last, axis, up), lax.ppermute(first, axis, down))  7.17 us
    ppermute x5, starting transfers between devices, scatter_rows(): got = lax.ppermute(send, axis, pairs)  5.6 us
  transfers between devices with their start and end apart: 14, of which 11 were waited for; matrix products, arithmetic and copies ran while one was open for 3% of the time, Pallas kernels for 0%

profile of v4, /device:TPU:24, one launch (start us, length us, event | category | flops | bytes accessed | tf_op | source)
XLA Modules:
  0.0 199.9 jit_solution(10489806519861778651)
XLA Ops:
  0.6 0.8 fusion.20
  1.4 7.3 %collective-permute-start.2 = (f32[2,16,1,4,128]{4,1,3,0,2:T(8,128)S(1)}, f32[2,16,1,4,128]{4,1,3,0,2:T(8,128)S(1)}, u32[]{:S(2)}, u32[]{:S(2)}) collective-permute-start(f32[2,16,1,4,128]{4,1,3,0,2:T(8,128)S(1)} %maximum_bitcast_fusion.1), channel_id=1, source_target_pairs={{0,16},{1,17},{2,18},{3,19},{4,20},{5,21},{6,22},{7,23},{8,24},{9,... | collective-permute-start | bytes 196616 | tf_op jit(solution)/shard_map/ppermute | solution.py:189
  8.7 2.4 %collective-permute-done.2 = f32[2,16,1,4,128]{4,1,3,0,2:T(8,128)S(1)} collective-permute-done((f32[2,16,1,4,128]{4,1,3,0,2:T(8,128)S(1)}, f32[2,16,1,4,128]{4,1,3,0,2:T(8,128)S(1)}, u32[]{:S(2)}, u32[]{:S(2)}) %collective-permute-start.2) | collective-permute-done | bytes 65568 | tf_op jit(solution)/shard_map/ppermute | solution.py:189
  11.2 3.0 %collective-permute-start.3 = (f32[2,16,2,4,128]{4,1,3,2,0:T(8,128)S(1)}, f32[2,16,2,4,128]{4,1,3,2,0:T(8,128)S(1)}, u32[]{:S(2)}, u32[]{:S(2)}) collective-permute-start(f32[2,16,2,4,128]{4,1,3,2,0:T(8,128)S(1)} %maximum_bitcast_fusion), channel_id=1, source_target_pairs={{0,8},{1,9},{2,10},{3,11},{4,12},{5,13},{6,14},{7,15},{8,0},{9,1},... | collective-permute-start | bytes 393224 | tf_op jit(solution)/shard_map/ppermute | solution.py:189
  14.2 5.1 %collective-permute-done.3 = f32[2,16,2,4,128]{4,1,3,2,0:T(8,128)S(1)} collective-permute-done((f32[2,16,2,4,128]{4,1,3,2,0:T(8,128)S(1)}, f32[2,16,2,4,128]{4,1,3,2,0:T(8,128)S(1)}, u32[]{:S(2)}, u32[]{:S(2)}) %collective-permute-start.3) | collective-permute-done | bytes 131104 | tf_op jit(solution)/shard_map/ppermute | solution.py:189
  19.3 0.1 collective-permute-start.4
  19.4 7.6 %collective-permute-done.4 = f32[2,16,4,4,128]{4,1,3,2,0:T(8,128)S(1)} collective-permute-done((f32[2,16,4,4,128]{4,1,3,2,0:T(8,128)S(1)}, f32[2,16,4,4,128]{4,1,3,2,0:T(8,128)S(1)}, u32[]{:S(2)}, u32[]{:S(2)}) %collective-permute-start.4) | collective-permute-done | bytes 262176 | tf_op jit(solution)/shard_map/ppermute | solution.py:189
  27.2 0.8 collective-permute-start.5
  28.0 11.7 %collective-permute-done.5 = f32[2,16,8,4,128]{4,1,3,2,0:T(8,128)S(1)} collective-permute-done((f32[2,16,8,4,128]{4,1,3,2,0:T(8,128)S(1)}, f32[2,16,8,4,128]{4,1,3,2,0:T(8,128)S(1)}, u32[]{:S(2)}, u32[]{:S(2)}) %collective-permute-start.5) | collective-permute-done | bytes 524320 | tf_op jit(solution)/shard_map/ppermute | solution.py:189
  39.6 0.1 select_bitcast_fusion.3
  39.8 0.0 copy-start.1
  39.8 0.1 pad_maximum_fusion.1
  39.9 0.0 copy-start.2
  39.9 0.1 copy.42
  40.0 0.1 collective-permute-start.6
  40.1 0.9 copy-done.1
  41.0 0.1 constant_dynamic-update-slice_fusion.1
  41.1 0.3 copy-done.2
  41.3 0.1 constant_dynamic-update-slice_fusion
  41.4 1.1 fusion.28
  42.5 3.4 %collective-permute-start = (f32[2,4,128,128]{3,2,1,0:T(8,128)}, f32[2,4,128,128]{3,2,1,0:T(8,128)S(1)}, u32[]{:S(2)}, u32[]{:S(2)}) collective-permute-start(f32[2,4,128,128]{3,2,1,0:T(8,128)} %get-tuple-element.17), channel_id=1, source_target_pairs={{0,32},{32,64},{64,96},{96,128},{128,160},{160,192},{192,224},{1,3... | collective-permute-start | bytes 1572872 | tf_op jit(solution)/shard_map/ppermute | solution.py:176
  45.9 6.1 %collective-permute-start.1 = (f32[2,4,128,128]{3,2,1,0:T(8,128)}, f32[2,4,128,128]{3,2,1,0:T(8,128)S(1)}, u32[]{:S(2)}, u32[]{:S(2)}) collective-permute-start(f32[2,4,128,128]{3,2,1,0:T(8,128)} %get-tuple-element.16), channel_id=1, source_target_pairs={{32,0},{64,32},{96,64},{128,96},{160,128},{192,160},{224,192},{33,... | collective-permute-start | bytes 1572872 | tf_op jit(solution)/shard_map/ppermute | solution.py:176
  52.0 0.0 copy-done.7
  52.0 0.0 collective-permute-done.6
  52.0 0.2 select_bitcast_fusion.1
  52.2 0.1 pad_maximum_fusion
  52.3 0.8 copy.43
  53.1 0.0 copy-start
  53.1 0.0 copy-start.8
  53.2 0.0 copy-start.9
  53.2 1.0 fusion.27
  54.2 1.9 collective-permute-start.7
  56.1 7.5 %collective-permute-start.8 = (f32[2,4,128,128]{3,2,1,0:T(8,128)}, f32[2,4,128,128]{3,2,1,0:T(8,128)}, u32[]{:S(2)}, u32[]{:S(2)}) collective-permute-start(f32[2,4,128,128]{3,2,1,0:T(8,128)} %get-tuple-element.12), channel_id=1, source_target_pairs={{32,0},{64,32},{96,64},{128,96},{160,128},{192,160},{224,192},{33,... | collective-permute-start | bytes 1572872 | tf_op jit(solution)/shard_map/ppermute | solution.py:176
  63.7 0.0 copy-done.8
  63.7 0.0 copy-done.9
  63.7 0.4 convolution_bitcast_fusion
  64.8 0.4 convolution_bitcast_fusion.1
  65.2 0.4 convolution_bitcast_fusion.2
  65.6 0.4 convolution_bitcast_fusion.3
  66.0 0.7 maximum_multiply_fusion.src_hbm
  66.7 0.0 collective-permute-done.adj_lo
  66.7 0.0 collective-permute-done.1.adj_hi
  66.7 0.0 copy-start.4
  66.7 6.0 %collective-permute-done.7.mat_lo = f32[2,4,128,128]{3,2,1,0:T(8,128)} collective-permute-done((f32[2,4,128,128]{3,2,1,0:T(8,128)}, f32[2,4,128,128]{3,2,1,0:T(8,128)}, u32[]{:S(2)}, u32[]{:S(2)}) %collective-permute-start.7) | collective-permute-done | bytes 524320 | tf_op jit(solution)/shard_map/ppermute | solution.py:176
  72.7 1.2 collective-permute-done.8.mat_hi
  73.9 0.0 copy-done
  73.9 0.0 copy-done.3
  73.9 93.5 %shard_map.112 = (f32[16,128,128]{2,1,0:T(8,128)}, f32[16,128,128]{2,1,0:T(8,128)}, f32[16,128,128]{2,1,0:T(8,128)}) custom-call(f32[1]{0:T(128)S(6)} %convert_element_type.4.count_ref, f32[16,128,128]{2,1,0:T(8,128)} %bitcast.91, f32[16,128,128]{2,1,0:T(8,128)} %bitcast.92, f32[2,4,128,128]{3,2,1,0:T(8,128)} %copy-done.3, f32[2,4,128,128]{3,2,1,0:T(8,128)} %copy-done.4, ...), custom_call_target="tpu_custom_call" | custom-call | tf_op jit(solution)/shard_map/pallas_call | solution.py:157
  167.4 1.4 constant_dynamic-slice_fusion.1
  168.8 0.3 copy.56
  169.1 0.0 copy-start.5
  169.1 0.0 copy-start.6
  169.1 0.1 collective-permute-start.9
  169.2 1.9 collective-permute-done.9
  171.1 0.3 bitcast_add_fusion
  171.5 0.8 collective-permute-start.10
  172.3 7.6 %collective-permute-done.10 = f32[16,2,2,2,4,128]{5,0,4,3,2,1:T(8,128)S(1)} collective-permute-done((f32[16,2,2,2,4,128]{5,0,4,3,2,1:T(8,128)S(1)}, f32[16,2,2,2,4,128]{5,0,4,3,2,1:T(8,128)S(1)}, u32[]{:S(2)}, u32[]{:S(2)}) %collective-permute-start.10) | collective-permute-done | bytes 262176 | tf_op jit(solution)/shard_map/ppermute | solution.py:215
  180.0 0.7 collective-permute-start.11
  180.6 4.4 %collective-permute-done.11 = f32[16,2,2,4,128]{4,0,3,2,1:T(8,128)S(1)} collective-permute-done((f32[16,2,2,4,128]{4,0,3,2,1:T(8,128)S(1)}, f32[16,2,2,4,128]{4,0,3,2,1:T(8,128)S(1)}, u32[]{:S(2)}, u32[]{:S(2)}) %collective-permute-start.11) | collective-permute-done | bytes 131104 | tf_op jit(solution)/shard_map/ppermute | solution.py:215
  185.1 0.1 collective-permute-start.12
  185.2 5.9 %collective-permute-done.12 = f32[16,2,4,128]{3,0,2,1:T(8,128)S(1)} collective-permute-done((f32[16,2,4,128]{3,0,2,1:T(8,128)S(1)}, f32[16,2,4,128]{3,0,2,1:T(8,128)S(1)}, u32[]{:S(2)}, u32[]{:S(2)}) %collective-permute-start.12) | collective-permute-done | bytes 65568 | tf_op jit(solution)/shard_map/ppermute | solution.py:215
  191.1 3.9 %collective-permute-start.13 = (f32[16,4,128]{2,0,1:T(8,128)S(1)}, f32[16,4,128]{2,0,1:T(8,128)S(1)}, u32[]{:S(2)}, u32[]{:S(2)}) collective-permute-start(f32[16,4,128]{2,0,1:T(8,128)S(1)} %dynamic-slice_bitcast_fusion.3), channel_id=1, source_target_pairs={{0,16},{1,17},{2,18},{3,19},{4,20},{5,21},{6,22},{7,23},{8,24},{9,... | collective-permute-start | bytes 98312 | tf_op jit(solution)/shard_map/ppermute | solution.py:215
  195.0 4.3 %collective-permute-done.13 = f32[16,4,128]{2,0,1:T(8,128)S(1)} collective-permute-done((f32[16,4,128]{2,0,1:T(8,128)S(1)}, f32[16,4,128]{2,0,1:T(8,128)S(1)}, u32[]{:S(2)}, u32[]{:S(2)}) %collective-permute-start.13) | collective-permute-done | bytes 32800 | tf_op jit(solution)/shard_map/ppermute | solution.py:215
  199.3 0.6 copy.48
  (22 shorter events, 0.3 us)
Async XLA Ops:
  1.4 9.7 %collective-permute-start.2 = (f32[2,16,1,4,128]{4,1,3,0,2:T(8,128)S(1)}, f32[2,16,1,4,128]{4,1,3,0,2:T(8,128)S(1)}, u32[]{:S(2)}, u32[]{:S(2)}) collective-permute-start(f32[2,16,1,4,128]{4,1,3,0,2:T(8,128)S(1)} %maximum_bitcast_fusion.1), channel_id=1, source_target_pairs={{0,16},{1,17},{2,18},{3,19},{4,20},{5,21},{6,22},{7,23},{8,24},{9,... | collective-permute-start | bytes 196616 | tf_op jit(solution)/shard_map/ppermute | solution.py:189
  11.2 8.1 %collective-permute-start.3 = (f32[2,16,2,4,128]{4,1,3,2,0:T(8,128)S(1)}, f32[2,16,2,4,128]{4,1,3,2,0:T(8,128)S(1)}, u32[]{:S(2)}, u32[]{:S(2)}) collective-permute-start(f32[2,16,2,4,128]{4,1,3,2,0:T(8,128)S(1)} %maximum_bitcast_fusion), channel_id=1, source_target_pairs={{0,8},{1,9},{2,10},{3,11},{4,12},{5,13},{6,14},{7,15},{8,0},{9,1},... | collective-permute-start | bytes 393224 | tf_op jit(solution)/shard_map/ppermute | solution.py:189
  19.3 7.7 %collective-permute-start.4 = (f32[2,16,4,4,128]{4,1,3,2,0:T(8,128)S(1)}, f32[2,16,4,4,128]{4,1,3,2,0:T(8,128)S(1)}, u32[]{:S(2)}, u32[]{:S(2)}) collective-permute-start(f32[2,16,4,4,128]{4,1,3,2,0:T(8,128)S(1)} %bitcast.99), channel_id=1, source_target_pairs={{0,4},{1,5},{2,6},{3,7},{4,0},{5,1},{6,2},{7,3},{8,12},{9,13},{10,... | collective-permute-start | bytes 786440 | tf_op jit(solution)/shard_map/ppermute | solution.py:189
  27.2 12.5 %collective-permute-start.5 = (f32[2,16,8,4,128]{4,1,3,2,0:T(8,128)S(1)}, f32[2,16,8,4,128]{4,1,3,2,0:T(8,128)S(1)}, u32[]{:S(2)}, u32[]{:S(2)}) collective-permute-start(f32[2,16,8,4,128]{4,1,3,2,0:T(8,128)S(1)} %bitcast.96), channel_id=1, source_target_pairs={{0,2},{1,3},{2,0},{3,1},{4,6},{5,7},{6,4},{7,5},{8,10},{9,11},{10,... | collective-permute-start | bytes 1572872 | tf_op jit(solution)/shard_map/ppermute | solution.py:189
  39.8 1.2 copy-start.1
  39.9 1.5 copy-start.2
  40.0 12.0 %collective-permute-start.6 = (f32[2,16,16,4,128]{4,1,3,2,0:T(8,128)S(1)}, f32[2,16,16,4,128]{4,1,3,2,0:T(8,128)S(1)}, u32[]{:S(2)}, u32[]{:S(2)}) collective-permute-start(f32[2,16,16,4,128]{4,1,3,2,0:T(8,128)S(1)} %bitcast.93), channel_id=1, source_target_pairs={{0,1},{1,0},{2,3},{3,2},{4,5},{5,4},{6,7},{7,6},{8,9},{9,8},{10,11... | collective-permute-start | bytes 3145736 | tf_op jit(solution)/shard_map/ppermute | solution.py:189
  41.3 10.6 %copy-start.7 = (f32[1,4,256]{2,1,0:T(4,128)S(1)}, f32[1,4,256]{2,1,0:T(4,128)}, u32[]{:S(2)}) copy-start(f32[1,4,256]{2,1,0:T(4,128)} %param.17) | copy-start | bytes 12292
  42.5 24.2 %collective-permute-start = (f32[2,4,128,128]{3,2,1,0:T(8,128)}, f32[2,4,128,128]{3,2,1,0:T(8,128)S(1)}, u32[]{:S(2)}, u32[]{:S(2)}) collective-permute-start(f32[2,4,128,128]{3,2,1,0:T(8,128)} %get-tuple-element.17), channel_id=1, source_target_pairs={{0,32},{32,64},{64,96},{96,128},{128,160},{160,192},{192,224},{1,3... | collective-permute-start | bytes 1572872 | tf_op jit(solution)/shard_map/ppermute | solution.py:176
  45.9 20.8 %collective-permute-start.1 = (f32[2,4,128,128]{3,2,1,0:T(8,128)}, f32[2,4,128,128]{3,2,1,0:T(8,128)S(1)}, u32[]{:S(2)}, u32[]{:S(2)}) collective-permute-start(f32[2,4,128,128]{3,2,1,0:T(8,128)} %get-tuple-element.16), channel_id=1, source_target_pairs={{32,0},{64,32},{96,64},{128,96},{160,128},{192,160},{224,192},{33,... | collective-permute-start | bytes 1572872 | tf_op jit(solution)/shard_map/ppermute | solution.py:176
  53.1 20.8 %copy-start = (f32[2,16,16,2,4,128]{5,4,3,2,1,0:T(4,128)}, f32[2,16,16,2,4,128]{5,4,3,2,1,0:T(4,128)S(1)}, u32[]{:S(2)}) copy-start(f32[2,16,16,2,4,128]{5,4,3,2,1,0:T(4,128)S(1)} %copy.43) | copy-start | bytes 6291460
  53.1 10.5 %copy-start.8 = (s32[1,256]{1,0:T(1,128)S(1)}, s32[1,256]{1,0:T(1,128)}, u32[]{:S(2)}) copy-start(s32[1,256]{1,0:T(1,128)} %param.16) | copy-start | bytes 3076
  53.2 10.5 %copy-start.9 = (s32[1,256]{1,0:T(1,128)S(1)}, s32[1,256]{1,0:T(1,128)}, u32[]{:S(2)}) copy-start(s32[1,256]{1,0:T(1,128)} %param.15) | copy-start | bytes 3076
  54.2 18.5 %collective-permute-start.7 = (f32[2,4,128,128]{3,2,1,0:T(8,128)}, f32[2,4,128,128]{3,2,1,0:T(8,128)}, u32[]{:S(2)}, u32[]{:S(2)}) collective-permute-start(f32[2,4,128,128]{3,2,1,0:T(8,128)} %get-tuple-element.13), channel_id=1, source_target_pairs={{0,32},{32,64},{64,96},{96,128},{128,160},{160,192},{192,224},{1,3... | collective-permute-start | bytes 1572872 | tf_op jit(solution)/shard_map/ppermute | solution.py:176
  56.1 17.8 %collective-permute-start.8 = (f32[2,4,128,128]{3,2,1,0:T(8,128)}, f32[2,4,128,128]{3,2,1,0:T(8,128)}, u32[]{:S(2)}, u32[]{:S(2)}) collective-permute-start(f32[2,4,128,128]{3,2,1,0:T(8,128)} %get-tuple-element.12), channel_id=1, source_target_pairs={{32,0},{64,32},{96,64},{128,96},{160,128},{192,160},{224,192},{33,... | collective-permute-start | bytes 1572872 | tf_op jit(solution)/shard_map/ppermute | solution.py:176
  66.7 7.2 %copy-start.3 = (f32[2,4,128,128]{3,2,1,0:T(8,128)}, f32[2,4,128,128]{3,2,1,0:T(8,128)S(1)}, u32[]{:S(2)}) copy-start(f32[2,4,128,128]{3,2,1,0:T(8,128)S(1)} %collective-permute-done.adj_lo) | copy-start | bytes 1572868
  66.7 7.2 %copy-start.4 = (f32[2,4,128,128]{3,2,1,0:T(8,128)}, f32[2,4,128,128]{3,2,1,0:T(8,128)S(1)}, u32[]{:S(2)}) copy-start(f32[2,4,128,128]{3,2,1,0:T(8,128)S(1)} %collective-permute-done.1.adj_hi) | copy-start | bytes 1572868
  169.1 30.2 %copy-start.5 = (f32[16,4,128]{2,1,0:T(4,128)S(1)}, f32[16,4,128]{2,1,0:T(4,128)}, u32[]{:S(2)}) copy-start(f32[16,4,128]{2,1,0:T(4,128)} %param.12) | copy-start | bytes 98308
  169.1 30.2 %copy-start.6 = (f32[16,4,128]{2,1,0:T(4,128)S(1)}, f32[16,4,128]{2,1,0:T(4,128)}, u32[]{:S(2)}) copy-start(f32[16,4,128]{2,1,0:T(4,128)} %param.13) | copy-start | bytes 98308
  169.1 2.0 collective-permute-start.9
  171.5 8.4 %collective-permute-start.10 = (f32[16,2,2,2,4,128]{5,0,4,3,2,1:T(8,128)S(1)}, f32[16,2,2,2,4,128]{5,0,4,3,2,1:T(8,128)S(1)}, u32[]{:S(2)}, u32[]{:S(2)}) collective-permute-start(f32[16,2,2,2,4,128]{5,0,4,3,2,1:T(8,128)S(1)} %dynamic-slice_bitcast_fusion), channel_id=1, source_target_pairs={{0,2},{1,3},{2,0},{3,1},{4,6},{5,7},{6,4},{7,5},{8,10},{9,11},{10,... | collective-permute-start | bytes 786440 | tf_op jit(solution)/shard_map/ppermute | solution.py:215
  180.0 5.1 %collective-permute-start.11 = (f32[16,2,2,4,128]{4,0,3,2,1:T(8,128)S(1)}, f32[16,2,2,4,128]{4,0,3,2,1:T(8,128)S(1)}, u32[]{:S(2)}, u32[]{:S(2)}) collective-permute-start(f32[16,2,2,4,128]{4,0,3,2,1:T(8,128)S(1)} %dynamic-slice_bitcast_fusion.1), channel_id=1, source_target_pairs={{0,4},{1,5},{2,6},{3,7},{4,0},{5,1},{6,2},{7,3},{8,12},{9,13},{10,... | collective-permute-start | bytes 393224 | tf_op jit(solution)/shard_map/ppermute | solution.py:215
  185.1 6.0 %collective-permute-start.12 = (f32[16,2,4,128]{3,0,2,1:T(8,128)S(1)}, f32[16,2,4,128]{3,0,2,1:T(8,128)S(1)}, u32[]{:S(2)}, u32[]{:S(2)}) collective-permute-start(f32[16,2,4,128]{3,0,2,1:T(8,128)S(1)} %dynamic-slice_bitcast_fusion.2), channel_id=1, source_target_pairs={{0,8},{1,9},{2,10},{3,11},{4,12},{5,13},{6,14},{7,15},{8,0},{9,1},... | collective-permute-start | bytes 196616 | tf_op jit(solution)/shard_map/ppermute | solution.py:215
  191.1 8.2 %collective-permute-start.13 = (f32[16,4,128]{2,0,1:T(8,128)S(1)}, f32[16,4,128]{2,0,1:T(8,128)S(1)}, u32[]{:S(2)}, u32[]{:S(2)}) collective-permute-start(f32[16,4,128]{2,0,1:T(8,128)S(1)} %dynamic-slice_bitcast_fusion.3), channel_id=1, source_target_pairs={{0,16},{1,17},{2,18},{3,19},{4,20},{5,21},{6,22},{7,23},{8,24},{9,... | collective-permute-start | bytes 98312 | tf_op jit(solution)/shard_map/ppermute | solution.py:215

commit v5 on v2

--- a/solution.py
+++ b/solution.py
@@ -204,6 +204,25 @@
     return jnp.dot((onehot_x * amounts[:, None]).T, onehot_y, precision=lax.Precision.HIGHEST)
 
 
+def split_halo(shard, width):
+    depth, shots = lax.axis_size("depth"), lax.axis_size("shots")
+    core = lax.axis_index("shots") % 2
+    length = shard.shape[1]
+    start = jnp.where(core == 0, length - width, 0)
+    sent = lax.dynamic_slice_in_dim(shard, start, width, axis=1)
+    pairs = []
+    for d in range(depth):
+        for s in range(shots):
+            to = d + 1 if s % 2 == 0 else d - 1
+            if 0 <= to < depth:
+                pairs.append((d * shots + s, to * shots + s))
+    got = lax.ppermute(sent, ("depth", "shots"), pairs)
+    other = lax.ppermute(got, "shots", [(s, s ^ 1) for s in range(shots)])
+    lo = jnp.where(core == 0, got, other)
+    hi = jnp.where(core == 0, other, got)
+    return lo, hi
+
+
 def body(adj_now, adj_prev, fwd_snap, velocity, density, shot_count, rec_x, rec_y, residual):
     width_x = adj_now.shape[2]
     width_y = adj_now.shape[3]
@@ -212,7 +231,7 @@
     adj_lo, adj_hi = halo_of(jnp.stack([adj_now[0], adj_prev[0]]), "depth", 1, HALO)
     local = jnp.stack([density * velocity * velocity, 1.0 / density])
     packed = gather_rows(local, "shots", 2)
-    mat_lo, mat_hi = halo_of(packed, "depth", 1, HALO)
+    mat_lo, mat_hi = split_halo(packed, HALO)
     holds_source = (lax.axis_index("depth") == 0).astype(jnp.float32)
     src = jnp.stack(
         [source_plane(rec_x[0], rec_y[0], residual[0, t], width_x, width_y) for t in range(steps)]

time: 125 us -> 121 us (0.968)
  starting transfers between devices: 34 us -> 28.4 us
  other arithmetic: 2.55 us -> 4.66 us
  local copies, waits for them, and re-layouts: 6.8 us -> 5.34 us
    ppermute x4 -> x2, starting transfers between devices: 16.4 us -> 5.84 us  [halo_of(): return (lax.ppermute(last, axis, up), lax.ppermute(first, axis, down))]
    ppermute x0 -> x2, starting transfers between devices: none -> 5.15 us  [the longest x1 5.15 us: split_halo(): got = lax.ppermute(sent, ('depth', 'shots'), pairs)]
    ppermute x4 -> x2, waiting for transfers between devices: 13.3 us -> 8.42 us  [halo_of(): return (lax.ppermute(last, axis, up), lax.ppermute(first, axis, down))]
    ppermute x0 -> x2, waiting for transfers between devices: none -> 3.9 us  [the longest x1 3.89 us: split_halo(): got = lax.ppermute(sent, ('depth', 'shots'), pairs)]
    select_n x0 -> x1, other arithmetic: none -> 2.12 us  [split_halo(): hi = jnp.where(core == 0, other, got)]
    slice x2 -> x1, local copies, waits for them, and re-layouts: 2.11 us -> 0.07 us  [halo_of(): first = lax.slice_in_dim(shard, 0, width, axis=dim)]
    ppermute x5, waiting for transfers between devices: 26 us -> 27.6 us  [gather_rows(): got = lax.ppermute(pieces, axis, pairs)]
  transfers between devices with their start and end apart: 14 -> 14, of which waited for: 12 -> 13; matrix products, arithmetic and copies ran while one was open for 5% -> 4% of each run, Pallas kernels for 0% -> 0%
where the time goes in v5:
time: 121 us
  waiting for transfers between devices  64.2 us (53%)
  starting transfers between devices  28.4 us (23%)
  Pallas kernels  14.9 us (12%)
  local copies, waits for them, and re-layouts  5.34 us (4%)
  other arithmetic  4.66 us (4%)
  between operations  1.71 us (1%)
  matrix products  1.61 us (1%)
    ppermute x5, waiting for transfers between devices, gather_rows(): got = lax.ppermute(pieces, axis, pairs)  27.6 us
    ppermute x5, waiting for transfers between devices, scatter_rows(): got = lax.ppermute(send, axis, pairs)  24.3 us
    pallas_call x1, Pallas kernels, run_steps(): pl.pallas_call(stencil_kernel, out_shape=out_shape, in_specs=[pl.BlockSpe...  14.9 us
    ppermute x5, starting transfers between devices, gather_rows(): got = lax.ppermute(pieces, axis, pairs)  12.1 us
    ppermute x2, waiting for transfers between devices, halo_of(): return (lax.ppermute(last, axis, up), lax.ppermute(first, axis, down))  8.42 us
    ppermute x2, starting transfers between devices, halo_of(): return (lax.ppermute(last, axis, up), lax.ppermute(first, axis, down))  5.84 us
    ppermute x5, starting transfers between devices, scatter_rows(): got = lax.ppermute(send, axis, pairs)  5.33 us
    ppermute x1, starting transfers between devices, split_halo(): got = lax.ppermute(sent, ('depth', 'shots'), pairs)  5.15 us
  transfers between devices with their start and end apart: 14, of which 13 were waited for; matrix products, arithmetic and copies ran while one was open for 4% of the time, Pallas kernels for 0%

profile of v5, /device:TPU:6, one launch (start us, length us, event | category | flops | bytes accessed | tf_op | source)
XLA Modules:
  0.0 120.9 jit_solution(17386220086846751403)
XLA Ops:
  0.6 0.8 fusion.20
  1.4 7.3 %collective-permute-start.2 = (f32[2,16,1,4,128]{4,1,3,0,2:T(8,128)S(1)}, f32[2,16,1,4,128]{4,1,3,0,2:T(8,128)S(1)}, u32[]{:S(2)}, u32[]{:S(2)}) collective-permute-start(f32[2,16,1,4,128]{4,1,3,0,2:T(8,128)S(1)} %maximum_bitcast_fusion.1), channel_id=1, source_target_pairs={{0,16},{1,17},{2,18},{3,19},{4,20},{5,21},{6,22},{7,23},{8,24},{9,... | collective-permute-start | bytes 196616 | tf_op jit(solution)/shard_map/ppermute | solution.py:166
  8.7 2.4 %collective-permute-done.2 = f32[2,16,1,4,128]{4,1,3,0,2:T(8,128)S(1)} collective-permute-done((f32[2,16,1,4,128]{4,1,3,0,2:T(8,128)S(1)}, f32[2,16,1,4,128]{4,1,3,0,2:T(8,128)S(1)}, u32[]{:S(2)}, u32[]{:S(2)}) %collective-permute-start.2) | collective-permute-done | bytes 65568 | tf_op jit(solution)/shard_map/ppermute | solution.py:166
  11.2 3.0 %collective-permute-start.3 = (f32[2,16,2,4,128]{4,1,3,2,0:T(8,128)S(1)}, f32[2,16,2,4,128]{4,1,3,2,0:T(8,128)S(1)}, u32[]{:S(2)}, u32[]{:S(2)}) collective-permute-start(f32[2,16,2,4,128]{4,1,3,2,0:T(8,128)S(1)} %maximum_bitcast_fusion), channel_id=1, source_target_pairs={{0,8},{1,9},{2,10},{3,11},{4,12},{5,13},{6,14},{7,15},{8,0},{9,1},... | collective-permute-start | bytes 393224 | tf_op jit(solution)/shard_map/ppermute | solution.py:166
  14.2 5.1 %collective-permute-done.3 = f32[2,16,2,4,128]{4,1,3,2,0:T(8,128)S(1)} collective-permute-done((f32[2,16,2,4,128]{4,1,3,2,0:T(8,128)S(1)}, f32[2,16,2,4,128]{4,1,3,2,0:T(8,128)S(1)}, u32[]{:S(2)}, u32[]{:S(2)}) %collective-permute-start.3) | collective-permute-done | bytes 131104 | tf_op jit(solution)/shard_map/ppermute | solution.py:166
  19.3 0.1 collective-permute-start.4
  19.4 7.6 %collective-permute-done.4 = f32[2,16,4,4,128]{4,1,3,2,0:T(8,128)S(1)} collective-permute-done((f32[2,16,4,4,128]{4,1,3,2,0:T(8,128)S(1)}, f32[2,16,4,4,128]{4,1,3,2,0:T(8,128)S(1)}, u32[]{:S(2)}, u32[]{:S(2)}) %collective-permute-start.4) | collective-permute-done | bytes 262176 | tf_op jit(solution)/shard_map/ppermute | solution.py:166
  27.2 1.7 %collective-permute-start.5 = (f32[2,16,8,4,128]{4,1,3,2,0:T(8,128)S(1)}, f32[2,16,8,4,128]{4,1,3,2,0:T(8,128)S(1)}, u32[]{:S(2)}, u32[]{:S(2)}) collective-permute-start(f32[2,16,8,4,128]{4,1,3,2,0:T(8,128)S(1)} %bitcast.96), channel_id=1, source_target_pairs={{0,2},{1,3},{2,0},{3,1},{4,6},{5,7},{6,4},{7,5},{8,10},{9,11},{10,... | collective-permute-start | bytes 1572872 | tf_op jit(solution)/shard_map/ppermute | solution.py:166
  28.8 10.8 %collective-permute-done.5 = f32[2,16,8,4,128]{4,1,3,2,0:T(8,128)S(1)} collective-permute-done((f32[2,16,8,4,128]{4,1,3,2,0:T(8,128)S(1)}, f32[2,16,8,4,128]{4,1,3,2,0:T(8,128)S(1)}, u32[]{:S(2)}, u32[]{:S(2)}) %collective-permute-start.5) | collective-permute-done | bytes 524320 | tf_op jit(solution)/shard_map/ppermute | solution.py:166
  39.6 0.1 select_bitcast_fusion.3
  39.8 0.0 copy-start.1
  39.8 0.1 pad_maximum_fusion.1
  39.9 0.1 copy.42
  40.0 0.1 collective-permute-start.6
  40.1 0.9 copy-done.1
  41.0 0.1 constant_dynamic-update-slice_fusion.1
  41.1 1.7 %collective-permute-done.6 = f32[2,16,16,4,128]{4,1,3,2,0:T(8,128)S(1)} collective-permute-done((f32[2,16,16,4,128]{4,1,3,2,0:T(8,128)S(1)}, f32[2,16,16,4,128]{4,1,3,2,0:T(8,128)S(1)}, u32[]{:S(2)}, u32[]{:S(2)}) %collective-permute-start.6) | collective-permute-done | bytes 1048608 | tf_op jit(solution)/shard_map/ppermute | solution.py:166
  42.7 0.2 select_bitcast_fusion.1
  42.9 0.1 pad_maximum_fusion
  43.0 0.0 copy-start.2
  43.1 0.8 copy.43
  43.9 0.0 copy-start
  43.9 0.0 copy-start.7
  43.9 0.0 copy-start.8
  44.0 0.0 copy-start.9
  44.0 5.2 %collective-permute-start.7 = (f32[2,4,128,128]{3,2,1,0:T(8,128)S(1)}, f32[2,4,128,128]{3,2,1,0:T(8,128)}, u32[]{:S(2)}, u32[]{:S(2)}) collective-permute-start(f32[2,4,128,128]{3,2,1,0:T(8,128)S(1)} %constant_dynamic-slice_fusion.2), channel_id=1, source_target_pairs={{0,32},{2,34},{4,36},{6,38},{8,40},{10,42},{12,44},{14,46},{16,48}... | collective-permute-start | bytes 1572872 | tf_op jit(solution)/shard_map/ppermute | solution.py:219
  49.1 0.0 copy-done.2
  49.1 0.1 constant_dynamic-update-slice_fusion
  49.2 0.1 fusion.27
  49.3 0.0 copy-done
  49.3 3.4 %collective-permute-start = (f32[2,4,128,128]{3,2,1,0:T(8,128)S(1)}, f32[2,4,128,128]{3,2,1,0:T(8,128)S(1)}, u32[]{:S(2)}, u32[]{:S(2)}) collective-permute-start(f32[2,4,128,128]{3,2,1,0:T(8,128)S(1)} %get-tuple-element.15), channel_id=1, source_target_pairs={{0,32},{32,64},{64,96},{96,128},{128,160},{160,192},{192,224},{1,3... | collective-permute-start | bytes 1572872 | tf_op jit(solution)/shard_map/ppermute | solution.py:153
  52.7 2.4 %collective-permute-start.1 = (f32[2,4,128,128]{3,2,1,0:T(8,128)S(1)}, f32[2,4,128,128]{3,2,1,0:T(8,128)S(1)}, u32[]{:S(2)}, u32[]{:S(2)}) collective-permute-start(f32[2,4,128,128]{3,2,1,0:T(8,128)S(1)} %get-tuple-element.14), channel_id=1, source_target_pairs={{32,0},{64,32},{96,64},{128,96},{160,128},{192,160},{224,192},{33,... | collective-permute-start | bytes 1572872 | tf_op jit(solution)/shard_map/ppermute | solution.py:153
  55.2 0.0 copy-done.7
  55.2 3.9 %collective-permute-done.7 = f32[2,4,128,128]{3,2,1,0:T(8,128)} collective-permute-done((f32[2,4,128,128]{3,2,1,0:T(8,128)S(1)}, f32[2,4,128,128]{3,2,1,0:T(8,128)}, u32[]{:S(2)}, u32[]{:S(2)}) %collective-permute-start.7) | collective-permute-done | bytes 524320 | tf_op jit(solution)/shard_map/ppermute | solution.py:219
  59.1 0.0 collective-permute-start.8
  59.1 0.0 copy-done.9
  59.1 0.4 convolution_bitcast_fusion
  59.5 0.4 convolution_bitcast_fusion.1
  59.9 0.4 convolution_bitcast_fusion.2
  61.0 0.4 convolution_bitcast_fusion.3
  61.4 0.7 maximum_multiply_fusion.src_hbm
  62.1 0.0 collective-permute-done.8
  62.1 2.1 %broadcast_select_fusion = (f32[2,4,128,128]{3,2,1,0:T(8,128)}, f32[2,4,128,128]{3,2,1,0:T(8,128)}) fusion(f32[2,4,128,128]{3,2,1,0:T(8,128)S(1)} %collective-permute-done.8, f32[2,4,128,128]{3,2,1,0:T(8,128)} %collective-permute-done.7, pred[]{:T(512)S(6)} %eq.37), kind=kLoop, calls=%fused_computation.19 | loop fusion | flops 262144 | bytes 2097153 | tf_op jit(solution)/shard_map/jit(_where)/select_n | solution.py:222
  64.2 2.8 %collective-permute-done.adj_lo = f32[2,4,128,128]{3,2,1,0:T(8,128)S(1)} collective-permute-done((f32[2,4,128,128]{3,2,1,0:T(8,128)S(1)}, f32[2,4,128,128]{3,2,1,0:T(8,128)S(1)}, u32[]{:S(2)}, u32[]{:S(2)}) %collective-permute-start) | collective-permute-done | bytes 524320 | tf_op jit(solution)/shard_map/ppermute | solution.py:153
  67.0 5.6 %collective-permute-done.1.adj_hi = f32[2,4,128,128]{3,2,1,0:T(8,128)S(1)} collective-permute-done((f32[2,4,128,128]{3,2,1,0:T(8,128)S(1)}, f32[2,4,128,128]{3,2,1,0:T(8,128)S(1)}, u32[]{:S(2)}, u32[]{:S(2)}) %collective-permute-start.1) | collective-permute-done | bytes 524320 | tf_op jit(solution)/shard_map/ppermute | solution.py:153
  72.7 0.8 copy-done.4
  73.5 14.9 %shard_map.112 = (f32[16,128,128]{2,1,0:T(8,128)}, f32[16,128,128]{2,1,0:T(8,128)}, f32[16,128,128]{2,1,0:T(8,128)}) custom-call(f32[1]{0:T(128)S(6)} %convert_element_type.4.count_ref, f32[16,128,128]{2,1,0:T(8,128)} %bitcast.91, f32[16,128,128]{2,1,0:T(8,128)} %bitcast.92, f32[2,4,128,128]{3,2,1,0:T(8,128)} %copy-done.3, f32[2,4,128,128]{3,2,1,0:T(8,128)} %copy-done.4, ...), custom_call_target="tpu_custom_call" | custom-call | tf_op jit(solution)/shard_map/pallas_call | solution.py:134
  88.4 1.4 %constant_dynamic-slice_fusion.1 = (f32[16,2,2,2,2,1,4,128]{7,6,5,4,3,2,1,0:T(4,128)S(1)}, f32[16,2,2,2,2,1,4,128]{7,6,5,4,3,2,1,0:T(4,128)S(1)}) fusion(f32[16,2,2,2,2,2,4,128]{7,6,5,4,3,2,1,0:T(4,128)} %bitcast.98, s32[]{:T(128)S(6)} %select_n.139, s32[]{:T(128)S(6)} %select_n.140), kind=kLoop, calls=%fused_computation.63 | loop fusion | bytes 2097160 | tf_op jit(solution)/shard_map/jit(dynamic_index_in_dim)/dynamic_slice | solution.py:189
  89.7 0.3 copy.56
  90.0 0.0 copy-start.5
  90.0 0.0 copy-start.6
  90.1 0.1 collective-permute-start.9
  90.2 1.9 %collective-permute-done.9 = f32[16,2,2,2,2,4,128]{6,0,5,4,3,2,1:T(8,128)S(1)} collective-permute-done((f32[16,2,2,2,2,4,128]{6,0,5,4,3,2,1:T(8,128)S(1)}, f32[16,2,2,2,2,4,128]{6,0,5,4,3,2,1:T(8,128)S(1)}, u32[]{:S(2)}, u32[]{:S(2)}) %collective-permute-start.9) | collective-permute-done | bytes 524320 | tf_op jit(solution)/shard_map/ppermute | solution.py:192
  92.1 0.3 bitcast_add_fusion
  92.4 0.6 collective-permute-start.10
  93.0 7.9 %collective-permute-done.10 = f32[16,2,2,2,4,128]{5,0,4,3,2,1:T(8,128)S(1)} collective-permute-done((f32[16,2,2,2,4,128]{5,0,4,3,2,1:T(8,128)S(1)}, f32[16,2,2,2,4,128]{5,0,4,3,2,1:T(8,128)S(1)}, u32[]{:S(2)}, u32[]{:S(2)}) %collective-permute-start.10) | collective-permute-done | bytes 262176 | tf_op jit(solution)/shard_map/ppermute | solution.py:192
  100.9 0.7 collective-permute-start.11
  101.6 4.4 %collective-permute-done.11 = f32[16,2,2,4,128]{4,0,3,2,1:T(8,128)S(1)} collective-permute-done((f32[16,2,2,4,128]{4,0,3,2,1:T(8,128)S(1)}, f32[16,2,2,4,128]{4,0,3,2,1:T(8,128)S(1)}, u32[]{:S(2)}, u32[]{:S(2)}) %collective-permute-start.11) | collective-permute-done | bytes 131104 | tf_op jit(solution)/shard_map/ppermute | solution.py:192
  106.0 0.1 collective-permute-start.12
  106.1 5.9 %collective-permute-done.12 = f32[16,2,4,128]{3,0,2,1:T(8,128)S(1)} collective-permute-done((f32[16,2,4,128]{3,0,2,1:T(8,128)S(1)}, f32[16,2,4,128]{3,0,2,1:T(8,128)S(1)}, u32[]{:S(2)}, u32[]{:S(2)}) %collective-permute-start.12) | collective-permute-done | bytes 65568 | tf_op jit(solution)/shard_map/ppermute | solution.py:192
  112.0 3.9 %collective-permute-start.13 = (f32[16,4,128]{2,0,1:T(8,128)S(1)}, f32[16,4,128]{2,0,1:T(8,128)S(1)}, u32[]{:S(2)}, u32[]{:S(2)}) collective-permute-start(f32[16,4,128]{2,0,1:T(8,128)S(1)} %dynamic-slice_bitcast_fusion.3), channel_id=1, source_target_pairs={{0,16},{1,17},{2,18},{3,19},{4,20},{5,21},{6,22},{7,23},{8,24},{9,... | collective-permute-start | bytes 98312 | tf_op jit(solution)/shard_map/ppermute | solution.py:192
  115.9 4.3 %collective-permute-done.13 = f32[16,4,128]{2,0,1:T(8,128)S(1)} collective-permute-done((f32[16,4,128]{2,0,1:T(8,128)S(1)}, f32[16,4,128]{2,0,1:T(8,128)S(1)}, u32[]{:S(2)}, u32[]{:S(2)}) %collective-permute-start.13) | collective-permute-done | bytes 32800 | tf_op jit(solution)/shard_map/ppermute | solution.py:192
  120.2 0.0 copy-done.5
  120.2 0.6 copy.48
  (23 shorter events, 0.4 us)
Async XLA Ops:
  1.4 9.7 %collective-permute-start.2 = (f32[2,16,1,4,128]{4,1,3,0,2:T(8,128)S(1)}, f32[2,16,1,4,128]{4,1,3,0,2:T(8,128)S(1)}, u32[]{:S(2)}, u32[]{:S(2)}) collective-permute-start(f32[2,16,1,4,128]{4,1,3,0,2:T(8,128)S(1)} %maximum_bitcast_fusion.1), channel_id=1, source_target_pairs={{0,16},{1,17},{2,18},{3,19},{4,20},{5,21},{6,22},{7,23},{8,24},{9,... | collective-permute-start | bytes 196616 | tf_op jit(solution)/shard_map/ppermute | solution.py:166
  11.2 8.1 %collective-permute-start.3 = (f32[2,16,2,4,128]{4,1,3,2,0:T(8,128)S(1)}, f32[2,16,2,4,128]{4,1,3,2,0:T(8,128)S(1)}, u32[]{:S(2)}, u32[]{:S(2)}) collective-permute-start(f32[2,16,2,4,128]{4,1,3,2,0:T(8,128)S(1)} %maximum_bitcast_fusion), channel_id=1, source_target_pairs={{0,8},{1,9},{2,10},{3,11},{4,12},{5,13},{6,14},{7,15},{8,0},{9,1},... | collective-permute-start | bytes 393224 | tf_op jit(solution)/shard_map/ppermute | solution.py:166
  19.3 7.7 %collective-permute-start.4 = (f32[2,16,4,4,128]{4,1,3,2,0:T(8,128)S(1)}, f32[2,16,4,4,128]{4,1,3,2,0:T(8,128)S(1)}, u32[]{:S(2)}, u32[]{:S(2)}) collective-permute-start(f32[2,16,4,4,128]{4,1,3,2,0:T(8,128)S(1)} %bitcast.99), channel_id=1, source_target_pairs={{0,4},{1,5},{2,6},{3,7},{4,0},{5,1},{6,2},{7,3},{8,12},{9,13},{10,... | collective-permute-start | bytes 786440 | tf_op jit(solution)/shard_map/ppermute | solution.py:166
  27.2 12.5 %collective-permute-start.5 = (f32[2,16,8,4,128]{4,1,3,2,0:T(8,128)S(1)}, f32[2,16,8,4,128]{4,1,3,2,0:T(8,128)S(1)}, u32[]{:S(2)}, u32[]{:S(2)}) collective-permute-start(f32[2,16,8,4,128]{4,1,3,2,0:T(8,128)S(1)} %bitcast.96), channel_id=1, source_target_pairs={{0,2},{1,3},{2,0},{3,1},{4,6},{5,7},{6,4},{7,5},{8,10},{9,11},{10,... | collective-permute-start | bytes 1572872 | tf_op jit(solution)/shard_map/ppermute | solution.py:166
  39.8 1.2 %copy-start.1 = (f32[1,16,128,128]{3,2,1,0:T(8,128)S(1)}, f32[1,16,128,128]{3,2,1,0:T(8,128)}, u32[]{:S(2)}) copy-start(f32[1,16,128,128]{3,2,1,0:T(8,128)} %param.9) | copy-start | bytes 3145732
  40.0 2.7 %collective-permute-start.6 = (f32[2,16,16,4,128]{4,1,3,2,0:T(8,128)S(1)}, f32[2,16,16,4,128]{4,1,3,2,0:T(8,128)S(1)}, u32[]{:S(2)}, u32[]{:S(2)}) collective-permute-start(f32[2,16,16,4,128]{4,1,3,2,0:T(8,128)S(1)} %bitcast.93), channel_id=1, source_target_pairs={{0,1},{1,0},{2,3},{3,2},{4,5},{5,4},{6,7},{7,6},{8,9},{9,8},{10,11... | collective-permute-start | bytes 3145736 | tf_op jit(solution)/shard_map/ppermute | solution.py:166
  43.0 6.1 %copy-start.2 = (f32[1,16,128,128]{3,2,1,0:T(8,128)S(1)}, f32[1,16,128,128]{3,2,1,0:T(8,128)}, u32[]{:S(2)}) copy-start(f32[1,16,128,128]{3,2,1,0:T(8,128)} %param.10) | copy-start | bytes 3145732
  43.9 5.4 %copy-start = (f32[2,16,16,2,4,128]{5,4,3,2,1,0:T(4,128)}, f32[2,16,16,2,4,128]{5,4,3,2,1,0:T(4,128)S(1)}, u32[]{:S(2)}) copy-start(f32[2,16,16,2,4,128]{5,4,3,2,1,0:T(4,128)S(1)} %copy.43) | copy-start | bytes 6291460
  43.9 11.2 %copy-start.7 = (f32[1,4,256]{2,1,0:T(4,128)S(1)}, f32[1,4,256]{2,1,0:T(4,128)}, u32[]{:S(2)}) copy-start(f32[1,4,256]{2,1,0:T(4,128)} %param.17) | copy-start | bytes 12292
  43.9 15.1 %copy-start.8 = (s32[1,256]{1,0:T(1,128)S(1)}, s32[1,256]{1,0:T(1,128)}, u32[]{:S(2)}) copy-start(s32[1,256]{1,0:T(1,128)} %param.16) | copy-start | bytes 3076
  44.0 15.1 %copy-start.9 = (s32[1,256]{1,0:T(1,128)S(1)}, s32[1,256]{1,0:T(1,128)}, u32[]{:S(2)}) copy-start(s32[1,256]{1,0:T(1,128)} %param.15) | copy-start | bytes 3076
  44.0 15.1 %collective-permute-start.7 = (f32[2,4,128,128]{3,2,1,0:T(8,128)S(1)}, f32[2,4,128,128]{3,2,1,0:T(8,128)}, u32[]{:S(2)}, u32[]{:S(2)}) collective-permute-start(f32[2,4,128,128]{3,2,1,0:T(8,128)S(1)} %constant_dynamic-slice_fusion.2), channel_id=1, source_target_pairs={{0,32},{2,34},{4,36},{6,38},{8,40},{10,42},{12,44},{14,46},{16,48}... | collective-permute-start | bytes 1572872 | tf_op jit(solution)/shard_map/ppermute | solution.py:219
  49.3 17.7 %collective-permute-start = (f32[2,4,128,128]{3,2,1,0:T(8,128)S(1)}, f32[2,4,128,128]{3,2,1,0:T(8,128)S(1)}, u32[]{:S(2)}, u32[]{:S(2)}) collective-permute-start(f32[2,4,128,128]{3,2,1,0:T(8,128)S(1)} %get-tuple-element.15), channel_id=1, source_target_pairs={{0,32},{32,64},{64,96},{96,128},{128,160},{160,192},{192,224},{1,3... | collective-permute-start | bytes 1572872 | tf_op jit(solution)/shard_map/ppermute | solution.py:153
  52.7 20.0 %collective-permute-start.1 = (f32[2,4,128,128]{3,2,1,0:T(8,128)S(1)}, f32[2,4,128,128]{3,2,1,0:T(8,128)S(1)}, u32[]{:S(2)}, u32[]{:S(2)}) collective-permute-start(f32[2,4,128,128]{3,2,1,0:T(8,128)S(1)} %get-tuple-element.14), channel_id=1, source_target_pairs={{32,0},{64,32},{96,64},{128,96},{160,128},{192,160},{224,192},{33,... | collective-permute-start | bytes 1572872 | tf_op jit(solution)/shard_map/ppermute | solution.py:153
  59.1 3.0 %collective-permute-start.8 = (f32[2,4,128,128]{3,2,1,0:T(8,128)}, f32[2,4,128,128]{3,2,1,0:T(8,128)S(1)}, u32[]{:S(2)}, u32[]{:S(2)}) collective-permute-start(f32[2,4,128,128]{3,2,1,0:T(8,128)} %collective-permute-done.7), channel_id=1, source_target_pairs={{0,1},{1,0},{2,3},{3,2},{4,5},{5,4},{6,7},{7,6},{8,9},{9,8},{10,11... | collective-permute-start | bytes 1572872 | tf_op jit(solution)/shard_map/ppermute | solution.py:220
  67.0 5.6 %copy-start.3 = (f32[2,4,128,128]{3,2,1,0:T(8,128)}, f32[2,4,128,128]{3,2,1,0:T(8,128)S(1)}, u32[]{:S(2)}) copy-start(f32[2,4,128,128]{3,2,1,0:T(8,128)S(1)} %collective-permute-done.adj_lo) | copy-start | bytes 1572868
  72.7 0.8 copy-start.4
  90.0 30.2 %copy-start.5 = (f32[16,4,128]{2,1,0:T(4,128)S(1)}, f32[16,4,128]{2,1,0:T(4,128)}, u32[]{:S(2)}) copy-start(f32[16,4,128]{2,1,0:T(4,128)} %param.12) | copy-start | bytes 98308
  90.0 30.2 %copy-start.6 = (f32[16,4,128]{2,1,0:T(4,128)S(1)}, f32[16,4,128]{2,1,0:T(4,128)}, u32[]{:S(2)}) copy-start(f32[16,4,128]{2,1,0:T(4,128)} %param.13) | copy-start | bytes 98308
  90.1 2.0 %collective-permute-start.9 = (f32[16,2,2,2,2,4,128]{6,0,5,4,3,2,1:T(8,128)S(1)}, f32[16,2,2,2,2,4,128]{6,0,5,4,3,2,1:T(8,128)S(1)}, u32[]{:S(2)}, u32[]{:S(2)}) collective-permute-start(f32[16,2,2,2,2,4,128]{6,0,5,4,3,2,1:T(8,128)S(1)} %bitcast.101), channel_id=1, source_target_pairs={{0,1},{1,0},{2,3},{3,2},{4,5},{5,4},{6,7},{7,6},{8,9},{9,8},{10,11... | collective-permute-start | bytes 1572872 | tf_op jit(solution)/shard_map/ppermute | solution.py:192
  92.4 8.4 %collective-permute-start.10 = (f32[16,2,2,2,4,128]{5,0,4,3,2,1:T(8,128)S(1)}, f32[16,2,2,2,4,128]{5,0,4,3,2,1:T(8,128)S(1)}, u32[]{:S(2)}, u32[]{:S(2)}) collective-permute-start(f32[16,2,2,2,4,128]{5,0,4,3,2,1:T(8,128)S(1)} %dynamic-slice_bitcast_fusion), channel_id=1, source_target_pairs={{0,2},{1,3},{2,0},{3,1},{4,6},{5,7},{6,4},{7,5},{8,10},{9,11},{10,... | collective-permute-start | bytes 786440 | tf_op jit(solution)/shard_map/ppermute | solution.py:192
  100.9 5.1 %collective-permute-start.11 = (f32[16,2,2,4,128]{4,0,3,2,1:T(8,128)S(1)}, f32[16,2,2,4,128]{4,0,3,2,1:T(8,128)S(1)}, u32[]{:S(2)}, u32[]{:S(2)}) collective-permute-start(f32[16,2,2,4,128]{4,0,3,2,1:T(8,128)S(1)} %dynamic-slice_bitcast_fusion.1), channel_id=1, source_target_pairs={{0,4},{1,5},{2,6},{3,7},{4,0},{5,1},{6,2},{7,3},{8,12},{9,13},{10,... | collective-permute-start | bytes 393224 | tf_op jit(solution)/shard_map/ppermute | solution.py:192
  106.0 6.0 %collective-permute-start.12 = (f32[16,2,4,128]{3,0,2,1:T(8,128)S(1)}, f32[16,2,4,128]{3,0,2,1:T(8,128)S(1)}, u32[]{:S(2)}, u32[]{:S(2)}) collective-permute-start(f32[16,2,4,128]{3,0,2,1:T(8,128)S(1)} %dynamic-slice_bitcast_fusion.2), channel_id=1, source_target_pairs={{0,8},{1,9},{2,10},{3,11},{4,12},{5,13},{6,14},{7,15},{8,0},{9,1},... | collective-permute-start | bytes 196616 | tf_op jit(solution)/shard_map/ppermute | solution.py:192
  112.0 8.2 %collective-permute-start.13 = (f32[16,4,128]{2,0,1:T(8,128)S(1)}, f32[16,4,128]{2,0,1:T(8,128)S(1)}, u32[]{:S(2)}, u32[]{:S(2)}) collective-permute-start(f32[16,4,128]{2,0,1:T(8,128)S(1)} %dynamic-slice_bitcast_fusion.3), channel_id=1, source_target_pairs={{0,16},{1,17},{2,18},{3,19},{4,20},{5,21},{6,22},{7,23},{8,24},{9,... | collective-permute-start | bytes 98312 | tf_op jit(solution)/shard_map/ppermute | solution.py:192

commit v6 on v5

--- a/solution.py
+++ b/solution.py
@@ -39,8 +39,21 @@
         return c
 
     inner_at, lo_at, hi_at = pl.ds(HALO, planes), pl.ds(0, HALO), pl.ds(HALO + planes, HALO)
-    need_mat = [fetch(mat_hbm, matb.at[:, inner_at]), fetch(mat_lo, matb.at[:, lo_at]),
-                fetch(mat_hi, matb.at[:, hi_at])]
+    need_mat = [fetch(mat_hbm, matb.at[:, inner_at])]
+    own = pltpu.make_async_copy(mat_lo, matb.at[:, lo_at], sems.at[10 + steps])
+    swapped = pltpu.make_async_copy(mat_hi, matb.at[:, hi_at], sems.at[11 + steps])
+
+    @pl.when(count_ref[1] == 0.0)
+    def _():
+        own.start()
+        swapped.start()
+
+    @pl.when(count_ref[1] != 0.0)
+    def _():
+        pltpu.make_async_copy(mat_lo, matb.at[:, hi_at], sems.at[11 + steps]).start()
+        pltpu.make_async_copy(mat_hi, matb.at[:, lo_at], sems.at[10 + steps]).start()
+
+    need_mat += [own, swapped]
     need_adj = [fetch(now_hbm, curb.at[inner_at]), fetch(adj_lo.at[0], curb.at[lo_at]),
                 fetch(adj_hi.at[0], curb.at[hi_at]), fetch(prev_hbm, oldb.at[inner_at]),
                 fetch(adj_lo.at[1], oldb.at[lo_at]), fetch(adj_hi.at[1], oldb.at[hi_at]),
@@ -91,7 +104,7 @@
 
             return carry
 
-        lax.fori_loop(lo, hi, plane, 0)
+        lax.fori_loop(lo, hi, plane, 0, unroll=2)
 
     def rd(ref):
         return lambda e: ref[e]
@@ -138,7 +151,7 @@
         out_specs=[pl.BlockSpec(memory_space=vmem)] * 3,
         scratch_shapes=[field, field, pltpu.VMEM((2, ext, nx, ny), jnp.float32),
                         pltpu.VMEM(snaps.shape, snaps.dtype), pltpu.VMEM(src.shape, jnp.float32)]
-        + [field] * 8 + [pltpu.SemaphoreType.DMA((10 + steps,))],
+        + [field] * 8 + [pltpu.SemaphoreType.DMA((12 + steps,))],
         compiler_params=pltpu.CompilerParams(vmem_limit_bytes=56 * 1024 * 1024),
         interpret=INTERPRET,
     )(count, adj_now, adj_prev, adj_lo, adj_hi, mat, mat_lo, mat_hi, snaps, src)
@@ -218,9 +231,7 @@
                 pairs.append((d * shots + s, to * shots + s))
     got = lax.ppermute(sent, ("depth", "shots"), pairs)
     other = lax.ppermute(got, "shots", [(s, s ^ 1) for s in range(shots)])
-    lo = jnp.where(core == 0, got, other)
-    hi = jnp.where(core == 0, other, got)
-    return lo, hi
+    return got, other
 
 
 def body(adj_now, adj_prev, fwd_snap, velocity, density, shot_count, rec_x, rec_y, residual):
@@ -236,7 +247,8 @@
     src = jnp.stack(
         [source_plane(rec_x[0], rec_y[0], residual[0, t], width_x, width_y) for t in range(steps)]
     ) * holds_source
-    count = shot_count.astype(jnp.float32)
+    core = (lax.axis_index("shots") % 2).astype(jnp.float32)
+    count = jnp.concatenate([shot_count.astype(jnp.float32), core[None]])
     current, older, weighted = run_steps(
         count, adj_now[0], adj_prev[0], adj_lo, adj_hi, packed, mat_lo, mat_hi, fwd_snap[0], src
     )

time: 121 us -> 124 us (1.025)
  waiting for transfers between devices: 64.2 us -> 65.7 us
    ppermute x2, waiting for transfers between devices: 8.42 us -> 12.8 us  [halo_of(): return (lax.ppermute(last, axis, up), lax.ppermute(first, axis, down))]
    ppermute x1, waiting for transfers between devices: 3.89 us -> 1.23 us  [split_halo(): got = lax.ppermute(sent, ('depth', 'shots'), pairs)]
    select_n x1 -> x0, other arithmetic: 2.12 us -> none  [split_halo(): hi = jnp.where(core == 0, other, got)]
  transfers between devices with their start and end apart: 14 -> 14, of which waited for: 13 -> 13; matrix products, arithmetic and copies ran while one was open for 4% -> 3% of each run, Pallas kernels for 0% -> 0%
where the time goes in v6:
time: 124 us
  waiting for transfers between devices  65.7 us (53%)
  starting transfers between devices  28.3 us (23%)
  Pallas kernels  15.5 us (12%)
  local copies, waits for them, and re-layouts  6.56 us (5%)
  other arithmetic  4.46 us (4%)
  between operations  1.69 us (1%)
  matrix products  1.61 us (1%)
    ppermute x5, waiting for transfers between devices, gather_rows(): got = lax.ppermute(pieces, axis, pairs)  27.4 us
    ppermute x5, waiting for transfers between devices, scatter_rows(): got = lax.ppermute(send, axis, pairs)  24.3 us
    pallas_call x1, Pallas kernels, run_steps(): pl.pallas_call(stencil_kernel, out_shape=out_shape, in_specs=[pl.BlockSpe...  15.5 us
    ppermute x2, waiting for transfers between devices, halo_of(): return (lax.ppermute(last, axis, up), lax.ppermute(first, axis, down))  12.8 us
    ppermute x5, starting transfers between devices, gather_rows(): got = lax.ppermute(pieces, axis, pairs)  12.1 us
    ppermute x2, starting transfers between devices, halo_of(): return (lax.ppermute(last, axis, up), lax.ppermute(first, axis, down))  5.83 us
    ppermute x5, starting transfers between devices, scatter_rows(): got = lax.ppermute(send, axis, pairs)  5.33 us
    ppermute x1, starting transfers between devices, split_halo(): got = lax.ppermute(sent, ('depth', 'shots'), pairs)  5 us
  transfers between devices with their start and end apart: 14, of which 13 were waited for; matrix products, arithmetic and copies ran while one was open for 3% of the time, Pallas kernels for 0%

profile of v6, /device:TPU:6, one launch (start us, length us, event | category | flops | bytes accessed | tf_op | source)
XLA Modules:
  0.0 123.8 jit_solution(8475102094148001413)
XLA Ops:
  0.6 0.8 fusion.20
  1.4 7.3 %collective-permute-start.2 = (f32[2,16,1,4,128]{4,1,3,0,2:T(8,128)S(1)}, f32[2,16,1,4,128]{4,1,3,0,2:T(8,128)S(1)}, u32[]{:S(2)}, u32[]{:S(2)}) collective-permute-start(f32[2,16,1,4,128]{4,1,3,0,2:T(8,128)S(1)} %maximum_bitcast_fusion.1), channel_id=1, source_target_pairs={{0,16},{1,17},{2,18},{3,19},{4,20},{5,21},{6,22},{7,23},{8,24},{9,... | collective-permute-start | bytes 196616 | tf_op jit(solution)/shard_map/ppermute | solution.py:179
  8.7 2.4 %collective-permute-done.2 = f32[2,16,1,4,128]{4,1,3,0,2:T(8,128)S(1)} collective-permute-done((f32[2,16,1,4,128]{4,1,3,0,2:T(8,128)S(1)}, f32[2,16,1,4,128]{4,1,3,0,2:T(8,128)S(1)}, u32[]{:S(2)}, u32[]{:S(2)}) %collective-permute-start.2) | collective-permute-done | bytes 65568 | tf_op jit(solution)/shard_map/ppermute | solution.py:179
  11.2 3.0 %collective-permute-start.3 = (f32[2,16,2,4,128]{4,1,3,2,0:T(8,128)S(1)}, f32[2,16,2,4,128]{4,1,3,2,0:T(8,128)S(1)}, u32[]{:S(2)}, u32[]{:S(2)}) collective-permute-start(f32[2,16,2,4,128]{4,1,3,2,0:T(8,128)S(1)} %maximum_bitcast_fusion), channel_id=1, source_target_pairs={{0,8},{1,9},{2,10},{3,11},{4,12},{5,13},{6,14},{7,15},{8,0},{9,1},... | collective-permute-start | bytes 393224 | tf_op jit(solution)/shard_map/ppermute | solution.py:179
  14.2 5.1 %collective-permute-done.3 = f32[2,16,2,4,128]{4,1,3,2,0:T(8,128)S(1)} collective-permute-done((f32[2,16,2,4,128]{4,1,3,2,0:T(8,128)S(1)}, f32[2,16,2,4,128]{4,1,3,2,0:T(8,128)S(1)}, u32[]{:S(2)}, u32[]{:S(2)}) %collective-permute-start.3) | collective-permute-done | bytes 131104 | tf_op jit(solution)/shard_map/ppermute | solution.py:179
  19.3 0.1 collective-permute-start.4
  19.4 7.6 %collective-permute-done.4 = f32[2,16,4,4,128]{4,1,3,2,0:T(8,128)S(1)} collective-permute-done((f32[2,16,4,4,128]{4,1,3,2,0:T(8,128)S(1)}, f32[2,16,4,4,128]{4,1,3,2,0:T(8,128)S(1)}, u32[]{:S(2)}, u32[]{:S(2)}) %collective-permute-start.4) | collective-permute-done | bytes 262176 | tf_op jit(solution)/shard_map/ppermute | solution.py:179
  27.2 1.7 %collective-permute-start.5 = (f32[2,16,8,4,128]{4,1,3,2,0:T(8,128)S(1)}, f32[2,16,8,4,128]{4,1,3,2,0:T(8,128)S(1)}, u32[]{:S(2)}, u32[]{:S(2)}) collective-permute-start(f32[2,16,8,4,128]{4,1,3,2,0:T(8,128)S(1)} %bitcast.97), channel_id=1, source_target_pairs={{0,2},{1,3},{2,0},{3,1},{4,6},{5,7},{6,4},{7,5},{8,10},{9,11},{10,... | collective-permute-start | bytes 1572872 | tf_op jit(solution)/shard_map/ppermute | solution.py:179
  28.8 10.8 %collective-permute-done.5 = f32[2,16,8,4,128]{4,1,3,2,0:T(8,128)S(1)} collective-permute-done((f32[2,16,8,4,128]{4,1,3,2,0:T(8,128)S(1)}, f32[2,16,8,4,128]{4,1,3,2,0:T(8,128)S(1)}, u32[]{:S(2)}, u32[]{:S(2)}) %collective-permute-start.5) | collective-permute-done | bytes 524320 | tf_op jit(solution)/shard_map/ppermute | solution.py:179
  39.6 0.1 select_bitcast_fusion.3
  39.8 0.0 copy-start.1
  39.8 0.1 pad_maximum_fusion.1
  39.9 0.0 copy-start.2
  39.9 0.1 copy.42
  40.0 0.1 collective-permute-start.6
  40.1 0.9 copy-done.1
  41.0 0.1 constant_dynamic-update-slice_fusion.1
  41.1 0.3 copy-done.2
  41.3 0.1 constant_dynamic-update-slice_fusion
  41.4 1.4 %collective-permute-done.6 = f32[2,16,16,4,128]{4,1,3,2,0:T(8,128)} collective-permute-done((f32[2,16,16,4,128]{4,1,3,2,0:T(8,128)S(1)}, f32[2,16,16,4,128]{4,1,3,2,0:T(8,128)}, u32[]{:S(2)}, u32[]{:S(2)}) %collective-permute-start.6) | collective-permute-done | bytes 1048608 | tf_op jit(solution)/shard_map/ppermute | solution.py:179
  42.8 1.4 %select_bitcast_fusion.1 = (f32[2,16,16,1,4,128]{5,1,4,2,0,3:T(8,128)S(1)}, f32[2,16,16,1,4,128]{5,1,4,2,0,3:T(8,128)S(1)}) fusion(f32[2,16,16,4,128]{4,1,3,2,0:T(8,128)S(1)} %bitcast.95, f32[2,16,16,4,128]{4,1,3,2,0:T(8,128)} %collective-permute-done.6, pred[]{:T(512)S(6)} %eq.33), kind=kLoop, calls=%fused_computation.7 | loop fusion | flops 524288 | bytes 4194305 | tf_op jit(solution)/shard_map/stack | solution.py:183
  44.2 0.1 pad_maximum_fusion
  44.4 0.8 copy.43
  45.2 0.0 copy-start
  45.2 0.0 copy-start.7
  45.2 0.0 copy-start.8
  45.2 0.0 copy-start.9
  45.3 0.8 constant_dynamic-slice_fusion.2
  46.1 5.0 %collective-permute-start.7 = (f32[2,4,128,128]{3,2,1,0:T(8,128)}, f32[2,4,128,128]{3,2,1,0:T(8,128)S(1)}, u32[]{:S(2)}, u32[]{:S(2)}) collective-permute-start(f32[2,4,128,128]{3,2,1,0:T(8,128)} %constant_dynamic-slice_fusion.2), channel_id=1, source_target_pairs={{0,32},{2,34},{4,36},{6,38},{8,40},{10,42},{12,44},{14,46},{16,48}... | collective-permute-start | bytes 1572872 | tf_op jit(solution)/shard_map/ppermute | solution.py:232
  51.1 1.0 fusion.27
  52.2 3.4 %collective-permute-start = (f32[2,4,128,128]{3,2,1,0:T(8,128)}, f32[2,4,128,128]{3,2,1,0:T(8,128)S(1)}, u32[]{:S(2)}, u32[]{:S(2)}) collective-permute-start(f32[2,4,128,128]{3,2,1,0:T(8,128)} %get-tuple-element.15), channel_id=1, source_target_pairs={{0,32},{32,64},{64,96},{96,128},{128,160},{160,192},{192,224},{1,3... | collective-permute-start | bytes 1572872 | tf_op jit(solution)/shard_map/ppermute | solution.py:166
  55.6 2.4 %collective-permute-start.1 = (f32[2,4,128,128]{3,2,1,0:T(8,128)}, f32[2,4,128,128]{3,2,1,0:T(8,128)}, u32[]{:S(2)}, u32[]{:S(2)}) collective-permute-start(f32[2,4,128,128]{3,2,1,0:T(8,128)} %get-tuple-element.14), channel_id=1, source_target_pairs={{32,0},{64,32},{96,64},{128,96},{160,128},{192,160},{224,192},{33,... | collective-permute-start | bytes 1572872 | tf_op jit(solution)/shard_map/ppermute | solution.py:166
  58.7 0.0 copy-done.7
  58.7 0.0 copy-done.8
  58.7 0.4 convolution_bitcast_fusion
  59.1 1.2 collective-permute-done.7.mat_lo
  60.3 0.0 collective-permute-start.8
  60.3 0.7 pad_maximum_fusion.4.count_ref
  61.0 0.4 convolution_bitcast_fusion.1
  61.4 0.4 convolution_bitcast_fusion.2
  61.8 0.4 convolution_bitcast_fusion.3
  62.2 0.7 maximum_multiply_fusion.src_hbm
  63.0 0.0 copy-done
  63.0 6.4 %collective-permute-done.adj_lo = f32[2,4,128,128]{3,2,1,0:T(8,128)S(1)} collective-permute-done((f32[2,4,128,128]{3,2,1,0:T(8,128)}, f32[2,4,128,128]{3,2,1,0:T(8,128)S(1)}, u32[]{:S(2)}, u32[]{:S(2)}) %collective-permute-start) | collective-permute-done | bytes 524320 | tf_op jit(solution)/shard_map/ppermute | solution.py:166
  69.3 6.5 %collective-permute-done.1.adj_hi = f32[2,4,128,128]{3,2,1,0:T(8,128)} collective-permute-done((f32[2,4,128,128]{3,2,1,0:T(8,128)}, f32[2,4,128,128]{3,2,1,0:T(8,128)}, u32[]{:S(2)}, u32[]{:S(2)}) %collective-permute-start.1) | collective-permute-done | bytes 524320 | tf_op jit(solution)/shard_map/ppermute | solution.py:166
  75.8 0.0 collective-permute-done.8.mat_hi
  75.8 15.5 %shard_map.112 = (f32[16,128,128]{2,1,0:T(8,128)}, f32[16,128,128]{2,1,0:T(8,128)}, f32[16,128,128]{2,1,0:T(8,128)}) custom-call(f32[2]{0:T(128)} %pad_maximum_fusion.4.count_ref, f32[16,128,128]{2,1,0:T(8,128)} %bitcast.92, f32[16,128,128]{2,1,0:T(8,128)} %bitcast.93, f32[2,4,128,128]{3,2,1,0:T(8,128)} %copy-done.4, ...), custom_call_target="tpu_custom_call" | custom-call | tf_op jit(solution)/shard_map/pallas_call | solution.py:147
  91.3 1.4 %constant_dynamic-slice_fusion.1 = (f32[16,2,2,2,2,1,4,128]{7,6,5,4,3,2,1,0:T(4,128)S(1)}, f32[16,2,2,2,2,1,4,128]{7,6,5,4,3,2,1,0:T(4,128)S(1)}) fusion(f32[16,2,2,2,2,2,4,128]{7,6,5,4,3,2,1,0:T(4,128)} %bitcast.99, s32[]{:T(128)S(6)} %select_n.126, s32[]{:T(128)S(6)} %select_n.127), kind=kLoop, calls=%fused_computation.61 | loop fusion | bytes 2097160 | tf_op jit(solution)/shard_map/jit(dynamic_index_in_dim)/dynamic_slice | solution.py:202
  92.7 0.3 copy.56
  93.0 0.0 copy-start.5
  93.0 0.0 copy-start.6
  93.0 0.1 collective-permute-start.9
  93.1 1.9 %collective-permute-done.9 = f32[16,2,2,2,2,4,128]{6,0,5,4,3,2,1:T(8,128)S(1)} collective-permute-done((f32[16,2,2,2,2,4,128]{6,0,5,4,3,2,1:T(8,128)S(1)}, f32[16,2,2,2,2,4,128]{6,0,5,4,3,2,1:T(8,128)S(1)}, u32[]{:S(2)}, u32[]{:S(2)}) %collective-permute-start.9) | collective-permute-done | bytes 524320 | tf_op jit(solution)/shard_map/ppermute | solution.py:205
  95.0 0.3 bitcast_add_fusion
  95.4 0.6 collective-permute-start.10
  96.0 7.9 %collective-permute-done.10 = f32[16,2,2,2,4,128]{5,0,4,3,2,1:T(8,128)S(1)} collective-permute-done((f32[16,2,2,2,4,128]{5,0,4,3,2,1:T(8,128)S(1)}, f32[16,2,2,2,4,128]{5,0,4,3,2,1:T(8,128)S(1)}, u32[]{:S(2)}, u32[]{:S(2)}) %collective-permute-start.10) | collective-permute-done | bytes 262176 | tf_op jit(solution)/shard_map/ppermute | solution.py:205
  103.9 0.7 collective-permute-start.11
  104.5 4.4 %collective-permute-done.11 = f32[16,2,2,4,128]{4,0,3,2,1:T(8,128)S(1)} collective-permute-done((f32[16,2,2,4,128]{4,0,3,2,1:T(8,128)S(1)}, f32[16,2,2,4,128]{4,0,3,2,1:T(8,128)S(1)}, u32[]{:S(2)}, u32[]{:S(2)}) %collective-permute-start.11) | collective-permute-done | bytes 131104 | tf_op jit(solution)/shard_map/ppermute | solution.py:205
  109.0 0.1 collective-permute-start.12
  109.1 5.9 %collective-permute-done.12 = f32[16,2,4,128]{3,0,2,1:T(8,128)S(1)} collective-permute-done((f32[16,2,4,128]{3,0,2,1:T(8,128)S(1)}, f32[16,2,4,128]{3,0,2,1:T(8,128)S(1)}, u32[]{:S(2)}, u32[]{:S(2)}) %collective-permute-start.12) | collective-permute-done | bytes 65568 | tf_op jit(solution)/shard_map/ppermute | solution.py:205
  115.0 3.9 %collective-permute-start.13 = (f32[16,4,128]{2,0,1:T(8,128)S(1)}, f32[16,4,128]{2,0,1:T(8,128)S(1)}, u32[]{:S(2)}, u32[]{:S(2)}) collective-permute-start(f32[16,4,128]{2,0,1:T(8,128)S(1)} %dynamic-slice_bitcast_fusion.3), channel_id=1, source_target_pairs={{0,16},{1,17},{2,18},{3,19},{4,20},{5,21},{6,22},{7,23},{8,24},{9,... | collective-permute-start | bytes 98312 | tf_op jit(solution)/shard_map/ppermute | solution.py:205
  118.9 4.3 %collective-permute-done.13 = f32[16,4,128]{2,0,1:T(8,128)S(1)} collective-permute-done((f32[16,4,128]{2,0,1:T(8,128)S(1)}, f32[16,4,128]{2,0,1:T(8,128)S(1)}, u32[]{:S(2)}, u32[]{:S(2)}) %collective-permute-start.13) | collective-permute-done | bytes 32800 | tf_op jit(solution)/shard_map/ppermute | solution.py:205
  123.2 0.0 copy-done.6
  123.2 0.6 copy.48
  (23 shorter events, 0.3 us)
Async XLA Ops:
  1.4 9.7 %collective-permute-start.2 = (f32[2,16,1,4,128]{4,1,3,0,2:T(8,128)S(1)}, f32[2,16,1,4,128]{4,1,3,0,2:T(8,128)S(1)}, u32[]{:S(2)}, u32[]{:S(2)}) collective-permute-start(f32[2,16,1,4,128]{4,1,3,0,2:T(8,128)S(1)} %maximum_bitcast_fusion.1), channel_id=1, source_target_pairs={{0,16},{1,17},{2,18},{3,19},{4,20},{5,21},{6,22},{7,23},{8,24},{9,... | collective-permute-start | bytes 196616 | tf_op jit(solution)/shard_map/ppermute | solution.py:179
  11.2 8.1 %collective-permute-start.3 = (f32[2,16,2,4,128]{4,1,3,2,0:T(8,128)S(1)}, f32[2,16,2,4,128]{4,1,3,2,0:T(8,128)S(1)}, u32[]{:S(2)}, u32[]{:S(2)}) collective-permute-start(f32[2,16,2,4,128]{4,1,3,2,0:T(8,128)S(1)} %maximum_bitcast_fusion), channel_id=1, source_target_pairs={{0,8},{1,9},{2,10},{3,11},{4,12},{5,13},{6,14},{7,15},{8,0},{9,1},... | collective-permute-start | bytes 393224 | tf_op jit(solution)/shard_map/ppermute | solution.py:179
  19.3 7.7 %collective-permute-start.4 = (f32[2,16,4,4,128]{4,1,3,2,0:T(8,128)S(1)}, f32[2,16,4,4,128]{4,1,3,2,0:T(8,128)S(1)}, u32[]{:S(2)}, u32[]{:S(2)}) collective-permute-start(f32[2,16,4,4,128]{4,1,3,2,0:T(8,128)S(1)} %bitcast.100), channel_id=1, source_target_pairs={{0,4},{1,5},{2,6},{3,7},{4,0},{5,1},{6,2},{7,3},{8,12},{9,13},{10,... | collective-permute-start | bytes 786440 | tf_op jit(solution)/shard_map/ppermute | solution.py:179
  27.2 12.5 %collective-permute-start.5 = (f32[2,16,8,4,128]{4,1,3,2,0:T(8,128)S(1)}, f32[2,16,8,4,128]{4,1,3,2,0:T(8,128)S(1)}, u32[]{:S(2)}, u32[]{:S(2)}) collective-permute-start(f32[2,16,8,4,128]{4,1,3,2,0:T(8,128)S(1)} %bitcast.97), channel_id=1, source_target_pairs={{0,2},{1,3},{2,0},{3,1},{4,6},{5,7},{6,4},{7,5},{8,10},{9,11},{10,... | collective-permute-start | bytes 1572872 | tf_op jit(solution)/shard_map/ppermute | solution.py:179
  39.8 1.2 copy-start.1
  39.9 1.5 %copy-start.2 = (f32[1,16,128,128]{3,2,1,0:T(8,128)S(1)}, f32[1,16,128,128]{3,2,1,0:T(8,128)}, u32[]{:S(2)}) copy-start(f32[1,16,128,128]{3,2,1,0:T(8,128)} %param.10) | copy-start | bytes 3145732
  40.0 2.9 %collective-permute-start.6 = (f32[2,16,16,4,128]{4,1,3,2,0:T(8,128)S(1)}, f32[2,16,16,4,128]{4,1,3,2,0:T(8,128)}, u32[]{:S(2)}, u32[]{:S(2)}) collective-permute-start(f32[2,16,16,4,128]{4,1,3,2,0:T(8,128)S(1)} %bitcast.94), channel_id=1, source_target_pairs={{0,1},{1,0},{2,3},{3,2},{4,5},{5,4},{6,7},{7,6},{8,9},{9,8},{10,11... | collective-permute-start | bytes 3145736 | tf_op jit(solution)/shard_map/ppermute | solution.py:179
  45.2 17.8 %copy-start = (f32[2,16,16,2,4,128]{5,4,3,2,1,0:T(4,128)}, f32[2,16,16,2,4,128]{5,4,3,2,1,0:T(4,128)S(1)}, u32[]{:S(2)}) copy-start(f32[2,16,16,2,4,128]{5,4,3,2,1,0:T(4,128)S(1)} %copy.43) | copy-start | bytes 6291460
  45.2 13.4 %copy-start.7 = (f32[1,4,256]{2,1,0:T(4,128)S(1)}, f32[1,4,256]{2,1,0:T(4,128)}, u32[]{:S(2)}) copy-start(f32[1,4,256]{2,1,0:T(4,128)} %param.17) | copy-start | bytes 12292
  45.2 13.4 %copy-start.8 = (s32[1,256]{1,0:T(1,128)S(1)}, s32[1,256]{1,0:T(1,128)}, u32[]{:S(2)}) copy-start(s32[1,256]{1,0:T(1,128)} %param.16) | copy-start | bytes 3076
  45.2 13.4 %copy-start.9 = (s32[1,256]{1,0:T(1,128)S(1)}, s32[1,256]{1,0:T(1,128)}, u32[]{:S(2)}) copy-start(s32[1,256]{1,0:T(1,128)} %param.15) | copy-start | bytes 3076
  46.1 14.2 %collective-permute-start.7 = (f32[2,4,128,128]{3,2,1,0:T(8,128)}, f32[2,4,128,128]{3,2,1,0:T(8,128)S(1)}, u32[]{:S(2)}, u32[]{:S(2)}) collective-permute-start(f32[2,4,128,128]{3,2,1,0:T(8,128)} %constant_dynamic-slice_fusion.2), channel_id=1, source_target_pairs={{0,32},{2,34},{4,36},{6,38},{8,40},{10,42},{12,44},{14,46},{16,48}... | collective-permute-start | bytes 1572872 | tf_op jit(solution)/shard_map/ppermute | solution.py:232
  52.2 17.2 %collective-permute-start = (f32[2,4,128,128]{3,2,1,0:T(8,128)}, f32[2,4,128,128]{3,2,1,0:T(8,128)S(1)}, u32[]{:S(2)}, u32[]{:S(2)}) collective-permute-start(f32[2,4,128,128]{3,2,1,0:T(8,128)} %get-tuple-element.15), channel_id=1, source_target_pairs={{0,32},{32,64},{64,96},{96,128},{128,160},{160,192},{192,224},{1,3... | collective-permute-start | bytes 1572872 | tf_op jit(solution)/shard_map/ppermute | solution.py:166
  55.6 20.3 %collective-permute-start.1 = (f32[2,4,128,128]{3,2,1,0:T(8,128)}, f32[2,4,128,128]{3,2,1,0:T(8,128)}, u32[]{:S(2)}, u32[]{:S(2)}) collective-permute-start(f32[2,4,128,128]{3,2,1,0:T(8,128)} %get-tuple-element.14), channel_id=1, source_target_pairs={{32,0},{64,32},{96,64},{128,96},{160,128},{192,160},{224,192},{33,... | collective-permute-start | bytes 1572872 | tf_op jit(solution)/shard_map/ppermute | solution.py:166
  60.3 15.5 %copy-start.3 = (f32[2,4,128,128]{3,2,1,0:T(8,128)}, f32[2,4,128,128]{3,2,1,0:T(8,128)S(1)}, u32[]{:S(2)}) copy-start(f32[2,4,128,128]{3,2,1,0:T(8,128)S(1)} %collective-permute-done.7.mat_lo) | copy-start | bytes 1572868
  60.3 15.5 %collective-permute-start.8 = (f32[2,4,128,128]{3,2,1,0:T(8,128)S(1)}, f32[2,4,128,128]{3,2,1,0:T(8,128)}, u32[]{:S(2)}, u32[]{:S(2)}) collective-permute-start(f32[2,4,128,128]{3,2,1,0:T(8,128)S(1)} %collective-permute-done.7.mat_lo), channel_id=1, source_target_pairs={{0,1},{1,0},{2,3},{3,2},{4,5},{5,4},{6,7},{7,6},{8,9},{9,8},{10,11... | collective-permute-start | bytes 1572872 | tf_op jit(solution)/shard_map/ppermute | solution.py:233
  69.3 6.5 %copy-start.4 = (f32[2,4,128,128]{3,2,1,0:T(8,128)}, f32[2,4,128,128]{3,2,1,0:T(8,128)S(1)}, u32[]{:S(2)}) copy-start(f32[2,4,128,128]{3,2,1,0:T(8,128)S(1)} %collective-permute-done.adj_lo) | copy-start | bytes 1572868
  93.0 30.2 %copy-start.5 = (f32[16,4,128]{2,1,0:T(4,128)S(1)}, f32[16,4,128]{2,1,0:T(4,128)}, u32[]{:S(2)}) copy-start(f32[16,4,128]{2,1,0:T(4,128)} %param.12) | copy-start | bytes 98308
  93.0 30.2 %copy-start.6 = (f32[16,4,128]{2,1,0:T(4,128)S(1)}, f32[16,4,128]{2,1,0:T(4,128)}, u32[]{:S(2)}) copy-start(f32[16,4,128]{2,1,0:T(4,128)} %param.13) | copy-start | bytes 98308
  93.0 2.0 %collective-permute-start.9 = (f32[16,2,2,2,2,4,128]{6,0,5,4,3,2,1:T(8,128)S(1)}, f32[16,2,2,2,2,4,128]{6,0,5,4,3,2,1:T(8,128)S(1)}, u32[]{:S(2)}, u32[]{:S(2)}) collective-permute-start(f32[16,2,2,2,2,4,128]{6,0,5,4,3,2,1:T(8,128)S(1)} %bitcast.102), channel_id=1, source_target_pairs={{0,1},{1,0},{2,3},{3,2},{4,5},{5,4},{6,7},{7,6},{8,9},{9,8},{10,11... | collective-permute-start | bytes 1572872 | tf_op jit(solution)/shard_map/ppermute | solution.py:205
  95.4 8.4 %collective-permute-start.10 = (f32[16,2,2,2,4,128]{5,0,4,3,2,1:T(8,128)S(1)}, f32[16,2,2,2,4,128]{5,0,4,3,2,1:T(8,128)S(1)}, u32[]{:S(2)}, u32[]{:S(2)}) collective-permute-start(f32[16,2,2,2,4,128]{5,0,4,3,2,1:T(8,128)S(1)} %dynamic-slice_bitcast_fusion), channel_id=1, source_target_pairs={{0,2},{1,3},{2,0},{3,1},{4,6},{5,7},{6,4},{7,5},{8,10},{9,11},{10,... | collective-permute-start | bytes 786440 | tf_op jit(solution)/shard_map/ppermute | solution.py:205
  103.9 5.1 %collective-permute-start.11 = (f32[16,2,2,4,128]{4,0,3,2,1:T(8,128)S(1)}, f32[16,2,2,4,128]{4,0,3,2,1:T(8,128)S(1)}, u32[]{:S(2)}, u32[]{:S(2)}) collective-permute-start(f32[16,2,2,4,128]{4,0,3,2,1:T(8,128)S(1)} %dynamic-slice_bitcast_fusion.1), channel_id=1, source_target_pairs={{0,4},{1,5},{2,6},{3,7},{4,0},{5,1},{6,2},{7,3},{8,12},{9,13},{10,... | collective-permute-start | bytes 393224 | tf_op jit(solution)/shard_map/ppermute | solution.py:205
  109.0 6.0 %collective-permute-start.12 = (f32[16,2,4,128]{3,0,2,1:T(8,128)S(1)}, f32[16,2,4,128]{3,0,2,1:T(8,128)S(1)}, u32[]{:S(2)}, u32[]{:S(2)}) collective-permute-start(f32[16,2,4,128]{3,0,2,1:T(8,128)S(1)} %dynamic-slice_bitcast_fusion.2), channel_id=1, source_target_pairs={{0,8},{1,9},{2,10},{3,11},{4,12},{5,13},{6,14},{7,15},{8,0},{9,1},... | collective-permute-start | bytes 196616 | tf_op jit(solution)/shard_map/ppermute | solution.py:205
  115.0 8.2 %collective-permute-start.13 = (f32[16,4,128]{2,0,1:T(8,128)S(1)}, f32[16,4,128]{2,0,1:T(8,128)S(1)}, u32[]{:S(2)}, u32[]{:S(2)}) collective-permute-start(f32[16,4,128]{2,0,1:T(8,128)S(1)} %dynamic-slice_bitcast_fusion.3), channel_id=1, source_target_pairs={{0,16},{1,17},{2,18},{3,19},{4,20},{5,21},{6,22},{7,23},{8,24},{9,... | collective-permute-start | bytes 98312 | tf_op jit(solution)/shard_map/ppermute | solution.py:205

commit v7 on v6

--- a/solution.py
+++ b/solution.py
@@ -81,13 +81,14 @@
         moment = steps - 1 - step
         need_snap[step].wait()
 
-        def plane(e, carry):
+        def plane(e, with_source):
             pc = cur(e)
             total = kz[e] * (cur(e + 1) - pc) - kz[e - 1] * (pc - cur(e - 1))
             total = total + (kxf[e] * (shift_fwd(pc, 0, nx) - pc) - kxb[e] * (pc - shift_bwd(pc, 0)))
             total = total + (kyf[e] * (shift_fwd(pc, 1, ny) - pc) - kyb[e] * (pc - shift_bwd(pc, 1)))
-            weight = jnp.where(e == HALO + 2, 1.0, 0.0)
-            new = 2.0 * pc - old(e) + kk[e] * total + 0.08 * srcb[moment] * weight
+            new = 2.0 * pc - old(e) + kk[e] * total
+            if with_source:
+                new = new + 0.08 * srcb[moment]
             dst(e, new)
             inner = jnp.logical_and(e >= HALO, e < ext - HALO)
 
@@ -102,9 +103,14 @@
                 else:
                     img_ref[z] = img_ref[z] + gained
 
+        def plain(e, carry):
+            plane(e, False)
             return carry
 
-        lax.fori_loop(lo, hi, plane, 0, unroll=2)
+        at_source = HALO + 2
+        lax.fori_loop(lo, at_source, plain, 0)
+        plane(at_source, True)
+        lax.fori_loop(at_source + 1, hi, plain, 0, unroll=2)
 
     def rd(ref):
         return lambda e: ref[e]

time: 124 us -> 124 us (level)
  no operation moved by 1% of the time
where the time goes in v7:
time: 124 us
  waiting for transfers between devices  65.7 us (53%)
  starting transfers between devices  28.3 us (23%)
  Pallas kernels  15.3 us (12%)
  local copies, waits for them, and re-layouts  6.56 us (5%)
  other arithmetic  4.46 us (4%)
  between operations  1.69 us (1%)
  matrix products  1.61 us (1%)
    ppermute x5, waiting for transfers between devices, gather_rows(): got = lax.ppermute(pieces, axis, pairs)  27.4 us
    ppermute x5, waiting for transfers between devices, scatter_rows(): got = lax.ppermute(send, axis, pairs)  24.3 us
    pallas_call x1, Pallas kernels, run_steps(): pl.pallas_call(stencil_kernel, out_shape=out_shape, in_specs=[pl.BlockSpe...  15.3 us
    ppermute x2, waiting for transfers between devices, halo_of(): return (lax.ppermute(last, axis, up), lax.ppermute(first, axis, down))  12.8 us
    ppermute x5, starting transfers between devices, gather_rows(): got = lax.ppermute(pieces, axis, pairs)  12.1 us
    ppermute x2, starting transfers between devices, halo_of(): return (lax.ppermute(last, axis, up), lax.ppermute(first, axis, down))  5.83 us
    ppermute x5, starting transfers between devices, scatter_rows(): got = lax.ppermute(send, axis, pairs)  5.33 us
    ppermute x1, starting transfers between devices, split_halo(): got = lax.ppermute(sent, ('depth', 'shots'), pairs)  5 us
  transfers between devices with their start and end apart: 14, of which 13 were waited for; matrix products, arithmetic and copies ran while one was open for 3% of the time, Pallas kernels for 0%

profile of v7, /device:TPU:6, one launch (start us, length us, event | category | flops | bytes accessed | tf_op | source)
XLA Modules:
  0.0 123.6 jit_solution(4150988613389731464)
XLA Ops:
  0.6 0.8 fusion.20
  1.4 7.3 %collective-permute-start.2 = (f32[2,16,1,4,128]{4,1,3,0,2:T(8,128)S(1)}, f32[2,16,1,4,128]{4,1,3,0,2:T(8,128)S(1)}, u32[]{:S(2)}, u32[]{:S(2)}) collective-permute-start(f32[2,16,1,4,128]{4,1,3,0,2:T(8,128)S(1)} %maximum_bitcast_fusion.1), channel_id=1, source_target_pairs={{0,16},{1,17},{2,18},{3,19},{4,20},{5,21},{6,22},{7,23},{8,24},{9,... | collective-permute-start | bytes 196616 | tf_op jit(solution)/shard_map/ppermute | solution.py:185
  8.7 2.4 %collective-permute-done.2 = f32[2,16,1,4,128]{4,1,3,0,2:T(8,128)S(1)} collective-permute-done((f32[2,16,1,4,128]{4,1,3,0,2:T(8,128)S(1)}, f32[2,16,1,4,128]{4,1,3,0,2:T(8,128)S(1)}, u32[]{:S(2)}, u32[]{:S(2)}) %collective-permute-start.2) | collective-permute-done | bytes 65568 | tf_op jit(solution)/shard_map/ppermute | solution.py:185
  11.2 3.0 %collective-permute-start.3 = (f32[2,16,2,4,128]{4,1,3,2,0:T(8,128)S(1)}, f32[2,16,2,4,128]{4,1,3,2,0:T(8,128)S(1)}, u32[]{:S(2)}, u32[]{:S(2)}) collective-permute-start(f32[2,16,2,4,128]{4,1,3,2,0:T(8,128)S(1)} %maximum_bitcast_fusion), channel_id=1, source_target_pairs={{0,8},{1,9},{2,10},{3,11},{4,12},{5,13},{6,14},{7,15},{8,0},{9,1},... | collective-permute-start | bytes 393224 | tf_op jit(solution)/shard_map/ppermute | solution.py:185
  14.2 5.1 %collective-permute-done.3 = f32[2,16,2,4,128]{4,1,3,2,0:T(8,128)S(1)} collective-permute-done((f32[2,16,2,4,128]{4,1,3,2,0:T(8,128)S(1)}, f32[2,16,2,4,128]{4,1,3,2,0:T(8,128)S(1)}, u32[]{:S(2)}, u32[]{:S(2)}) %collective-permute-start.3) | collective-permute-done | bytes 131104 | tf_op jit(solution)/shard_map/ppermute | solution.py:185
  19.3 0.1 collective-permute-start.4
  19.4 7.6 %collective-permute-done.4 = f32[2,16,4,4,128]{4,1,3,2,0:T(8,128)S(1)} collective-permute-done((f32[2,16,4,4,128]{4,1,3,2,0:T(8,128)S(1)}, f32[2,16,4,4,128]{4,1,3,2,0:T(8,128)S(1)}, u32[]{:S(2)}, u32[]{:S(2)}) %collective-permute-start.4) | collective-permute-done | bytes 262176 | tf_op jit(solution)/shard_map/ppermute | solution.py:185
  27.2 1.7 %collective-permute-start.5 = (f32[2,16,8,4,128]{4,1,3,2,0:T(8,128)S(1)}, f32[2,16,8,4,128]{4,1,3,2,0:T(8,128)S(1)}, u32[]{:S(2)}, u32[]{:S(2)}) collective-permute-start(f32[2,16,8,4,128]{4,1,3,2,0:T(8,128)S(1)} %bitcast.97), channel_id=1, source_target_pairs={{0,2},{1,3},{2,0},{3,1},{4,6},{5,7},{6,4},{7,5},{8,10},{9,11},{10,... | collective-permute-start | bytes 1572872 | tf_op jit(solution)/shard_map/ppermute | solution.py:185
  28.8 10.8 %collective-permute-done.5 = f32[2,16,8,4,128]{4,1,3,2,0:T(8,128)S(1)} collective-permute-done((f32[2,16,8,4,128]{4,1,3,2,0:T(8,128)S(1)}, f32[2,16,8,4,128]{4,1,3,2,0:T(8,128)S(1)}, u32[]{:S(2)}, u32[]{:S(2)}) %collective-permute-start.5) | collective-permute-done | bytes 524320 | tf_op jit(solution)/shard_map/ppermute | solution.py:185
  39.6 0.1 select_bitcast_fusion.3
  39.8 0.0 copy-start.1
  39.8 0.1 pad_maximum_fusion.1
  39.9 0.0 copy-start.2
  39.9 0.1 copy.42
  40.0 0.1 collective-permute-start.6
  40.1 0.9 copy-done.1
  41.0 0.1 constant_dynamic-update-slice_fusion.1
  41.1 0.3 copy-done.2
  41.3 0.1 constant_dynamic-update-slice_fusion
  41.4 1.4 %collective-permute-done.6 = f32[2,16,16,4,128]{4,1,3,2,0:T(8,128)} collective-permute-done((f32[2,16,16,4,128]{4,1,3,2,0:T(8,128)S(1)}, f32[2,16,16,4,128]{4,1,3,2,0:T(8,128)}, u32[]{:S(2)}, u32[]{:S(2)}) %collective-permute-start.6) | collective-permute-done | bytes 1048608 | tf_op jit(solution)/shard_map/ppermute | solution.py:185
  42.8 1.4 %select_bitcast_fusion.1 = (f32[2,16,16,1,4,128]{5,1,4,2,0,3:T(8,128)S(1)}, f32[2,16,16,1,4,128]{5,1,4,2,0,3:T(8,128)S(1)}) fusion(f32[2,16,16,4,128]{4,1,3,2,0:T(8,128)S(1)} %bitcast.95, f32[2,16,16,4,128]{4,1,3,2,0:T(8,128)} %collective-permute-done.6, pred[]{:T(512)S(6)} %eq.33), kind=kLoop, calls=%fused_computation.7 | loop fusion | flops 524288 | bytes 4194305 | tf_op jit(solution)/shard_map/stack | solution.py:189
  44.2 0.1 pad_maximum_fusion
  44.4 0.8 copy.43
  45.2 0.0 copy-start
  45.2 0.0 copy-start.7
  45.2 0.0 copy-start.8
  45.2 0.0 copy-start.9
  45.3 0.8 constant_dynamic-slice_fusion.2
  46.1 5.0 %collective-permute-start.7 = (f32[2,4,128,128]{3,2,1,0:T(8,128)}, f32[2,4,128,128]{3,2,1,0:T(8,128)S(1)}, u32[]{:S(2)}, u32[]{:S(2)}) collective-permute-start(f32[2,4,128,128]{3,2,1,0:T(8,128)} %constant_dynamic-slice_fusion.2), channel_id=1, source_target_pairs={{0,32},{2,34},{4,36},{6,38},{8,40},{10,42},{12,44},{14,46},{16,48}... | collective-permute-start | bytes 1572872 | tf_op jit(solution)/shard_map/ppermute | solution.py:238
  51.1 1.0 fusion.27
  52.2 3.4 %collective-permute-start = (f32[2,4,128,128]{3,2,1,0:T(8,128)}, f32[2,4,128,128]{3,2,1,0:T(8,128)S(1)}, u32[]{:S(2)}, u32[]{:S(2)}) collective-permute-start(f32[2,4,128,128]{3,2,1,0:T(8,128)} %get-tuple-element.15), channel_id=1, source_target_pairs={{0,32},{32,64},{64,96},{96,128},{128,160},{160,192},{192,224},{1,3... | collective-permute-start | bytes 1572872 | tf_op jit(solution)/shard_map/ppermute | solution.py:172
  55.6 2.4 %collective-permute-start.1 = (f32[2,4,128,128]{3,2,1,0:T(8,128)}, f32[2,4,128,128]{3,2,1,0:T(8,128)}, u32[]{:S(2)}, u32[]{:S(2)}) collective-permute-start(f32[2,4,128,128]{3,2,1,0:T(8,128)} %get-tuple-element.14), channel_id=1, source_target_pairs={{32,0},{64,32},{96,64},{128,96},{160,128},{192,160},{224,192},{33,... | collective-permute-start | bytes 1572872 | tf_op jit(solution)/shard_map/ppermute | solution.py:172
  58.7 0.0 copy-done.7
  58.7 0.0 copy-done.8
  58.7 0.4 convolution_bitcast_fusion
  59.1 1.2 collective-permute-done.7.mat_lo
  60.3 0.0 collective-permute-start.8
  60.3 0.7 pad_maximum_fusion.4.count_ref
  61.0 0.4 convolution_bitcast_fusion.1
  61.4 0.4 convolution_bitcast_fusion.2
  61.8 0.4 convolution_bitcast_fusion.3
  62.2 0.7 maximum_multiply_fusion.src_hbm
  63.0 0.0 copy-done
  63.0 6.4 %collective-permute-done.adj_lo = f32[2,4,128,128]{3,2,1,0:T(8,128)S(1)} collective-permute-done((f32[2,4,128,128]{3,2,1,0:T(8,128)}, f32[2,4,128,128]{3,2,1,0:T(8,128)S(1)}, u32[]{:S(2)}, u32[]{:S(2)}) %collective-permute-start) | collective-permute-done | bytes 524320 | tf_op jit(solution)/shard_map/ppermute | solution.py:172
  69.3 6.5 %collective-permute-done.1.adj_hi = f32[2,4,128,128]{3,2,1,0:T(8,128)} collective-permute-done((f32[2,4,128,128]{3,2,1,0:T(8,128)}, f32[2,4,128,128]{3,2,1,0:T(8,128)}, u32[]{:S(2)}, u32[]{:S(2)}) %collective-permute-start.1) | collective-permute-done | bytes 524320 | tf_op jit(solution)/shard_map/ppermute | solution.py:172
  75.8 0.0 collective-permute-done.8.mat_hi
  75.8 15.3 %shard_map.112 = (f32[16,128,128]{2,1,0:T(8,128)}, f32[16,128,128]{2,1,0:T(8,128)}, f32[16,128,128]{2,1,0:T(8,128)}) custom-call(f32[2]{0:T(128)} %pad_maximum_fusion.4.count_ref, f32[16,128,128]{2,1,0:T(8,128)} %bitcast.92, f32[16,128,128]{2,1,0:T(8,128)} %bitcast.93, f32[2,4,128,128]{3,2,1,0:T(8,128)} %copy-done.4, ...), custom_call_target="tpu_custom_call" | custom-call | tf_op jit(solution)/shard_map/pallas_call | solution.py:153
  91.1 1.4 %constant_dynamic-slice_fusion.1 = (f32[16,2,2,2,2,1,4,128]{7,6,5,4,3,2,1,0:T(4,128)S(1)}, f32[16,2,2,2,2,1,4,128]{7,6,5,4,3,2,1,0:T(4,128)S(1)}) fusion(f32[16,2,2,2,2,2,4,128]{7,6,5,4,3,2,1,0:T(4,128)} %bitcast.99, s32[]{:T(128)S(6)} %select_n.126, s32[]{:T(128)S(6)} %select_n.127), kind=kLoop, calls=%fused_computation.61 | loop fusion | bytes 2097160 | tf_op jit(solution)/shard_map/jit(dynamic_index_in_dim)/dynamic_slice | solution.py:208
  92.5 0.3 copy.56
  92.8 0.0 copy-start.5
  92.8 0.0 copy-start.6
  92.8 0.1 collective-permute-start.9
  92.9 1.9 %collective-permute-done.9 = f32[16,2,2,2,2,4,128]{6,0,5,4,3,2,1:T(8,128)S(1)} collective-permute-done((f32[16,2,2,2,2,4,128]{6,0,5,4,3,2,1:T(8,128)S(1)}, f32[16,2,2,2,2,4,128]{6,0,5,4,3,2,1:T(8,128)S(1)}, u32[]{:S(2)}, u32[]{:S(2)}) %collective-permute-start.9) | collective-permute-done | bytes 524320 | tf_op jit(solution)/shard_map/ppermute | solution.py:211
  94.8 0.3 bitcast_add_fusion
  95.2 0.6 collective-permute-start.10
  95.8 7.9 %collective-permute-done.10 = f32[16,2,2,2,4,128]{5,0,4,3,2,1:T(8,128)S(1)} collective-permute-done((f32[16,2,2,2,4,128]{5,0,4,3,2,1:T(8,128)S(1)}, f32[16,2,2,2,4,128]{5,0,4,3,2,1:T(8,128)S(1)}, u32[]{:S(2)}, u32[]{:S(2)}) %collective-permute-start.10) | collective-permute-done | bytes 262176 | tf_op jit(solution)/shard_map/ppermute | solution.py:211
  103.7 0.7 collective-permute-start.11
  104.3 4.4 %collective-permute-done.11 = f32[16,2,2,4,128]{4,0,3,2,1:T(8,128)S(1)} collective-permute-done((f32[16,2,2,4,128]{4,0,3,2,1:T(8,128)S(1)}, f32[16,2,2,4,128]{4,0,3,2,1:T(8,128)S(1)}, u32[]{:S(2)}, u32[]{:S(2)}) %collective-permute-start.11) | collective-permute-done | bytes 131104 | tf_op jit(solution)/shard_map/ppermute | solution.py:211
  108.8 0.1 collective-permute-start.12
  108.9 5.9 %collective-permute-done.12 = f32[16,2,4,128]{3,0,2,1:T(8,128)S(1)} collective-permute-done((f32[16,2,4,128]{3,0,2,1:T(8,128)S(1)}, f32[16,2,4,128]{3,0,2,1:T(8,128)S(1)}, u32[]{:S(2)}, u32[]{:S(2)}) %collective-permute-start.12) | collective-permute-done | bytes 65568 | tf_op jit(solution)/shard_map/ppermute | solution.py:211
  114.8 3.9 %collective-permute-start.13 = (f32[16,4,128]{2,0,1:T(8,128)S(1)}, f32[16,4,128]{2,0,1:T(8,128)S(1)}, u32[]{:S(2)}, u32[]{:S(2)}) collective-permute-start(f32[16,4,128]{2,0,1:T(8,128)S(1)} %dynamic-slice_bitcast_fusion.3), channel_id=1, source_target_pairs={{0,16},{1,17},{2,18},{3,19},{4,20},{5,21},{6,22},{7,23},{8,24},{9,... | collective-permute-start | bytes 98312 | tf_op jit(solution)/shard_map/ppermute | solution.py:211
  118.7 4.3 %collective-permute-done.13 = f32[16,4,128]{2,0,1:T(8,128)S(1)} collective-permute-done((f32[16,4,128]{2,0,1:T(8,128)S(1)}, f32[16,4,128]{2,0,1:T(8,128)S(1)}, u32[]{:S(2)}, u32[]{:S(2)}) %collective-permute-start.13) | collective-permute-done | bytes 32800 | tf_op jit(solution)/shard_map/ppermute | solution.py:211
  123.0 0.0 copy-done.6
  123.0 0.6 copy.48
  (23 shorter events, 0.3 us)
Async XLA Ops:
  1.4 9.7 %collective-permute-start.2 = (f32[2,16,1,4,128]{4,1,3,0,2:T(8,128)S(1)}, f32[2,16,1,4,128]{4,1,3,0,2:T(8,128)S(1)}, u32[]{:S(2)}, u32[]{:S(2)}) collective-permute-start(f32[2,16,1,4,128]{4,1,3,0,2:T(8,128)S(1)} %maximum_bitcast_fusion.1), channel_id=1, source_target_pairs={{0,16},{1,17},{2,18},{3,19},{4,20},{5,21},{6,22},{7,23},{8,24},{9,... | collective-permute-start | bytes 196616 | tf_op jit(solution)/shard_map/ppermute | solution.py:185
  11.2 8.1 %collective-permute-start.3 = (f32[2,16,2,4,128]{4,1,3,2,0:T(8,128)S(1)}, f32[2,16,2,4,128]{4,1,3,2,0:T(8,128)S(1)}, u32[]{:S(2)}, u32[]{:S(2)}) collective-permute-start(f32[2,16,2,4,128]{4,1,3,2,0:T(8,128)S(1)} %maximum_bitcast_fusion), channel_id=1, source_target_pairs={{0,8},{1,9},{2,10},{3,11},{4,12},{5,13},{6,14},{7,15},{8,0},{9,1},... | collective-permute-start | bytes 393224 | tf_op jit(solution)/shard_map/ppermute | solution.py:185
  19.3 7.7 %collective-permute-start.4 = (f32[2,16,4,4,128]{4,1,3,2,0:T(8,128)S(1)}, f32[2,16,4,4,128]{4,1,3,2,0:T(8,128)S(1)}, u32[]{:S(2)}, u32[]{:S(2)}) collective-permute-start(f32[2,16,4,4,128]{4,1,3,2,0:T(8,128)S(1)} %bitcast.100), channel_id=1, source_target_pairs={{0,4},{1,5},{2,6},{3,7},{4,0},{5,1},{6,2},{7,3},{8,12},{9,13},{10,... | collective-permute-start | bytes 786440 | tf_op jit(solution)/shard_map/ppermute | solution.py:185
  27.2 12.5 %collective-permute-start.5 = (f32[2,16,8,4,128]{4,1,3,2,0:T(8,128)S(1)}, f32[2,16,8,4,128]{4,1,3,2,0:T(8,128)S(1)}, u32[]{:S(2)}, u32[]{:S(2)}) collective-permute-start(f32[2,16,8,4,128]{4,1,3,2,0:T(8,128)S(1)} %bitcast.97), channel_id=1, source_target_pairs={{0,2},{1,3},{2,0},{3,1},{4,6},{5,7},{6,4},{7,5},{8,10},{9,11},{10,... | collective-permute-start | bytes 1572872 | tf_op jit(solution)/shard_map/ppermute | solution.py:185
  39.8 1.2 copy-start.1
  39.9 1.5 %copy-start.2 = (f32[1,16,128,128]{3,2,1,0:T(8,128)S(1)}, f32[1,16,128,128]{3,2,1,0:T(8,128)}, u32[]{:S(2)}) copy-start(f32[1,16,128,128]{3,2,1,0:T(8,128)} %param.10) | copy-start | bytes 3145732
  40.0 2.9 %collective-permute-start.6 = (f32[2,16,16,4,128]{4,1,3,2,0:T(8,128)S(1)}, f32[2,16,16,4,128]{4,1,3,2,0:T(8,128)}, u32[]{:S(2)}, u32[]{:S(2)}) collective-permute-start(f32[2,16,16,4,128]{4,1,3,2,0:T(8,128)S(1)} %bitcast.94), channel_id=1, source_target_pairs={{0,1},{1,0},{2,3},{3,2},{4,5},{5,4},{6,7},{7,6},{8,9},{9,8},{10,11... | collective-permute-start | bytes 3145736 | tf_op jit(solution)/shard_map/ppermute | solution.py:185
  45.2 17.8 %copy-start = (f32[2,16,16,2,4,128]{5,4,3,2,1,0:T(4,128)}, f32[2,16,16,2,4,128]{5,4,3,2,1,0:T(4,128)S(1)}, u32[]{:S(2)}) copy-start(f32[2,16,16,2,4,128]{5,4,3,2,1,0:T(4,128)S(1)} %copy.43) | copy-start | bytes 6291460
  45.2 13.4 %copy-start.7 = (f32[1,4,256]{2,1,0:T(4,128)S(1)}, f32[1,4,256]{2,1,0:T(4,128)}, u32[]{:S(2)}) copy-start(f32[1,4,256]{2,1,0:T(4,128)} %param.17) | copy-start | bytes 12292
  45.2 13.4 %copy-start.8 = (s32[1,256]{1,0:T(1,128)S(1)}, s32[1,256]{1,0:T(1,128)}, u32[]{:S(2)}) copy-start(s32[1,256]{1,0:T(1,128)} %param.16) | copy-start | bytes 3076
  45.2 13.4 %copy-start.9 = (s32[1,256]{1,0:T(1,128)S(1)}, s32[1,256]{1,0:T(1,128)}, u32[]{:S(2)}) copy-start(s32[1,256]{1,0:T(1,128)} %param.15) | copy-start | bytes 3076
  46.1 14.2 %collective-permute-start.7 = (f32[2,4,128,128]{3,2,1,0:T(8,128)}, f32[2,4,128,128]{3,2,1,0:T(8,128)S(1)}, u32[]{:S(2)}, u32[]{:S(2)}) collective-permute-start(f32[2,4,128,128]{3,2,1,0:T(8,128)} %constant_dynamic-slice_fusion.2), channel_id=1, source_target_pairs={{0,32},{2,34},{4,36},{6,38},{8,40},{10,42},{12,44},{14,46},{16,48}... | collective-permute-start | bytes 1572872 | tf_op jit(solution)/shard_map/ppermute | solution.py:238
  52.2 17.2 %collective-permute-start = (f32[2,4,128,128]{3,2,1,0:T(8,128)}, f32[2,4,128,128]{3,2,1,0:T(8,128)S(1)}, u32[]{:S(2)}, u32[]{:S(2)}) collective-permute-start(f32[2,4,128,128]{3,2,1,0:T(8,128)} %get-tuple-element.15), channel_id=1, source_target_pairs={{0,32},{32,64},{64,96},{96,128},{128,160},{160,192},{192,224},{1,3... | collective-permute-start | bytes 1572872 | tf_op jit(solution)/shard_map/ppermute | solution.py:172
  55.6 20.3 %collective-permute-start.1 = (f32[2,4,128,128]{3,2,1,0:T(8,128)}, f32[2,4,128,128]{3,2,1,0:T(8,128)}, u32[]{:S(2)}, u32[]{:S(2)}) collective-permute-start(f32[2,4,128,128]{3,2,1,0:T(8,128)} %get-tuple-element.14), channel_id=1, source_target_pairs={{32,0},{64,32},{96,64},{128,96},{160,128},{192,160},{224,192},{33,... | collective-permute-start | bytes 1572872 | tf_op jit(solution)/shard_map/ppermute | solution.py:172
  60.3 15.5 %copy-start.3 = (f32[2,4,128,128]{3,2,1,0:T(8,128)}, f32[2,4,128,128]{3,2,1,0:T(8,128)S(1)}, u32[]{:S(2)}) copy-start(f32[2,4,128,128]{3,2,1,0:T(8,128)S(1)} %collective-permute-done.7.mat_lo) | copy-start | bytes 1572868
  60.3 15.5 %collective-permute-start.8 = (f32[2,4,128,128]{3,2,1,0:T(8,128)S(1)}, f32[2,4,128,128]{3,2,1,0:T(8,128)}, u32[]{:S(2)}, u32[]{:S(2)}) collective-permute-start(f32[2,4,128,128]{3,2,1,0:T(8,128)S(1)} %collective-permute-done.7.mat_lo), channel_id=1, source_target_pairs={{0,1},{1,0},{2,3},{3,2},{4,5},{5,4},{6,7},{7,6},{8,9},{9,8},{10,11... | collective-permute-start | bytes 1572872 | tf_op jit(solution)/shard_map/ppermute | solution.py:239
  69.3 6.5 %copy-start.4 = (f32[2,4,128,128]{3,2,1,0:T(8,128)}, f32[2,4,128,128]{3,2,1,0:T(8,128)S(1)}, u32[]{:S(2)}) copy-start(f32[2,4,128,128]{3,2,1,0:T(8,128)S(1)} %collective-permute-done.adj_lo) | copy-start | bytes 1572868
  92.8 30.2 %copy-start.5 = (f32[16,4,128]{2,1,0:T(4,128)S(1)}, f32[16,4,128]{2,1,0:T(4,128)}, u32[]{:S(2)}) copy-start(f32[16,4,128]{2,1,0:T(4,128)} %param.12) | copy-start | bytes 98308
  92.8 30.2 %copy-start.6 = (f32[16,4,128]{2,1,0:T(4,128)S(1)}, f32[16,4,128]{2,1,0:T(4,128)}, u32[]{:S(2)}) copy-start(f32[16,4,128]{2,1,0:T(4,128)} %param.13) | copy-start | bytes 98308
  92.8 2.0 %collective-permute-start.9 = (f32[16,2,2,2,2,4,128]{6,0,5,4,3,2,1:T(8,128)S(1)}, f32[16,2,2,2,2,4,128]{6,0,5,4,3,2,1:T(8,128)S(1)}, u32[]{:S(2)}, u32[]{:S(2)}) collective-permute-start(f32[16,2,2,2,2,4,128]{6,0,5,4,3,2,1:T(8,128)S(1)} %bitcast.102), channel_id=1, source_target_pairs={{0,1},{1,0},{2,3},{3,2},{4,5},{5,4},{6,7},{7,6},{8,9},{9,8},{10,11... | collective-permute-start | bytes 1572872 | tf_op jit(solution)/shard_map/ppermute | solution.py:211
  95.2 8.4 %collective-permute-start.10 = (f32[16,2,2,2,4,128]{5,0,4,3,2,1:T(8,128)S(1)}, f32[16,2,2,2,4,128]{5,0,4,3,2,1:T(8,128)S(1)}, u32[]{:S(2)}, u32[]{:S(2)}) collective-permute-start(f32[16,2,2,2,4,128]{5,0,4,3,2,1:T(8,128)S(1)} %dynamic-slice_bitcast_fusion), channel_id=1, source_target_pairs={{0,2},{1,3},{2,0},{3,1},{4,6},{5,7},{6,4},{7,5},{8,10},{9,11},{10,... | collective-permute-start | bytes 786440 | tf_op jit(solution)/shard_map/ppermute | solution.py:211
  103.7 5.1 %collective-permute-start.11 = (f32[16,2,2,4,128]{4,0,3,2,1:T(8,128)S(1)}, f32[16,2,2,4,128]{4,0,3,2,1:T(8,128)S(1)}, u32[]{:S(2)}, u32[]{:S(2)}) collective-permute-start(f32[16,2,2,4,128]{4,0,3,2,1:T(8,128)S(1)} %dynamic-slice_bitcast_fusion.1), channel_id=1, source_target_pairs={{0,4},{1,5},{2,6},{3,7},{4,0},{5,1},{6,2},{7,3},{8,12},{9,13},{10,... | collective-permute-start | bytes 393224 | tf_op jit(solution)/shard_map/ppermute | solution.py:211
  108.8 6.0 %collective-permute-start.12 = (f32[16,2,4,128]{3,0,2,1:T(8,128)S(1)}, f32[16,2,4,128]{3,0,2,1:T(8,128)S(1)}, u32[]{:S(2)}, u32[]{:S(2)}) collective-permute-start(f32[16,2,4,128]{3,0,2,1:T(8,128)S(1)} %dynamic-slice_bitcast_fusion.2), channel_id=1, source_target_pairs={{0,8},{1,9},{2,10},{3,11},{4,12},{5,13},{6,14},{7,15},{8,0},{9,1},... | collective-permute-start | bytes 196616 | tf_op jit(solution)/shard_map/ppermute | solution.py:211
  114.8 8.2 %collective-permute-start.13 = (f32[16,4,128]{2,0,1:T(8,128)S(1)}, f32[16,4,128]{2,0,1:T(8,128)S(1)}, u32[]{:S(2)}, u32[]{:S(2)}) collective-permute-start(f32[16,4,128]{2,0,1:T(8,128)S(1)} %dynamic-slice_bitcast_fusion.3), channel_id=1, source_target_pairs={{0,16},{1,17},{2,18},{3,19},{4,20},{5,21},{6,22},{7,23},{8,24},{9,... | collective-permute-start | bytes 98312 | tf_op jit(solution)/shard_map/ppermute | solution.py:211

commit v8 on v7

--- a/solution.py
+++ b/solution.py
@@ -121,16 +121,6 @@
 
         return f
 
-    def wr_inner(ref, out):
-        def f(e, v):
-            ref[e] = v
-
-            @pl.when(jnp.logical_and(e >= HALO, e < ext - HALO))
-            def _():
-                out[e - HALO] = v
-
-        return f
-
     def wr_out(out):
         def f(e, v):
             out[e - HALO] = v
@@ -139,8 +129,11 @@
 
     one_step(0, rd(curb), rd(oldb), wr(pbuf), 1, ext - 1)
     one_step(1, rd(pbuf), rd(curb), wr(qbuf), 2, ext - 2)
-    one_step(2, rd(qbuf), rd(pbuf), wr_inner(pbuf, prev_ref), 3, ext - 3)
+    one_step(2, rd(qbuf), rd(pbuf), wr(pbuf), 3, ext - 3)
+    put_prev = pltpu.make_async_copy(pbuf.at[inner_at], prev_ref, sems.at[12])
+    put_prev.start()
     one_step(3, rd(pbuf), rd(qbuf), wr_out(now_ref), HALO, ext - HALO)
+    put_prev.wait()
 
 
 def run_steps(count, adj_now, adj_prev, adj_lo, adj_hi, mat, mat_lo, mat_hi, snaps, src):
@@ -154,7 +147,8 @@
         stencil_kernel,
         out_shape=out_shape,
         in_specs=[pl.BlockSpec(memory_space=pltpu.SMEM)] + [pl.BlockSpec(memory_space=pl.ANY)] * 9,
-        out_specs=[pl.BlockSpec(memory_space=vmem)] * 3,
+        out_specs=[pl.BlockSpec(memory_space=vmem), pl.BlockSpec(memory_space=pl.ANY),
+                   pl.BlockSpec(memory_space=vmem)],
         scratch_shapes=[field, field, pltpu.VMEM((2, ext, nx, ny), jnp.float32),
                         pltpu.VMEM(snaps.shape, snaps.dtype), pltpu.VMEM(src.shape, jnp.float32)]
         + [field] * 8 + [pltpu.SemaphoreType.DMA((12 + steps,))],

time: 124 us -> 124 us (level)
  no operation moved by 1% of the time
where the time goes in v8:
time: 124 us; the launch traced here: 123 us
  waiting for transfers between devices  65.7 us (53%)
  starting transfers between devices  28.3 us (23%)
  Pallas kernels  15 us (12%)
  local copies, waits for them, and re-layouts  6.56 us (5%)
  other arithmetic  4.46 us (4%)
  between operations  1.69 us (1%)
  matrix products  1.61 us (1%)
    ppermute x5, waiting for transfers between devices, gather_rows(): got = lax.ppermute(pieces, axis, pairs)  27.4 us
    ppermute x5, waiting for transfers between devices, scatter_rows(): got = lax.ppermute(send, axis, pairs)  24.3 us
    pallas_call x1, Pallas kernels, run_steps(): pl.pallas_call(stencil_kernel, out_shape=out_shape, in_specs=[pl.BlockSpe...  15 us
    ppermute x2, waiting for transfers between devices, halo_of(): return (lax.ppermute(last, axis, up), lax.ppermute(first, axis, down))  12.8 us
    ppermute x5, starting transfers between devices, gather_rows(): got = lax.ppermute(pieces, axis, pairs)  12.1 us
    ppermute x2, starting transfers between devices, halo_of(): return (lax.ppermute(last, axis, up), lax.ppermute(first, axis, down))  5.83 us
    ppermute x5, starting transfers between devices, scatter_rows(): got = lax.ppermute(send, axis, pairs)  5.33 us
    ppermute x1, starting transfers between devices, split_halo(): got = lax.ppermute(sent, ('depth', 'shots'), pairs)  5 us
  transfers between devices with their start and end apart: 14, of which 13 were waited for; matrix products, arithmetic and copies ran while one was open for 3% of the time, Pallas kernels for 0%

profile of v8, /device:TPU:6, one launch (start us, length us, event | category | flops | bytes accessed | tf_op | source)
XLA Modules:
  0.0 123.4 jit_solution(17098419259360023237)
XLA Ops:
  0.6 0.8 fusion.20
  1.4 7.3 %collective-permute-start.2 = (f32[2,16,1,4,128]{4,1,3,0,2:T(8,128)S(1)}, f32[2,16,1,4,128]{4,1,3,0,2:T(8,128)S(1)}, u32[]{:S(2)}, u32[]{:S(2)}) collective-permute-start(f32[2,16,1,4,128]{4,1,3,0,2:T(8,128)S(1)} %maximum_bitcast_fusion.1), channel_id=1, source_target_pairs={{0,16},{1,17},{2,18},{3,19},{4,20},{5,21},{6,22},{7,23},{8,24},{9,... | collective-permute-start | bytes 196616 | tf_op jit(solution)/shard_map/ppermute | solution.py:179
  8.7 2.4 %collective-permute-done.2 = f32[2,16,1,4,128]{4,1,3,0,2:T(8,128)S(1)} collective-permute-done((f32[2,16,1,4,128]{4,1,3,0,2:T(8,128)S(1)}, f32[2,16,1,4,128]{4,1,3,0,2:T(8,128)S(1)}, u32[]{:S(2)}, u32[]{:S(2)}) %collective-permute-start.2) | collective-permute-done | bytes 65568 | tf_op jit(solution)/shard_map/ppermute | solution.py:179
  11.2 3.0 %collective-permute-start.3 = (f32[2,16,2,4,128]{4,1,3,2,0:T(8,128)S(1)}, f32[2,16,2,4,128]{4,1,3,2,0:T(8,128)S(1)}, u32[]{:S(2)}, u32[]{:S(2)}) collective-permute-start(f32[2,16,2,4,128]{4,1,3,2,0:T(8,128)S(1)} %maximum_bitcast_fusion), channel_id=1, source_target_pairs={{0,8},{1,9},{2,10},{3,11},{4,12},{5,13},{6,14},{7,15},{8,0},{9,1},... | collective-permute-start | bytes 393224 | tf_op jit(solution)/shard_map/ppermute | solution.py:179
  14.2 5.1 %collective-permute-done.3 = f32[2,16,2,4,128]{4,1,3,2,0:T(8,128)S(1)} collective-permute-done((f32[2,16,2,4,128]{4,1,3,2,0:T(8,128)S(1)}, f32[2,16,2,4,128]{4,1,3,2,0:T(8,128)S(1)}, u32[]{:S(2)}, u32[]{:S(2)}) %collective-permute-start.3) | collective-permute-done | bytes 131104 | tf_op jit(solution)/shard_map/ppermute | solution.py:179
  19.3 0.1 collective-permute-start.4
  19.4 7.6 %collective-permute-done.4 = f32[2,16,4,4,128]{4,1,3,2,0:T(8,128)S(1)} collective-permute-done((f32[2,16,4,4,128]{4,1,3,2,0:T(8,128)S(1)}, f32[2,16,4,4,128]{4,1,3,2,0:T(8,128)S(1)}, u32[]{:S(2)}, u32[]{:S(2)}) %collective-permute-start.4) | collective-permute-done | bytes 262176 | tf_op jit(solution)/shard_map/ppermute | solution.py:179
  27.2 1.7 %collective-permute-start.5 = (f32[2,16,8,4,128]{4,1,3,2,0:T(8,128)S(1)}, f32[2,16,8,4,128]{4,1,3,2,0:T(8,128)S(1)}, u32[]{:S(2)}, u32[]{:S(2)}) collective-permute-start(f32[2,16,8,4,128]{4,1,3,2,0:T(8,128)S(1)} %bitcast.97), channel_id=1, source_target_pairs={{0,2},{1,3},{2,0},{3,1},{4,6},{5,7},{6,4},{7,5},{8,10},{9,11},{10,... | collective-permute-start | bytes 1572872 | tf_op jit(solution)/shard_map/ppermute | solution.py:179
  28.8 10.8 %collective-permute-done.5 = f32[2,16,8,4,128]{4,1,3,2,0:T(8,128)S(1)} collective-permute-done((f32[2,16,8,4,128]{4,1,3,2,0:T(8,128)S(1)}, f32[2,16,8,4,128]{4,1,3,2,0:T(8,128)S(1)}, u32[]{:S(2)}, u32[]{:S(2)}) %collective-permute-start.5) | collective-permute-done | bytes 524320 | tf_op jit(solution)/shard_map/ppermute | solution.py:179
  39.6 0.1 select_bitcast_fusion.3
  39.8 0.0 copy-start.1
  39.8 0.1 pad_maximum_fusion.1
  39.9 0.0 copy-start.2
  39.9 0.1 copy.42
  40.0 0.1 collective-permute-start.6
  40.1 0.9 copy-done.1
  41.0 0.1 constant_dynamic-update-slice_fusion.1
  41.1 0.3 copy-done.2
  41.3 0.1 constant_dynamic-update-slice_fusion
  41.4 1.4 %collective-permute-done.6 = f32[2,16,16,4,128]{4,1,3,2,0:T(8,128)} collective-permute-done((f32[2,16,16,4,128]{4,1,3,2,0:T(8,128)S(1)}, f32[2,16,16,4,128]{4,1,3,2,0:T(8,128)}, u32[]{:S(2)}, u32[]{:S(2)}) %collective-permute-start.6) | collective-permute-done | bytes 1048608 | tf_op jit(solution)/shard_map/ppermute | solution.py:179
  42.8 1.4 %select_bitcast_fusion.1 = (f32[2,16,16,1,4,128]{5,1,4,2,0,3:T(8,128)S(1)}, f32[2,16,16,1,4,128]{5,1,4,2,0,3:T(8,128)S(1)}) fusion(f32[2,16,16,4,128]{4,1,3,2,0:T(8,128)S(1)} %bitcast.95, f32[2,16,16,4,128]{4,1,3,2,0:T(8,128)} %collective-permute-done.6, pred[]{:T(512)S(6)} %eq.33), kind=kLoop, calls=%fused_computation.7 | loop fusion | flops 524288 | bytes 4194305 | tf_op jit(solution)/shard_map/stack | solution.py:183
  44.2 0.1 pad_maximum_fusion
  44.4 0.8 copy.43
  45.2 0.0 copy-start
  45.2 0.0 copy-start.7
  45.2 0.0 copy-start.8
  45.2 0.0 copy-start.9
  45.3 0.8 constant_dynamic-slice_fusion.2
  46.1 5.0 %collective-permute-start.7 = (f32[2,4,128,128]{3,2,1,0:T(8,128)}, f32[2,4,128,128]{3,2,1,0:T(8,128)S(1)}, u32[]{:S(2)}, u32[]{:S(2)}) collective-permute-start(f32[2,4,128,128]{3,2,1,0:T(8,128)} %constant_dynamic-slice_fusion.2), channel_id=1, source_target_pairs={{0,32},{2,34},{4,36},{6,38},{8,40},{10,42},{12,44},{14,46},{16,48}... | collective-permute-start | bytes 1572872 | tf_op jit(solution)/shard_map/ppermute | solution.py:232
  51.1 1.0 fusion.27
  52.2 3.4 %collective-permute-start = (f32[2,4,128,128]{3,2,1,0:T(8,128)}, f32[2,4,128,128]{3,2,1,0:T(8,128)S(1)}, u32[]{:S(2)}, u32[]{:S(2)}) collective-permute-start(f32[2,4,128,128]{3,2,1,0:T(8,128)} %get-tuple-element.15), channel_id=1, source_target_pairs={{0,32},{32,64},{64,96},{96,128},{128,160},{160,192},{192,224},{1,3... | collective-permute-start | bytes 1572872 | tf_op jit(solution)/shard_map/ppermute | solution.py:166
  55.6 2.4 %collective-permute-start.1 = (f32[2,4,128,128]{3,2,1,0:T(8,128)}, f32[2,4,128,128]{3,2,1,0:T(8,128)}, u32[]{:S(2)}, u32[]{:S(2)}) collective-permute-start(f32[2,4,128,128]{3,2,1,0:T(8,128)} %get-tuple-element.14), channel_id=1, source_target_pairs={{32,0},{64,32},{96,64},{128,96},{160,128},{192,160},{224,192},{33,... | collective-permute-start | bytes 1572872 | tf_op jit(solution)/shard_map/ppermute | solution.py:166
  58.7 0.0 copy-done.7
  58.7 0.0 copy-done.8
  58.7 0.0 copy-done.9
  58.7 0.4 convolution_bitcast_fusion
  59.1 1.2 collective-permute-done.7.mat_lo
  60.3 0.0 collective-permute-start.8
  60.3 0.7 pad_maximum_fusion.4.count_ref
  61.0 0.4 convolution_bitcast_fusion.1
  61.4 0.4 convolution_bitcast_fusion.2
  61.8 0.4 convolution_bitcast_fusion.3
  62.2 0.7 maximum_multiply_fusion.src_hbm
  63.0 0.0 copy-done
  63.0 6.4 %collective-permute-done.adj_lo = f32[2,4,128,128]{3,2,1,0:T(8,128)S(1)} collective-permute-done((f32[2,4,128,128]{3,2,1,0:T(8,128)}, f32[2,4,128,128]{3,2,1,0:T(8,128)S(1)}, u32[]{:S(2)}, u32[]{:S(2)}) %collective-permute-start) | collective-permute-done | bytes 524320 | tf_op jit(solution)/shard_map/ppermute | solution.py:166
  69.3 6.5 %collective-permute-done.1.adj_hi = f32[2,4,128,128]{3,2,1,0:T(8,128)} collective-permute-done((f32[2,4,128,128]{3,2,1,0:T(8,128)}, f32[2,4,128,128]{3,2,1,0:T(8,128)}, u32[]{:S(2)}, u32[]{:S(2)}) %collective-permute-start.1) | collective-permute-done | bytes 524320 | tf_op jit(solution)/shard_map/ppermute | solution.py:166
  75.8 0.0 collective-permute-done.8.mat_hi
  75.8 15.0 %shard_map.112 = (f32[16,128,128]{2,1,0:T(8,128)}, f32[16,128,128]{2,1,0:T(8,128)}, f32[16,128,128]{2,1,0:T(8,128)}) custom-call(f32[2]{0:T(128)} %pad_maximum_fusion.4.count_ref, f32[16,128,128]{2,1,0:T(8,128)} %bitcast.92, f32[16,128,128]{2,1,0:T(8,128)} %bitcast.93, f32[2,4,128,128]{3,2,1,0:T(8,128)} %copy-done.4, ...), custom_call_target="tpu_custom_call" | custom-call | tf_op jit(solution)/shard_map/pallas_call | solution.py:146
  90.9 1.4 %constant_dynamic-slice_fusion.1 = (f32[16,2,2,2,2,1,4,128]{7,6,5,4,3,2,1,0:T(4,128)S(1)}, f32[16,2,2,2,2,1,4,128]{7,6,5,4,3,2,1,0:T(4,128)S(1)}) fusion(f32[16,2,2,2,2,2,4,128]{7,6,5,4,3,2,1,0:T(4,128)} %bitcast.99, s32[]{:T(128)S(6)} %select_n.126, s32[]{:T(128)S(6)} %select_n.127), kind=kLoop, calls=%fused_computation.61 | loop fusion | bytes 2097160 | tf_op jit(solution)/shard_map/jit(dynamic_index_in_dim)/dynamic_slice | solution.py:202
  92.2 0.3 copy.56
  92.6 0.0 copy-start.5
  92.6 0.0 copy-start.6
  92.6 0.1 collective-permute-start.9
  92.7 1.9 %collective-permute-done.9 = f32[16,2,2,2,2,4,128]{6,0,5,4,3,2,1:T(8,128)S(1)} collective-permute-done((f32[16,2,2,2,2,4,128]{6,0,5,4,3,2,1:T(8,128)S(1)}, f32[16,2,2,2,2,4,128]{6,0,5,4,3,2,1:T(8,128)S(1)}, u32[]{:S(2)}, u32[]{:S(2)}) %collective-permute-start.9) | collective-permute-done | bytes 524320 | tf_op jit(solution)/shard_map/ppermute | solution.py:205
  94.6 0.3 bitcast_add_fusion
  94.9 0.6 collective-permute-start.10
  95.5 7.9 %collective-permute-done.10 = f32[16,2,2,2,4,128]{5,0,4,3,2,1:T(8,128)S(1)} collective-permute-done((f32[16,2,2,2,4,128]{5,0,4,3,2,1:T(8,128)S(1)}, f32[16,2,2,2,4,128]{5,0,4,3,2,1:T(8,128)S(1)}, u32[]{:S(2)}, u32[]{:S(2)}) %collective-permute-start.10) | collective-permute-done | bytes 262176 | tf_op jit(solution)/shard_map/ppermute | solution.py:205
  103.4 0.7 collective-permute-start.11
  104.1 4.4 %collective-permute-done.11 = f32[16,2,2,4,128]{4,0,3,2,1:T(8,128)S(1)} collective-permute-done((f32[16,2,2,4,128]{4,0,3,2,1:T(8,128)S(1)}, f32[16,2,2,4,128]{4,0,3,2,1:T(8,128)S(1)}, u32[]{:S(2)}, u32[]{:S(2)}) %collective-permute-start.11) | collective-permute-done | bytes 131104 | tf_op jit(solution)/shard_map/ppermute | solution.py:205
  108.5 0.1 collective-permute-start.12
  108.6 5.9 %collective-permute-done.12 = f32[16,2,4,128]{3,0,2,1:T(8,128)S(1)} collective-permute-done((f32[16,2,4,128]{3,0,2,1:T(8,128)S(1)}, f32[16,2,4,128]{3,0,2,1:T(8,128)S(1)}, u32[]{:S(2)}, u32[]{:S(2)}) %collective-permute-start.12) | collective-permute-done | bytes 65568 | tf_op jit(solution)/shard_map/ppermute | solution.py:205
  114.5 3.9 %collective-permute-start.13 = (f32[16,4,128]{2,0,1:T(8,128)S(1)}, f32[16,4,128]{2,0,1:T(8,128)S(1)}, u32[]{:S(2)}, u32[]{:S(2)}) collective-permute-start(f32[16,4,128]{2,0,1:T(8,128)S(1)} %dynamic-slice_bitcast_fusion.3), channel_id=1, source_target_pairs={{0,16},{1,17},{2,18},{3,19},{4,20},{5,21},{6,22},{7,23},{8,24},{9,... | collective-permute-start | bytes 98312 | tf_op jit(solution)/shard_map/ppermute | solution.py:205
  118.4 4.3 %collective-permute-done.13 = f32[16,4,128]{2,0,1:T(8,128)S(1)} collective-permute-done((f32[16,4,128]{2,0,1:T(8,128)S(1)}, f32[16,4,128]{2,0,1:T(8,128)S(1)}, u32[]{:S(2)}, u32[]{:S(2)}) %collective-permute-start.13) | collective-permute-done | bytes 32800 | tf_op jit(solution)/shard_map/ppermute | solution.py:205
  122.7 0.6 copy.48
  (23 shorter events, 0.3 us)
Async XLA Ops:
  1.4 9.7 %collective-permute-start.2 = (f32[2,16,1,4,128]{4,1,3,0,2:T(8,128)S(1)}, f32[2,16,1,4,128]{4,1,3,0,2:T(8,128)S(1)}, u32[]{:S(2)}, u32[]{:S(2)}) collective-permute-start(f32[2,16,1,4,128]{4,1,3,0,2:T(8,128)S(1)} %maximum_bitcast_fusion.1), channel_id=1, source_target_pairs={{0,16},{1,17},{2,18},{3,19},{4,20},{5,21},{6,22},{7,23},{8,24},{9,... | collective-permute-start | bytes 196616 | tf_op jit(solution)/shard_map/ppermute | solution.py:179
  11.2 8.1 %collective-permute-start.3 = (f32[2,16,2,4,128]{4,1,3,2,0:T(8,128)S(1)}, f32[2,16,2,4,128]{4,1,3,2,0:T(8,128)S(1)}, u32[]{:S(2)}, u32[]{:S(2)}) collective-permute-start(f32[2,16,2,4,128]{4,1,3,2,0:T(8,128)S(1)} %maximum_bitcast_fusion), channel_id=1, source_target_pairs={{0,8},{1,9},{2,10},{3,11},{4,12},{5,13},{6,14},{7,15},{8,0},{9,1},... | collective-permute-start | bytes 393224 | tf_op jit(solution)/shard_map/ppermute | solution.py:179
  19.3 7.7 %collective-permute-start.4 = (f32[2,16,4,4,128]{4,1,3,2,0:T(8,128)S(1)}, f32[2,16,4,4,128]{4,1,3,2,0:T(8,128)S(1)}, u32[]{:S(2)}, u32[]{:S(2)}) collective-permute-start(f32[2,16,4,4,128]{4,1,3,2,0:T(8,128)S(1)} %bitcast.100), channel_id=1, source_target_pairs={{0,4},{1,5},{2,6},{3,7},{4,0},{5,1},{6,2},{7,3},{8,12},{9,13},{10,... | collective-permute-start | bytes 786440 | tf_op jit(solution)/shard_map/ppermute | solution.py:179
  27.2 12.5 %collective-permute-start.5 = (f32[2,16,8,4,128]{4,1,3,2,0:T(8,128)S(1)}, f32[2,16,8,4,128]{4,1,3,2,0:T(8,128)S(1)}, u32[]{:S(2)}, u32[]{:S(2)}) collective-permute-start(f32[2,16,8,4,128]{4,1,3,2,0:T(8,128)S(1)} %bitcast.97), channel_id=1, source_target_pairs={{0,2},{1,3},{2,0},{3,1},{4,6},{5,7},{6,4},{7,5},{8,10},{9,11},{10,... | collective-permute-start | bytes 1572872 | tf_op jit(solution)/shard_map/ppermute | solution.py:179
  39.8 1.2 copy-start.1
  39.9 1.5 %copy-start.2 = (f32[1,16,128,128]{3,2,1,0:T(8,128)S(1)}, f32[1,16,128,128]{3,2,1,0:T(8,128)}, u32[]{:S(2)}) copy-start(f32[1,16,128,128]{3,2,1,0:T(8,128)} %param.10) | copy-start | bytes 3145732
  40.0 2.9 %collective-permute-start.6 = (f32[2,16,16,4,128]{4,1,3,2,0:T(8,128)S(1)}, f32[2,16,16,4,128]{4,1,3,2,0:T(8,128)}, u32[]{:S(2)}, u32[]{:S(2)}) collective-permute-start(f32[2,16,16,4,128]{4,1,3,2,0:T(8,128)S(1)} %bitcast.94), channel_id=1, source_target_pairs={{0,1},{1,0},{2,3},{3,2},{4,5},{5,4},{6,7},{7,6},{8,9},{9,8},{10,11... | collective-permute-start | bytes 3145736 | tf_op jit(solution)/shard_map/ppermute | solution.py:179
  45.2 17.8 %copy-start = (f32[2,16,16,2,4,128]{5,4,3,2,1,0:T(4,128)}, f32[2,16,16,2,4,128]{5,4,3,2,1,0:T(4,128)S(1)}, u32[]{:S(2)}) copy-start(f32[2,16,16,2,4,128]{5,4,3,2,1,0:T(4,128)S(1)} %copy.43) | copy-start | bytes 6291460
  45.2 13.4 %copy-start.7 = (f32[1,4,256]{2,1,0:T(4,128)S(1)}, f32[1,4,256]{2,1,0:T(4,128)}, u32[]{:S(2)}) copy-start(f32[1,4,256]{2,1,0:T(4,128)} %param.17) | copy-start | bytes 12292
  45.2 13.4 %copy-start.8 = (s32[1,256]{1,0:T(1,128)S(1)}, s32[1,256]{1,0:T(1,128)}, u32[]{:S(2)}) copy-start(s32[1,256]{1,0:T(1,128)} %param.16) | copy-start | bytes 3076
  45.2 13.4 %copy-start.9 = (s32[1,256]{1,0:T(1,128)S(1)}, s32[1,256]{1,0:T(1,128)}, u32[]{:S(2)}) copy-start(s32[1,256]{1,0:T(1,128)} %param.15) | copy-start | bytes 3076
  46.1 14.2 %collective-permute-start.7 = (f32[2,4,128,128]{3,2,1,0:T(8,128)}, f32[2,4,128,128]{3,2,1,0:T(8,128)S(1)}, u32[]{:S(2)}, u32[]{:S(2)}) collective-permute-start(f32[2,4,128,128]{3,2,1,0:T(8,128)} %constant_dynamic-slice_fusion.2), channel_id=1, source_target_pairs={{0,32},{2,34},{4,36},{6,38},{8,40},{10,42},{12,44},{14,46},{16,48}... | collective-permute-start | bytes 1572872 | tf_op jit(solution)/shard_map/ppermute | solution.py:232
  52.2 17.2 %collective-permute-start = (f32[2,4,128,128]{3,2,1,0:T(8,128)}, f32[2,4,128,128]{3,2,1,0:T(8,128)S(1)}, u32[]{:S(2)}, u32[]{:S(2)}) collective-permute-start(f32[2,4,128,128]{3,2,1,0:T(8,128)} %get-tuple-element.15), channel_id=1, source_target_pairs={{0,32},{32,64},{64,96},{96,128},{128,160},{160,192},{192,224},{1,3... | collective-permute-start | bytes 1572872 | tf_op jit(solution)/shard_map/ppermute | solution.py:166
  55.6 20.3 %collective-permute-start.1 = (f32[2,4,128,128]{3,2,1,0:T(8,128)}, f32[2,4,128,128]{3,2,1,0:T(8,128)}, u32[]{:S(2)}, u32[]{:S(2)}) collective-permute-start(f32[2,4,128,128]{3,2,1,0:T(8,128)} %get-tuple-element.14), channel_id=1, source_target_pairs={{32,0},{64,32},{96,64},{128,96},{160,128},{192,160},{224,192},{33,... | collective-permute-start | bytes 1572872 | tf_op jit(solution)/shard_map/ppermute | solution.py:166
  60.3 15.5 %copy-start.3 = (f32[2,4,128,128]{3,2,1,0:T(8,128)}, f32[2,4,128,128]{3,2,1,0:T(8,128)S(1)}, u32[]{:S(2)}) copy-start(f32[2,4,128,128]{3,2,1,0:T(8,128)S(1)} %collective-permute-done.7.mat_lo) | copy-start | bytes 1572868
  60.3 15.5 %collective-permute-start.8 = (f32[2,4,128,128]{3,2,1,0:T(8,128)S(1)}, f32[2,4,128,128]{3,2,1,0:T(8,128)}, u32[]{:S(2)}, u32[]{:S(2)}) collective-permute-start(f32[2,4,128,128]{3,2,1,0:T(8,128)S(1)} %collective-permute-done.7.mat_lo), channel_id=1, source_target_pairs={{0,1},{1,0},{2,3},{3,2},{4,5},{5,4},{6,7},{7,6},{8,9},{9,8},{10,11... | collective-permute-start | bytes 1572872 | tf_op jit(solution)/shard_map/ppermute | solution.py:233
  69.3 6.5 %copy-start.4 = (f32[2,4,128,128]{3,2,1,0:T(8,128)}, f32[2,4,128,128]{3,2,1,0:T(8,128)S(1)}, u32[]{:S(2)}) copy-start(f32[2,4,128,128]{3,2,1,0:T(8,128)S(1)} %collective-permute-done.adj_lo) | copy-start | bytes 1572868
  92.6 30.2 %copy-start.5 = (f32[16,4,128]{2,1,0:T(4,128)S(1)}, f32[16,4,128]{2,1,0:T(4,128)}, u32[]{:S(2)}) copy-start(f32[16,4,128]{2,1,0:T(4,128)} %param.12) | copy-start | bytes 98308
  92.6 30.2 %copy-start.6 = (f32[16,4,128]{2,1,0:T(4,128)S(1)}, f32[16,4,128]{2,1,0:T(4,128)}, u32[]{:S(2)}) copy-start(f32[16,4,128]{2,1,0:T(4,128)} %param.13) | copy-start | bytes 98308
  92.6 2.0 %collective-permute-start.9 = (f32[16,2,2,2,2,4,128]{6,0,5,4,3,2,1:T(8,128)S(1)}, f32[16,2,2,2,2,4,128]{6,0,5,4,3,2,1:T(8,128)S(1)}, u32[]{:S(2)}, u32[]{:S(2)}) collective-permute-start(f32[16,2,2,2,2,4,128]{6,0,5,4,3,2,1:T(8,128)S(1)} %bitcast.102), channel_id=1, source_target_pairs={{0,1},{1,0},{2,3},{3,2},{4,5},{5,4},{6,7},{7,6},{8,9},{9,8},{10,11... | collective-permute-start | bytes 1572872 | tf_op jit(solution)/shard_map/ppermute | solution.py:205
  94.9 8.4 %collective-permute-start.10 = (f32[16,2,2,2,4,128]{5,0,4,3,2,1:T(8,128)S(1)}, f32[16,2,2,2,4,128]{5,0,4,3,2,1:T(8,128)S(1)}, u32[]{:S(2)}, u32[]{:S(2)}) collective-permute-start(f32[16,2,2,2,4,128]{5,0,4,3,2,1:T(8,128)S(1)} %dynamic-slice_bitcast_fusion), channel_id=1, source_target_pairs={{0,2},{1,3},{2,0},{3,1},{4,6},{5,7},{6,4},{7,5},{8,10},{9,11},{10,... | collective-permute-start | bytes 786440 | tf_op jit(solution)/shard_map/ppermute | solution.py:205
  103.4 5.1 %collective-permute-start.11 = (f32[16,2,2,4,128]{4,0,3,2,1:T(8,128)S(1)}, f32[16,2,2,4,128]{4,0,3,2,1:T(8,128)S(1)}, u32[]{:S(2)}, u32[]{:S(2)}) collective-permute-start(f32[16,2,2,4,128]{4,0,3,2,1:T(8,128)S(1)} %dynamic-slice_bitcast_fusion.1), channel_id=1, source_target_pairs={{0,4},{1,5},{2,6},{3,7},{4,0},{5,1},{6,2},{7,3},{8,12},{9,13},{10,... | collective-permute-start | bytes 393224 | tf_op jit(solution)/shard_map/ppermute | solution.py:205
  108.5 6.0 %collective-permute-start.12 = (f32[16,2,4,128]{3,0,2,1:T(8,128)S(1)}, f32[16,2,4,128]{3,0,2,1:T(8,128)S(1)}, u32[]{:S(2)}, u32[]{:S(2)}) collective-permute-start(f32[16,2,4,128]{3,0,2,1:T(8,128)S(1)} %dynamic-slice_bitcast_fusion.2), channel_id=1, source_target_pairs={{0,8},{1,9},{2,10},{3,11},{4,12},{5,13},{6,14},{7,15},{8,0},{9,1},... | collective-permute-start | bytes 196616 | tf_op jit(solution)/shard_map/ppermute | solution.py:205
  114.5 8.2 %collective-permute-start.13 = (f32[16,4,128]{2,0,1:T(8,128)S(1)}, f32[16,4,128]{2,0,1:T(8,128)S(1)}, u32[]{:S(2)}, u32[]{:S(2)}) collective-permute-start(f32[16,4,128]{2,0,1:T(8,128)S(1)} %dynamic-slice_bitcast_fusion.3), channel_id=1, source_target_pairs={{0,16},{1,17},{2,18},{3,19},{4,20},{5,21},{6,22},{7,23},{8,24},{9,... | collective-permute-start | bytes 98312 | tf_op jit(solution)/shard_map/ppermute | solution.py:205

commit v9 on v8

--- a/solution.py
+++ b/solution.py
@@ -40,20 +40,32 @@
 
     inner_at, lo_at, hi_at = pl.ds(HALO, planes), pl.ds(0, HALO), pl.ds(HALO + planes, HALO)
     need_mat = [fetch(mat_hbm, matb.at[:, inner_at])]
-    own = pltpu.make_async_copy(mat_lo, matb.at[:, lo_at], sems.at[10 + steps])
-    swapped = pltpu.make_async_copy(mat_hi, matb.at[:, hi_at], sems.at[11 + steps])
+
+    def place(below, above):
+        return [
+            pltpu.make_async_copy(below.at[pl.ds(0, HALO)], matb.at[1, pl.ds(0, HALO)], sems.at[14]),
+            pltpu.make_async_copy(below.at[pl.ds(HALO, HALO - 1)], matb.at[0, pl.ds(1, HALO - 1)],
+                                  sems.at[15]),
+            pltpu.make_async_copy(above.at[pl.ds(0, HALO)], matb.at[1, pl.ds(HALO + planes, HALO)],
+                                  sems.at[16]),
+            pltpu.make_async_copy(above.at[pl.ds(HALO, HALO - 1)],
+                                  matb.at[0, pl.ds(HALO + planes, HALO - 1)], sems.at[17]),
+        ]
+
+    own = place(mat_lo, mat_hi)
+    swapped = place(mat_hi, mat_lo)
 
     @pl.when(count_ref[1] == 0.0)
     def _():
-        own.start()
-        swapped.start()
+        for c in own:
+            c.start()
 
     @pl.when(count_ref[1] != 0.0)
     def _():
-        pltpu.make_async_copy(mat_lo, matb.at[:, hi_at], sems.at[11 + steps]).start()
-        pltpu.make_async_copy(mat_hi, matb.at[:, lo_at], sems.at[10 + steps]).start()
-
-    need_mat += [own, swapped]
+        for c in swapped:
+            c.start()
+
+    need_mat += own
     need_adj = [fetch(now_hbm, curb.at[inner_at]), fetch(adj_lo.at[0], curb.at[lo_at]),
                 fetch(adj_hi.at[0], curb.at[hi_at]), fetch(prev_hbm, oldb.at[inner_at]),
                 fetch(adj_lo.at[1], oldb.at[lo_at]), fetch(adj_hi.at[1], oldb.at[hi_at]),
@@ -151,7 +163,7 @@
                    pl.BlockSpec(memory_space=vmem)],
         scratch_shapes=[field, field, pltpu.VMEM((2, ext, nx, ny), jnp.float32),
                         pltpu.VMEM(snaps.shape, snaps.dtype), pltpu.VMEM(src.shape, jnp.float32)]
-        + [field] * 8 + [pltpu.SemaphoreType.DMA((12 + steps,))],
+        + [field] * 8 + [pltpu.SemaphoreType.DMA((14 + steps,))],
         compiler_params=pltpu.CompilerParams(vmem_limit_bytes=56 * 1024 * 1024),
         interpret=INTERPRET,
     )(count, adj_now, adj_prev, adj_lo, adj_hi, mat, mat_lo, mat_hi, snaps, src)
@@ -221,8 +233,9 @@
     depth, shots = lax.axis_size("depth"), lax.axis_size("shots")
     core = lax.axis_index("shots") % 2
     length = shard.shape[1]
-    start = jnp.where(core == 0, length - width, 0)
-    sent = lax.dynamic_slice_in_dim(shard, start, width, axis=1)
+    buoy = lax.dynamic_slice_in_dim(shard[1], jnp.where(core == 0, length - width, 0), width, 0)
+    kappa = lax.dynamic_slice_in_dim(shard[0], jnp.where(core == 0, length - width + 1, 0), width - 1, 0)
+    sent = jnp.concatenate([buoy, kappa])
     pairs = []
     for d in range(depth):
         for s in range(shots):

time: 124 us -> 124 us (level)
  the two profiles are of different devices: /device:TPU:6 before, /device:TPU:24 now
where the time goes in v9:
time: 124 us; the launch traced here: 121 us
  waiting for transfers between devices  60.9 us (49%)
  starting transfers between devices  28.7 us (23%)
  Pallas kernels  15 us (12%)
  local copies, waits for them, and re-layouts  8.74 us (7%)
  other arithmetic  4.74 us (4%)
  between operations  1.75 us (1%)
  matrix products  1.61 us (1%)
    ppermute x5, waiting for transfers between devices, gather_rows(): got = lax.ppermute(pieces, axis, pairs)  26.8 us
    ppermute x5, waiting for transfers between devices, scatter_rows(): got = lax.ppermute(send, axis, pairs)  24 us
    pallas_call x1, Pallas kernels, run_steps(): pl.pallas_call(stencil_kernel, out_shape=out_shape, in_specs=[pl.BlockSpe...  15 us
    ppermute x5, starting transfers between devices, gather_rows(): got = lax.ppermute(pieces, axis, pairs)  11.3 us
    ppermute x1, waiting for transfers between devices, split_halo(): got = lax.ppermute(sent, ('depth', 'shots'), pairs)  10.1 us
    ppermute x2, starting transfers between devices, halo_of(): return (lax.ppermute(last, axis, up), lax.ppermute(first, axis, down))  9.45 us
    ppermute x5, starting transfers between devices, scatter_rows(): got = lax.ppermute(send, axis, pairs)  6.03 us
    unnamed x20, local copies, waits for them, and re-layouts  2.69 us
  transfers between devices with their start and end apart: 14, of which 10 were waited for; matrix products, arithmetic and copies ran while one was open for 8% of the time, Pallas kernels for 0%

profile of v9, /device:TPU:24, one launch (start us, length us, event | category | flops | bytes accessed | tf_op | source)
XLA Modules:
  0.0 121.4 jit_solution(4112925591473109196)
XLA Ops:
  0.6 0.8 fusion.22
  1.4 7.3 %collective-permute-start.2 = (f32[2,16,1,4,128]{4,1,3,0,2:T(8,128)S(1)}, f32[2,16,1,4,128]{4,1,3,0,2:T(8,128)S(1)}, u32[]{:S(2)}, u32[]{:S(2)}) collective-permute-start(f32[2,16,1,4,128]{4,1,3,0,2:T(8,128)S(1)} %maximum_bitcast_fusion.1), channel_id=1, source_target_pairs={{0,16},{1,17},{2,18},{3,19},{4,20},{5,21},{6,22},{7,23},{8,24},{9,... | collective-permute-start | bytes 196616 | tf_op jit(solution)/shard_map/ppermute | solution.py:191
  8.7 2.4 %collective-permute-done.2 = f32[2,16,1,4,128]{4,1,3,0,2:T(8,128)S(1)} collective-permute-done((f32[2,16,1,4,128]{4,1,3,0,2:T(8,128)S(1)}, f32[2,16,1,4,128]{4,1,3,0,2:T(8,128)S(1)}, u32[]{:S(2)}, u32[]{:S(2)}) %collective-permute-start.2) | collective-permute-done | bytes 65568 | tf_op jit(solution)/shard_map/ppermute | solution.py:191
  11.2 3.0 %collective-permute-start.3 = (f32[2,16,2,4,128]{4,1,3,2,0:T(8,128)S(1)}, f32[2,16,2,4,128]{4,1,3,2,0:T(8,128)S(1)}, u32[]{:S(2)}, u32[]{:S(2)}) collective-permute-start(f32[2,16,2,4,128]{4,1,3,2,0:T(8,128)S(1)} %maximum_bitcast_fusion), channel_id=1, source_target_pairs={{0,8},{1,9},{2,10},{3,11},{4,12},{5,13},{6,14},{7,15},{8,0},{9,1},... | collective-permute-start | bytes 393224 | tf_op jit(solution)/shard_map/ppermute | solution.py:191
  14.2 5.1 %collective-permute-done.3 = f32[2,16,2,4,128]{4,1,3,2,0:T(8,128)S(1)} collective-permute-done((f32[2,16,2,4,128]{4,1,3,2,0:T(8,128)S(1)}, f32[2,16,2,4,128]{4,1,3,2,0:T(8,128)S(1)}, u32[]{:S(2)}, u32[]{:S(2)}) %collective-permute-start.3) | collective-permute-done | bytes 131104 | tf_op jit(solution)/shard_map/ppermute | solution.py:191
  19.3 0.1 collective-permute-start.4
  19.4 7.6 %collective-permute-done.4 = f32[2,16,4,4,128]{4,1,3,2,0:T(8,128)S(1)} collective-permute-done((f32[2,16,4,4,128]{4,1,3,2,0:T(8,128)S(1)}, f32[2,16,4,4,128]{4,1,3,2,0:T(8,128)S(1)}, u32[]{:S(2)}, u32[]{:S(2)}) %collective-permute-start.4) | collective-permute-done | bytes 262176 | tf_op jit(solution)/shard_map/ppermute | solution.py:191
  27.2 0.8 collective-permute-start.5
  28.0 11.7 %collective-permute-done.5 = f32[2,16,8,4,128]{4,1,3,2,0:T(8,128)S(1)} collective-permute-done((f32[2,16,8,4,128]{4,1,3,2,0:T(8,128)S(1)}, f32[2,16,8,4,128]{4,1,3,2,0:T(8,128)S(1)}, u32[]{:S(2)}, u32[]{:S(2)}) %collective-permute-start.5) | collective-permute-done | bytes 524320 | tf_op jit(solution)/shard_map/ppermute | solution.py:191
  39.6 0.1 select_bitcast_fusion.3
  39.7 0.0 copy-start
  39.8 0.1 pad_maximum_fusion.1
  39.9 0.0 copy-start.1
  39.9 0.1 copy.42
  40.0 0.1 collective-permute-start.6
  40.1 0.9 copy-done
  41.0 0.1 constant_dynamic-update-slice_fusion.1
  41.1 0.2 copy-done.1
  41.3 0.1 constant_dynamic-update-slice_fusion
  41.4 1.1 fusion.29
  42.5 3.4 %collective-permute-start = (f32[2,4,128,128]{3,2,1,0:T(8,128)}, f32[2,4,128,128]{3,2,1,0:T(8,128)}, u32[]{:S(2)}, u32[]{:S(2)}) collective-permute-start(f32[2,4,128,128]{3,2,1,0:T(8,128)} %get-tuple-element.17), channel_id=1, source_target_pairs={{0,32},{32,64},{64,96},{96,128},{128,160},{160,192},{192,224},{1,3... | collective-permute-start | bytes 1572872 | tf_op jit(solution)/shard_map/ppermute | solution.py:178
  45.9 6.1 %collective-permute-start.1 = (f32[2,4,128,128]{3,2,1,0:T(8,128)}, f32[2,4,128,128]{3,2,1,0:T(8,128)}, u32[]{:S(2)}, u32[]{:S(2)}) collective-permute-start(f32[2,4,128,128]{3,2,1,0:T(8,128)} %get-tuple-element.16), channel_id=1, source_target_pairs={{32,0},{64,32},{96,64},{128,96},{160,128},{192,160},{224,192},{33,... | collective-permute-start | bytes 1572872 | tf_op jit(solution)/shard_map/ppermute | solution.py:178
  52.0 0.0 collective-permute-done.6
  52.0 1.4 %select_bitcast_fusion.1 = (f32[2,16,16,1,4,128]{5,1,4,2,0,3:T(8,128)S(1)}, f32[2,16,16,1,4,128]{5,1,4,2,0,3:T(8,128)S(1)}) fusion(f32[2,16,16,4,128]{4,1,3,2,0:T(8,128)S(1)} %bitcast.96, f32[2,16,16,4,128]{4,1,3,2,0:T(8,128)} %collective-permute-done.6, pred[]{:T(512)S(6)} %eq.33), kind=kLoop, calls=%fused_computation.13 | loop fusion | flops 524288 | bytes 4194305 | tf_op jit(solution)/shard_map/stack | solution.py:195
  53.4 0.1 fusion
  53.6 0.4 copy.44
  54.0 0.0 copy-start.6
  54.0 0.0 copy-start.7
  54.0 0.0 copy-start.8
  54.0 0.4 copy.45
  54.5 1.9 %collective-permute-start.7 = (f32[7,128,128]{2,1,0:T(8,128)S(1)}, f32[7,128,128]{2,1,0:T(8,128)S(1)}, u32[]{:S(2)}, u32[]{:S(2)}) collective-permute-start(f32[7,128,128]{2,1,0:T(8,128)S(1)} %pad_maximum_fusion.3), channel_id=1, source_target_pairs={{0,32},{2,34},{4,36},{6,38},{8,40},{10,42},{12,44},{14,46},{16,48}... | collective-permute-start | bytes 1376264 | tf_op jit(solution)/shard_map/ppermute | solution.py:245
  56.5 0.0 copy-done.6
  56.5 0.4 convolution_bitcast_fusion
  56.9 0.4 convolution_bitcast_fusion.1
  57.3 0.4 convolution_bitcast_fusion.2
  58.4 10.1 %collective-permute-done.7.mat_lo = f32[7,128,128]{2,1,0:T(8,128)S(1)} collective-permute-done((f32[7,128,128]{2,1,0:T(8,128)S(1)}, f32[7,128,128]{2,1,0:T(8,128)S(1)}, u32[]{:S(2)}, u32[]{:S(2)}) %collective-permute-start.7) | collective-permute-done | bytes 458784 | tf_op jit(solution)/shard_map/ppermute | solution.py:245
  68.5 0.0 collective-permute-start.8
  68.5 0.7 pad_maximum_fusion.5.count_ref
  69.2 0.4 convolution_bitcast_fusion.3
  69.6 0.7 maximum_multiply_fusion.src_hbm
  70.3 0.2 pad_maximum_fusion
  70.6 2.2 %copy.43 = f32[2,16,16,2,4,128]{5,4,3,2,1,0:T(4,128)} copy(f32[2,16,16,2,4,128]{5,1,4,2,0,3:T(8,128)S(1)} %pad_maximum_fusion) | data formatting | bytes 4194304 | tf_op jit(solution)/shard_map/stack | solution.py:195
  72.8 0.0 collective-permute-done.adj_lo
  72.8 0.0 collective-permute-done.1.adj_hi
  72.8 0.0 collective-permute-done.8.mat_hi
  72.8 0.8 copy-done.3
  73.5 15.0 %shard_map.112 = (f32[16,128,128]{2,1,0:T(8,128)}, f32[16,128,128]{2,1,0:T(8,128)}, f32[16,128,128]{2,1,0:T(8,128)}) custom-call(f32[2]{0:T(128)} %pad_maximum_fusion.5.count_ref, f32[16,128,128]{2,1,0:T(8,128)} %bitcast.93, f32[16,128,128]{2,1,0:T(8,128)} %bitcast.94, f32[2,4,128,128]{3,2,1,0:T(8,128)} %collective-permute-done.adj_lo, ...), custom_call_target="tpu_custom_call" | custom-call | tf_op jit(solution)/shard_map/pallas_call | solution.py:158
  88.5 1.4 %constant_dynamic-slice_fusion.1 = (f32[16,2,2,2,2,1,4,128]{7,6,5,4,3,2,1,0:T(4,128)S(1)}, f32[16,2,2,2,2,1,4,128]{7,6,5,4,3,2,1,0:T(4,128)S(1)}) fusion(f32[16,2,2,2,2,2,4,128]{7,6,5,4,3,2,1,0:T(4,128)} %bitcast.102, s32[]{:T(128)S(6)} %select_n.131, s32[]{:T(128)S(6)} %select_n.132), kind=kLoop, calls=%fused_computation.68 | loop fusion | bytes 2097160 | tf_op jit(solution)/shard_map/jit(dynamic_index_in_dim)/dynamic_slice | solution.py:214
  89.9 0.3 copy.58
  90.2 0.0 copy-start.4
  90.2 0.0 copy-start.5
  90.3 0.5 collective-permute-start.9
  90.8 1.5 %collective-permute-done.9 = f32[16,2,2,2,2,4,128]{6,0,5,4,3,2,1:T(8,128)S(1)} collective-permute-done((f32[16,2,2,2,2,4,128]{6,0,5,4,3,2,1:T(8,128)S(1)}, f32[16,2,2,2,2,4,128]{6,0,5,4,3,2,1:T(8,128)S(1)}, u32[]{:S(2)}, u32[]{:S(2)}) %collective-permute-start.9) | collective-permute-done | bytes 524320 | tf_op jit(solution)/shard_map/ppermute | solution.py:217
  92.3 0.3 bitcast_add_fusion
  92.7 0.8 collective-permute-start.10
  93.5 7.8 %collective-permute-done.10 = f32[16,2,2,2,4,128]{5,0,4,3,2,1:T(8,128)S(1)} collective-permute-done((f32[16,2,2,2,4,128]{5,0,4,3,2,1:T(8,128)S(1)}, f32[16,2,2,2,4,128]{5,0,4,3,2,1:T(8,128)S(1)}, u32[]{:S(2)}, u32[]{:S(2)}) %collective-permute-start.10) | collective-permute-done | bytes 262176 | tf_op jit(solution)/shard_map/ppermute | solution.py:217
  101.4 0.7 collective-permute-start.11
  102.1 4.4 %collective-permute-done.11 = f32[16,2,2,4,128]{4,0,3,2,1:T(8,128)S(1)} collective-permute-done((f32[16,2,2,4,128]{4,0,3,2,1:T(8,128)S(1)}, f32[16,2,2,4,128]{4,0,3,2,1:T(8,128)S(1)}, u32[]{:S(2)}, u32[]{:S(2)}) %collective-permute-start.11) | collective-permute-done | bytes 131104 | tf_op jit(solution)/shard_map/ppermute | solution.py:217
  106.5 0.1 collective-permute-start.12
  106.6 5.9 %collective-permute-done.12 = f32[16,2,4,128]{3,0,2,1:T(8,128)S(1)} collective-permute-done((f32[16,2,4,128]{3,0,2,1:T(8,128)S(1)}, f32[16,2,4,128]{3,0,2,1:T(8,128)S(1)}, u32[]{:S(2)}, u32[]{:S(2)}) %collective-permute-start.12) | collective-permute-done | bytes 65568 | tf_op jit(solution)/shard_map/ppermute | solution.py:217
  112.5 3.9 %collective-permute-start.13 = (f32[16,4,128]{2,0,1:T(8,128)S(1)}, f32[16,4,128]{2,0,1:T(8,128)S(1)}, u32[]{:S(2)}, u32[]{:S(2)}) collective-permute-start(f32[16,4,128]{2,0,1:T(8,128)S(1)} %dynamic-slice_bitcast_fusion.3), channel_id=1, source_target_pairs={{0,16},{1,17},{2,18},{3,19},{4,20},{5,21},{6,22},{7,23},{8,24},{9,... | collective-permute-start | bytes 98312 | tf_op jit(solution)/shard_map/ppermute | solution.py:217
  116.4 4.3 %collective-permute-done.13 = f32[16,4,128]{2,0,1:T(8,128)S(1)} collective-permute-done((f32[16,4,128]{2,0,1:T(8,128)S(1)}, f32[16,4,128]{2,0,1:T(8,128)S(1)}, u32[]{:S(2)}, u32[]{:S(2)}) %collective-permute-start.13) | collective-permute-done | bytes 32800 | tf_op jit(solution)/shard_map/ppermute | solution.py:217
  120.8 0.0 copy-done.4
  120.8 0.6 copy.50
  (26 shorter events, 0.4 us)
Async XLA Ops:
  1.4 9.7 %collective-permute-start.2 = (f32[2,16,1,4,128]{4,1,3,0,2:T(8,128)S(1)}, f32[2,16,1,4,128]{4,1,3,0,2:T(8,128)S(1)}, u32[]{:S(2)}, u32[]{:S(2)}) collective-permute-start(f32[2,16,1,4,128]{4,1,3,0,2:T(8,128)S(1)} %maximum_bitcast_fusion.1), channel_id=1, source_target_pairs={{0,16},{1,17},{2,18},{3,19},{4,20},{5,21},{6,22},{7,23},{8,24},{9,... | collective-permute-start | bytes 196616 | tf_op jit(solution)/shard_map/ppermute | solution.py:191
  11.2 8.1 %collective-permute-start.3 = (f32[2,16,2,4,128]{4,1,3,2,0:T(8,128)S(1)}, f32[2,16,2,4,128]{4,1,3,2,0:T(8,128)S(1)}, u32[]{:S(2)}, u32[]{:S(2)}) collective-permute-start(f32[2,16,2,4,128]{4,1,3,2,0:T(8,128)S(1)} %maximum_bitcast_fusion), channel_id=1, source_target_pairs={{0,8},{1,9},{2,10},{3,11},{4,12},{5,13},{6,14},{7,15},{8,0},{9,1},... | collective-permute-start | bytes 393224 | tf_op jit(solution)/shard_map/ppermute | solution.py:191
  19.3 7.7 %collective-permute-start.4 = (f32[2,16,4,4,128]{4,1,3,2,0:T(8,128)S(1)}, f32[2,16,4,4,128]{4,1,3,2,0:T(8,128)S(1)}, u32[]{:S(2)}, u32[]{:S(2)}) collective-permute-start(f32[2,16,4,4,128]{4,1,3,2,0:T(8,128)S(1)} %bitcast.103), channel_id=1, source_target_pairs={{0,4},{1,5},{2,6},{3,7},{4,0},{5,1},{6,2},{7,3},{8,12},{9,13},{10,... | collective-permute-start | bytes 786440 | tf_op jit(solution)/shard_map/ppermute | solution.py:191
  27.2 12.5 %collective-permute-start.5 = (f32[2,16,8,4,128]{4,1,3,2,0:T(8,128)S(1)}, f32[2,16,8,4,128]{4,1,3,2,0:T(8,128)S(1)}, u32[]{:S(2)}, u32[]{:S(2)}) collective-permute-start(f32[2,16,8,4,128]{4,1,3,2,0:T(8,128)S(1)} %bitcast.97), channel_id=1, source_target_pairs={{0,2},{1,3},{2,0},{3,1},{4,6},{5,7},{6,4},{7,5},{8,10},{9,11},{10,... | collective-permute-start | bytes 1572872 | tf_op jit(solution)/shard_map/ppermute | solution.py:191
  39.7 1.2 %copy-start = (f32[1,16,128,128]{3,2,1,0:T(8,128)S(1)}, f32[1,16,128,128]{3,2,1,0:T(8,128)}, u32[]{:S(2)}) copy-start(f32[1,16,128,128]{3,2,1,0:T(8,128)} %param.9) | copy-start | bytes 3145732
  39.9 1.5 %copy-start.1 = (f32[1,16,128,128]{3,2,1,0:T(8,128)S(1)}, f32[1,16,128,128]{3,2,1,0:T(8,128)}, u32[]{:S(2)}) copy-start(f32[1,16,128,128]{3,2,1,0:T(8,128)} %param.10) | copy-start | bytes 3145732
  40.0 12.0 %collective-permute-start.6 = (f32[2,16,16,4,128]{4,1,3,2,0:T(8,128)S(1)}, f32[2,16,16,4,128]{4,1,3,2,0:T(8,128)}, u32[]{:S(2)}, u32[]{:S(2)}) collective-permute-start(f32[2,16,16,4,128]{4,1,3,2,0:T(8,128)S(1)} %bitcast.95), channel_id=1, source_target_pairs={{0,1},{1,0},{2,3},{3,2},{4,5},{5,4},{6,7},{7,6},{8,9},{9,8},{10,11... | collective-permute-start | bytes 3145736 | tf_op jit(solution)/shard_map/ppermute | solution.py:191
  42.5 30.3 %collective-permute-start = (f32[2,4,128,128]{3,2,1,0:T(8,128)}, f32[2,4,128,128]{3,2,1,0:T(8,128)}, u32[]{:S(2)}, u32[]{:S(2)}) collective-permute-start(f32[2,4,128,128]{3,2,1,0:T(8,128)} %get-tuple-element.17), channel_id=1, source_target_pairs={{0,32},{32,64},{64,96},{96,128},{128,160},{160,192},{192,224},{1,3... | collective-permute-start | bytes 1572872 | tf_op jit(solution)/shard_map/ppermute | solution.py:178
  45.9 26.9 %collective-permute-start.1 = (f32[2,4,128,128]{3,2,1,0:T(8,128)}, f32[2,4,128,128]{3,2,1,0:T(8,128)}, u32[]{:S(2)}, u32[]{:S(2)}) collective-permute-start(f32[2,4,128,128]{3,2,1,0:T(8,128)} %get-tuple-element.16), channel_id=1, source_target_pairs={{32,0},{64,32},{96,64},{128,96},{160,128},{192,160},{224,192},{33,... | collective-permute-start | bytes 1572872 | tf_op jit(solution)/shard_map/ppermute | solution.py:178
  54.0 2.5 %copy-start.6 = (f32[1,4,256]{2,1,0:T(4,128)S(1)}, f32[1,4,256]{2,1,0:T(4,128)}, u32[]{:S(2)}) copy-start(f32[1,4,256]{2,1,0:T(4,128)} %param.17) | copy-start | bytes 12292
  54.0 2.5 %copy-start.7 = (s32[1,256]{1,0:T(1,128)S(1)}, s32[1,256]{1,0:T(1,128)}, u32[]{:S(2)}) copy-start(s32[1,256]{1,0:T(1,128)} %param.16) | copy-start | bytes 3076
  54.0 2.5 %copy-start.8 = (s32[1,256]{1,0:T(1,128)S(1)}, s32[1,256]{1,0:T(1,128)}, u32[]{:S(2)}) copy-start(s32[1,256]{1,0:T(1,128)} %param.15) | copy-start | bytes 3076
  54.5 14.0 %collective-permute-start.7 = (f32[7,128,128]{2,1,0:T(8,128)S(1)}, f32[7,128,128]{2,1,0:T(8,128)S(1)}, u32[]{:S(2)}, u32[]{:S(2)}) collective-permute-start(f32[7,128,128]{2,1,0:T(8,128)S(1)} %pad_maximum_fusion.3), channel_id=1, source_target_pairs={{0,32},{2,34},{4,36},{6,38},{8,40},{10,42},{12,44},{14,46},{16,48}... | collective-permute-start | bytes 1376264 | tf_op jit(solution)/shard_map/ppermute | solution.py:245
  68.5 2.0 %copy-start.2 = (f32[7,128,128]{2,1,0:T(8,128)}, f32[7,128,128]{2,1,0:T(8,128)S(1)}, u32[]{:S(2)}) copy-start(f32[7,128,128]{2,1,0:T(8,128)S(1)} %collective-permute-done.7.mat_lo) | copy-start | bytes 1376260
  68.5 4.2 %collective-permute-start.8 = (f32[7,128,128]{2,1,0:T(8,128)S(1)}, f32[7,128,128]{2,1,0:T(8,128)S(1)}, u32[]{:S(2)}, u32[]{:S(2)}) collective-permute-start(f32[7,128,128]{2,1,0:T(8,128)S(1)} %collective-permute-done.7.mat_lo), channel_id=1, source_target_pairs={{0,1},{1,0},{2,3},{3,2},{4,5},{5,4},{6,7},{7,6},{8,9},{9,8},{10,11... | collective-permute-start | bytes 1376264 | tf_op jit(solution)/shard_map/ppermute | solution.py:246
  72.8 0.8 copy-start.3
  90.2 30.5 %copy-start.4 = (f32[16,4,128]{2,1,0:T(4,128)S(1)}, f32[16,4,128]{2,1,0:T(4,128)}, u32[]{:S(2)}) copy-start(f32[16,4,128]{2,1,0:T(4,128)} %param.12) | copy-start | bytes 98308
  90.2 30.5 %copy-start.5 = (f32[16,4,128]{2,1,0:T(4,128)S(1)}, f32[16,4,128]{2,1,0:T(4,128)}, u32[]{:S(2)}) copy-start(f32[16,4,128]{2,1,0:T(4,128)} %param.13) | copy-start | bytes 98308
  90.3 2.1 %collective-permute-start.9 = (f32[16,2,2,2,2,4,128]{6,0,5,4,3,2,1:T(8,128)S(1)}, f32[16,2,2,2,2,4,128]{6,0,5,4,3,2,1:T(8,128)S(1)}, u32[]{:S(2)}, u32[]{:S(2)}) collective-permute-start(f32[16,2,2,2,2,4,128]{6,0,5,4,3,2,1:T(8,128)S(1)} %bitcast.105), channel_id=1, source_target_pairs={{0,1},{1,0},{2,3},{3,2},{4,5},{5,4},{6,7},{7,6},{8,9},{9,8},{10,11... | collective-permute-start | bytes 1572872 | tf_op jit(solution)/shard_map/ppermute | solution.py:217
  92.7 8.7 %collective-permute-start.10 = (f32[16,2,2,2,4,128]{5,0,4,3,2,1:T(8,128)S(1)}, f32[16,2,2,2,4,128]{5,0,4,3,2,1:T(8,128)S(1)}, u32[]{:S(2)}, u32[]{:S(2)}) collective-permute-start(f32[16,2,2,2,4,128]{5,0,4,3,2,1:T(8,128)S(1)} %dynamic-slice_bitcast_fusion), channel_id=1, source_target_pairs={{0,2},{1,3},{2,0},{3,1},{4,6},{5,7},{6,4},{7,5},{8,10},{9,11},{10,... | collective-permute-start | bytes 786440 | tf_op jit(solution)/shard_map/ppermute | solution.py:217
  101.4 5.1 %collective-permute-start.11 = (f32[16,2,2,4,128]{4,0,3,2,1:T(8,128)S(1)}, f32[16,2,2,4,128]{4,0,3,2,1:T(8,128)S(1)}, u32[]{:S(2)}, u32[]{:S(2)}) collective-permute-start(f32[16,2,2,4,128]{4,0,3,2,1:T(8,128)S(1)} %dynamic-slice_bitcast_fusion.1), channel_id=1, source_target_pairs={{0,4},{1,5},{2,6},{3,7},{4,0},{5,1},{6,2},{7,3},{8,12},{9,13},{10,... | collective-permute-start | bytes 393224 | tf_op jit(solution)/shard_map/ppermute | solution.py:217
  106.5 6.0 %collective-permute-start.12 = (f32[16,2,4,128]{3,0,2,1:T(8,128)S(1)}, f32[16,2,4,128]{3,0,2,1:T(8,128)S(1)}, u32[]{:S(2)}, u32[]{:S(2)}) collective-permute-start(f32[16,2,4,128]{3,0,2,1:T(8,128)S(1)} %dynamic-slice_bitcast_fusion.2), channel_id=1, source_target_pairs={{0,8},{1,9},{2,10},{3,11},{4,12},{5,13},{6,14},{7,15},{8,0},{9,1},... | collective-permute-start | bytes 196616 | tf_op jit(solution)/shard_map/ppermute | solution.py:217
  112.5 8.3 %collective-permute-start.13 = (f32[16,4,128]{2,0,1:T(8,128)S(1)}, f32[16,4,128]{2,0,1:T(8,128)S(1)}, u32[]{:S(2)}, u32[]{:S(2)}) collective-permute-start(f32[16,4,128]{2,0,1:T(8,128)S(1)} %dynamic-slice_bitcast_fusion.3), channel_id=1, source_target_pairs={{0,16},{1,17},{2,18},{3,19},{4,20},{5,21},{6,22},{7,23},{8,24},{9,... | collective-permute-start | bytes 98312 | tf_op jit(solution)/shard_map/ppermute | solution.py:217
